TPU v7x, 128 devices: a whole 4x4x4 slice. The times are simulated.
128 devices in a mesh: dp: 16 (over z, x), tensor: 8 (over y, core).
Axes of the slice: x: 4, y: 4, z: 4, core: 2. Of those that a mesh axis runs over, the one named last changes fastest.
Arguments:
- tokens: bfloat16 [8192, 8192], P('dp', 'tensor'), may hold values from -6 to 6
- cotangent: bfloat16 [8192, 4096], P('dp', 'tensor'), may hold values from -1.5 to 1.5
- frozen_query_weight: bfloat16 [8192, 4096], P(None, 'tensor'), may hold values from -0.0625 to 0.0625
- adapter_down_weight: bfloat16 [256, 8192, 64], P('dp', 'tensor'), may hold values from -0.0625 to 0.0625
- adapter_up_weight: bfloat16 [256, 64, 4096], P('dp', None, 'tensor'), may hold values from -0.75 to 0.75
- token_adapter: int32 [8192], P('dp'), may hold values from 0 to 255, as said below
Outputs:
- projected: bfloat16 [8192, 4096], P('dp', 'tensor')
- input_gradient: bfloat16 [8192, 8192], P('dp', 'tensor')
- down_grad: float32 [256, 8192, 64], P('dp', 'tensor')
- up_grad: float32 [256, 64, 4096], P('dp', None, 'tensor')
Inputs may be any that keep to these rules, and one draw needn't show every extreme that they name: `token_adapter`: adapter a belongs to index a // 16 of dp. Among the 512 tokens of one index of dp, at most 64 have adapters that belong to one index of dp, and for some index exactly 64 do.
All inputs are finite; a program needn't handle non-finite values.
Results may differ from a plain program's by a relative error of at most 0.0037.
Values may be sent and summed in bfloat16 or wider, within the bound.
No kernel may reach another device: no remote copies, remote signals or barrier semaphores. Data moves between devices by JAX's collectives and lax.ppermute only.
A program may use at most 192 MiB of HBM per device.

v0:
```python
import jax
import jax.numpy as jnp
from jax import lax
from jax.sharding import PartitionSpec as P

adapter_factor = 0.5


def tensor_sum(x):
    n = lax.axis_size("tensor")
    rows = x.shape[0]
    parts = x.reshape(n, rows // n, *x.shape[1:])
    got = lax.all_to_all(parts, "tensor", split_axis=0, concat_axis=0, tiled=True)
    mine = jnp.sum(got, axis=0)
    spread = jnp.broadcast_to(mine[None], (n,) + mine.shape)
    full = lax.all_to_all(spread, "tensor", split_axis=0, concat_axis=0, tiled=True)
    return full.reshape(x.shape)


def per_device(
    tokens, cotangent, frozen_query_weight, adapter_down_weight, adapter_up_weight, token_adapter
):
    tok_rows, feature_portion = tokens.shape
    query_portion = cotangent.shape[1]
    local_adapters, _, rank_columns = adapter_down_weight.shape
    dp_size = lax.axis_size("dp")
    capacity = tok_rows // dp_size * 2
    capacity = min(capacity, tok_rows)
    slot_count = dp_size * capacity
    oh_width = 128

    tokens_full = lax.all_gather(tokens, "tensor", axis=1, tiled=True)
    partial_term = lax.dot_general(
        cotangent, frozen_query_weight, (((1,), (1,)), ((), ())), preferred_element_type=jnp.float32
    )
    frozen_backward = lax.psum_scatter(partial_term, "tensor", scatter_dimension=1, tiled=True)

    owners = token_adapter // local_adapters
    local_ids = token_adapter % local_adapters
    owner_hits = (owners[:, None] == jnp.arange(dp_size, dtype=jnp.int32)[None, :]).astype(jnp.int32)
    earlier = jnp.cumsum(owner_hits, axis=0) - owner_hits
    rank_in = jnp.sum(earlier * owner_hits, axis=1)
    slot_of = owners * capacity + rank_in
    pick = (jnp.arange(slot_count, dtype=jnp.int32)[:, None] == slot_of[None, :]).astype(jnp.bfloat16)
    local_hot = (local_ids[:, None] == jnp.arange(oh_width, dtype=jnp.int32)[None, :]).astype(
        jnp.bfloat16
    )
    payload = jnp.concatenate([tokens, cotangent, local_hot], axis=1)
    send = jnp.dot(pick, payload, preferred_element_type=jnp.float32).astype(jnp.bfloat16)
    got = lax.all_to_all(send, "dp", split_axis=0, concat_axis=0, tiled=True)
    got_tok = got[:, :feature_portion]
    got_cot = got[:, feature_portion : feature_portion + query_portion]
    got_hot = got[:, feature_portion + query_portion : feature_portion + query_portion + local_adapters]
    hot_f = got_hot.astype(jnp.float32)

    hidden_all = jnp.einsum(
        "sd,adr->sar", got_tok, adapter_down_weight, preferred_element_type=jnp.float32
    )
    grad_all = jnp.einsum(
        "sq,arq->sar", got_cot, adapter_up_weight, preferred_element_type=jnp.float32
    )
    hidden_part = jnp.sum(hidden_all * hot_f[:, :, None], axis=1)
    grad_part = jnp.sum(grad_all * hot_f[:, :, None], axis=1)
    joined = tensor_sum(jnp.concatenate([hidden_part, grad_part], axis=1))
    lowrank_round = joined[:, :rank_columns].astype(jnp.bfloat16)
    gradient_round = (adapter_factor * joined[:, rank_columns:]).astype(jnp.bfloat16)
    low_spread = got_hot[:, :, None] * lowrank_round[:, None, :]
    grad_spread = got_hot[:, :, None] * gradient_round[:, None, :]

    adapter_output = (
        adapter_factor
        * jnp.einsum("sar,arq->sq", low_spread, adapter_up_weight, preferred_element_type=jnp.float32)
    ).astype(jnp.bfloat16)
    adapter_backward = jnp.einsum(
        "sar,adr->sd", grad_spread, adapter_down_weight, preferred_element_type=jnp.float32
    ).astype(jnp.bfloat16)
    down_grad = jnp.einsum("sd,sar->adr", got_tok, grad_spread, preferred_element_type=jnp.float32)
    up_grad = adapter_factor * jnp.einsum(
        "sar,sq->arq", low_spread, got_cot, preferred_element_type=jnp.float32
    )

    back = jnp.concatenate([adapter_output, adapter_backward], axis=1)
    back = lax.all_to_all(back, "dp", split_axis=0, concat_axis=0, tiled=True)
    mine = jnp.einsum("st,sc->tc", pick, back, preferred_element_type=jnp.float32)
    mine_out = mine[:, :query_portion]
    mine_grad = mine[:, query_portion:]

    frozen_output = jnp.dot(tokens_full, frozen_query_weight, preferred_element_type=jnp.float32)
    projected = (frozen_output + mine_out).astype(jnp.bfloat16)
    input_gradient = (frozen_backward + mine_grad).astype(jnp.bfloat16)
    return (projected, input_gradient, down_grad, up_grad)


def solution(mesh):
    in_specs = (
        P("dp", "tensor"),
        P("dp", "tensor"),
        P(None, "tensor"),
        P("dp", "tensor", None),
        P("dp", None, "tensor"),
        P("dp"),
    )
    out_specs = (
        P("dp", "tensor"),
        P("dp", "tensor"),
        P("dp", "tensor", None),
        P("dp", None, "tensor"),
    )
    return jax.shard_map(
        per_device, mesh=mesh, in_specs=in_specs, out_specs=out_specs, check_vma=False
    )
```

profile of v0, /device:TPU:1, one launch (start us, length us, event | category | flops | bytes accessed | tf_op | source)
XLA Modules:
  0.0 206.8 jit_solution(15552825506098094151)
XLA Ops:
  7.2 0.7 all-gather.2.cloned.1.call-update
  8.0 13.9 %fusion.48 = f32[512,8192]{1,0:T(8,128)} fusion(bf16[512,512]{1,0:T(8,128)(2,1)} %param.7, bf16[8192,512]{1,0:T(8,128)(2,1)} %param.8), kind=kOutput, calls=%fused_computation.68 | convolution fusion | flops 4294967296 | bytes 25690112 | tf_op jit(solution)/shard_map/dot_general | solution.py:33
  21.9 0.7 copy-done.5
  22.6 1.2 reduce-window.6
  23.8 0.2 slice_reduce_fusion
  24.0 0.1 fusion.44
  24.1 0.1 fusion.41
  24.3 3.3 %convolution_convert_fusion = bf16[1024,1664]{1,0:T(8,128)(2,1)S(1)} fusion(bf16[512,128]{1,0:T(8,128)(2,1)S(1)} %fusion.41, bf16[512,512]{1,0:T(8,128)(2,1)} %param.7, bf16[512,1024]{1,0:T(8,128)(2,1)S(1)} %copy-done.2, s32[512]{0:T(512)S(1)} %multiply_add_fusion), kind=kOutput, calls=%fused_computation.3 | convolution fusion | flops 1752170496 | bytes 5113856 | tf_op jit(solution)/shard_map/dot_general | solution.py:49
  27.6 50.1 %all_to_all.34 = bf16[16,64,1664]{2,1,0:T(8,128)(2,1)} all-to-all(bf16[16,64,1664]{2,1,0:T(8,128)(2,1)S(1)} %bitcast.60), channel_id=1, replica_groups=mesh['dp'=16,'tensor'=8] {'dp'}, dimensions={0} | all-to-all | bytes 6815744 | tf_op jit(solution)/shard_map/all_to_all | solution.py:50
  77.7 1.0 slice.38
  78.7 0.1 copy.53
  78.8 4.0 %fusion.18 = f32[1024,1024]{0,1:S(1)} fusion(bf16[1024,1024]{0,1:T(8,128)(2,1)S(1)} %bitcast.58, bf16[1024,1664]{1,0:T(8,128)(2,1)} %bitcast.3), kind=kOutput, calls=%fused_computation.22 | convolution fusion | flops 2147483648 | bytes 8388608
  82.9 0.5 multiply_reduce_fusion.1
  83.4 0.7 copy-done.6
  84.1 2.6 %multiply_reduce_fusion = f32[1024,64]{0,1:T(8,128)S(1)} fusion(bf16[16,64,512]{2,1,0:T(8,128)(2,1)S(1)} %copy-done.6, f32[1024,16]{0,1:T(8,128)S(1)} %convert_element_type.37, bf16[1024,1664]{1,0:T(8,128)(2,1)} %bitcast.3), kind=kOutput, calls=%fused_computation.1 | convolution fusion | flops 1075773440 | bytes 2424832 | tf_op jit(solution)/shard_map/sq,arq->sar/dot_general | solution.py:59
  86.7 19.1 %all_to_all.35 = f32[8,128,128]{1,2,0:T(8,128)S(1)} all-to-all(f32[8,128,128]{1,2,0:T(8,128)S(1)} %copy_bitcast_fusion), channel_id=1, replica_groups=mesh['dp'=16,'tensor'=8] {'tensor'}, dimensions={0} | all-to-all | bytes 1048576 | tf_op jit(solution)/shard_map/all_to_all | solution.py:13
  105.9 15.9 %all_to_all.36 = f32[8,128,128]{1,2,0:T(8,128)S(1)} all-to-all(f32[8,128,128]{1,2,0:T(8,128)S(1)} %broadcast_in_dim.2), channel_id=1, replica_groups=mesh['dp'=16,'tensor'=8] {'tensor'}, dimensions={0} | all-to-all | bytes 1048576 | tf_op jit(solution)/shard_map/all_to_all | solution.py:16
  121.7 0.2 copy.49
  122.0 0.2 slice.42
  122.2 0.1 copy.50
  122.3 0.2 copy.54
  122.5 2.5 %fusion.13 = bf16[1024,512]{0,1:T(8,128)(2,1)S(1)} fusion(bf16[16,64,512]{2,1,0:T(8,128)(2,1)} %param.10, bf16[1024,64]{0,1:T(8,128)(2,1)S(1)} %copy.50, bf16[1024,16]{0,1:T(8,128)(2,1)} %copy-done.3), kind=kOutput, calls=%fused_computation.18 | convolution fusion | flops 1075838976 | bytes 2260992 | tf_op jit(solution)/shard_map/sar,arq->sq/dot_general | solution.py:72
  125.1 2.4 %bitcast_convert_fusion = bf16[1024,1024]{0,1:T(8,128)(2,1)S(1)} fusion(bf16[16,1024,64]{1,2,0:T(8,128)(2,1)S(1)} %copy-done, bf16[1024,64]{0,1:T(8,128)(2,1)S(1)} %multiply_convert_fusion, bf16[1024,16]{0,1:T(8,128)(2,1)S(1)} %copy-done.4), kind=kOutput, calls=%fused_computation | convolution fusion | flops 2149580800 | bytes 4358144 | tf_op jit(solution)/shard_map/sar,adr->sd/dot_general | solution.py:74
  127.5 0.3 pad_maximum_fusion
  127.8 3.0 %copy.52 = bf16[1024,1536]{1,0:T(8,128)(2,1)} copy(bf16[1024,1536]{0,1:T(8,128)(2,1)S(1)} %pad_maximum_fusion) | data formatting | bytes 6291456 | tf_op jit(solution)/shard_map/concatenate | solution.py:82
  130.8 3.8 %all-to-all-start.3 = ((bf16[16,64,1536]{2,1,0:T(8,128)(2,1)}), bf16[16,64,1536]{2,1,0:T(8,128)(2,1)S(1)}, u32[]{:S(2)}, u32[]{:S(2)}) async-start(bf16[16,64,1536]{2,1,0:T(8,128)(2,1)} %bitcast.11), calls=%async_computation.3 | async-start | bytes 6291456 | tf_op jit(solution)/shard_map/all_to_all | solution.py:83
  134.5 3.8 %fusion.27 = f32[16,64,512]{2,1,0:T(8,128)} fusion(bf16[1024,64]{0,1:T(8,128)(2,1)S(1)} %copy.50, bf16[1024,16]{0,1:T(8,128)(2,1)S(1)} %copy-done.4, bf16[1024,1664]{1,0:T(8,128)(2,1)} %bitcast.3), kind=kOutput, calls=%fused_computation.29 | convolution fusion | flops 1075314688 | bytes 3309568 | tf_op jit(solution)/shard_map/sar,sq->arq/dot_general | solution.py:78
  138.4 6.0 %fusion.8 = f32[16,1024,64]{1,2,0:T(8,128)} fusion(bf16[1024,1664]{1,0:T(8,128)(2,1)} %bitcast.3, bf16[1024,64]{0,1:T(8,128)(2,1)S(1)} %multiply_convert_fusion, bf16[1024,16]{0,1:T(8,128)(2,1)S(1)} %copy-done.4), kind=kOutput, calls=%fused_computation.13 | convolution fusion | flops 2148532224 | bytes 6455296 | tf_op jit(solution)/shard_map/sd,sar->adr/dot_general | solution.py:77
  144.3 37.1 %all-to-all-done.3 = bf16[16,64,1536]{2,1,0:T(8,128)(2,1)S(1)} async-done(((bf16[16,64,1536]{2,1,0:T(8,128)(2,1)}), bf16[16,64,1536]{2,1,0:T(8,128)(2,1)S(1)}, u32[]{:S(2)}, u32[]{:S(2)}) %all-to-all-start.3) | async-done | bytes 3145760 | tf_op jit(solution)/shard_map/all_to_all | solution.py:83
  181.4 3.6 %fusion.14 = f32[512,1536]{1,0:T(8,128)} fusion(bf16[1024,1536]{1,0:T(8,128)(2,1)S(1)} %bitcast.63, s32[512]{0:T(512)S(1)} %multiply_add_fusion), kind=kOutput, calls=%fused_computation.20 | convolution fusion | flops 1611137024 | bytes 6293504 | tf_op jit(solution)/shard_map/st,sc->tc/dot_general | solution.py:84
  185.0 11.4 %fusion.30 = bf16[512,512]{1,0:T(8,128)(2,1)} fusion(bf16[512,8192]{1,0:T(8,128)(2,1)} %all-gather.2.cloned.1.call-done, bf16[8192,512]{1,0:T(8,128)(2,1)} %param.8, f32[512,1536]{1,0:T(8,128)} %fusion.14), kind=kOutput, calls=%fused_computation.31 | convolution fusion | flops 4295491584 | bytes 18350080 | tf_op jit(solution)/shard_map/dot_general | solution.py:88
  196.5 3.5 %fusion.11 = bf16[512,1024]{1,0:T(8,128)(2,1)} fusion(f32[512,1024]{1,0:T(8,128)} %reduce-scatter.2.cloned.1.call-done, f32[512,1536]{1,0:T(8,128)} %fusion.14), kind=kLoop, calls=%fused_computation.15 | loop fusion | flops 1048576 | bytes 5242880 | tf_op jit(solution)/shard_map/convert_element_type | solution.py:90
  (28 shorter events, 0.4 us)
Async XLA Ops:
  7.2 71.7 %copy-start = (bf16[16,1024,64]{1,2,0:T(8,128)(2,1)S(1)}, bf16[16,1024,64]{1,2,0:T(8,128)(2,1)}, u32[]{:S(2)}) copy-start(bf16[16,1024,64]{1,2,0:T(8,128)(2,1)} %param.9) | copy-start | bytes 6291460
  7.2 177.8 %all-gather.2.cloned.1.call-start = ((), (), s32[]{:S(2)}) async-start(), calls=%async_computation.5 | async-start | bytes 9437184 | tf_op jit(solution)/shard_map/all_gather | solution.py:32
  7.9 188.5 %reduce-scatter.2.cloned.1.call-start = ((), (), s32[]{:S(2)}) async-start(), calls=%async_computation.6 | async-start | bytes 18874368 | tf_op jit(solution)/shard_map/reduce_scatter | solution.py:36
  21.9 0.7 copy-start.5
  21.9 2.4 %copy-start.2 = (bf16[512,1024]{1,0:T(8,128)(2,1)S(1)}, bf16[512,1024]{1,0:T(8,128)(2,1)}, u32[]{:S(2)}) copy-start(bf16[512,1024]{1,0:T(8,128)(2,1)} %param.6) | copy-start | bytes 3145732
  78.8 4.1 %copy-start.3 = (bf16[1024,16]{0,1:T(8,128)(2,1)}, bf16[1024,16]{0,1:T(8,128)(2,1)S(1)}, u32[]{:S(2)}) copy-start(bf16[1024,16]{0,1:T(8,128)(2,1)S(1)} %copy.53) | copy-start | bytes 98308
  82.9 1.3 copy-start.6
  122.5 2.6 %copy-start.4 = (bf16[1024,16]{0,1:T(8,128)(2,1)S(1)}, bf16[1024,16]{0,1:T(8,128)(2,1)}, u32[]{:S(2)}) copy-start(bf16[1024,16]{0,1:T(8,128)(2,1)} %copy-done.3) | copy-start | bytes 98308
  130.8 50.7 %all-to-all-start.3 = ((bf16[16,64,1536]{2,1,0:T(8,128)(2,1)}), bf16[16,64,1536]{2,1,0:T(8,128)(2,1)S(1)}, u32[]{:S(2)}, u32[]{:S(2)}) async-start(bf16[16,64,1536]{2,1,0:T(8,128)(2,1)} %bitcast.11), calls=%async_computation.3 | async-start | bytes 6291456 | tf_op jit(solution)/shard_map/all_to_all | solution.py:83
  185.0 15.0 %copy-start.1 = (bf16[16,1024,64]{1,2,0:T(8,128)(2,1)S(1)}, bf16[16,1024,64]{1,2,0:T(8,128)(2,1)}, u32[]{:S(2)}) copy-start(bf16[16,1024,64]{1,2,0:T(8,128)(2,1)} %param.9) | copy-start | bytes 6291460
Sparse Core Ops, SparseCore 0:
  9.7 53.2 all-gather.1
  65.5 102.2 reduce-scatter.1
where the time goes:
time: 208 us; the launch traced here: 207 us
  blocking collectives  85 us (41%)
  matrix products  53.6 us (26%)
  waiting for transfers between devices  37.8 us (18%)
  between operations  14.3 us (7%)
  local copies, waits for them, and re-layouts  6.43 us (3%)
  other arithmetic  5.9 us (3%)
  starting transfers between devices  3.83 us (2%)
    all_to_all x1, blocking collectives, per_device(): got = lax.all_to_all(send, 'dp', split_axis=0, concat_axis=0, tiled=True)  50.1 us
    all_to_all x1, waiting for transfers between devices, per_device(): back = lax.all_to_all(back, 'dp', split_axis=0, concat_axis=0, tiled=True)  37.1 us
    all_to_all x1, blocking collectives, tensor_sum(): lax.all_to_all(parts, 'tensor', split_axis=0, concat_axis=0, tiled=True)  19.1 us
    all_to_all x1, blocking collectives, tensor_sum(): lax.all_to_all(spread, 'tensor', split_axis=0, concat_axis=0, tiled=True)  15.9 us
    dot_general x1, matrix products, per_device(): lax.dot_general(cotangent, frozen_query_weight, (((1,), (1,)), ((), ())),...  13.9 us
    dot_general x1, matrix products, per_device(): jnp.dot(tokens_full, frozen_query_weight, preferred_element_type=jnp.floa...  11.4 us
    dot_general x1, matrix products, per_device(): jnp.einsum('sd,sar->adr', got_tok, grad_spread, preferred_element_type=jn...  5.95 us
  transfers between devices with their start and end apart: 3, of which 1 were waited for; matrix products, arithmetic and copies ran while one was open for 29% of the time, Pallas kernels for 0%

commit v1 on v0

--- a/solution.py
+++ b/solution.py
@@ -30,10 +30,6 @@
     oh_width = 128
 
     tokens_full = lax.all_gather(tokens, "tensor", axis=1, tiled=True)
-    partial_term = lax.dot_general(
-        cotangent, frozen_query_weight, (((1,), (1,)), ((), ())), preferred_element_type=jnp.float32
-    )
-    frozen_backward = lax.psum_scatter(partial_term, "tensor", scatter_dimension=1, tiled=True)
 
     owners = token_adapter // local_adapters
     local_ids = token_adapter % local_adapters
@@ -47,6 +43,11 @@
     )
     payload = jnp.concatenate([tokens, cotangent, local_hot], axis=1)
     send = jnp.dot(pick, payload, preferred_element_type=jnp.float32).astype(jnp.bfloat16)
+    send, cot_late, weight_late = lax.optimization_barrier((send, cotangent, frozen_query_weight))
+    partial_term = lax.dot_general(
+        cot_late, weight_late, (((1,), (1,)), ((), ())), preferred_element_type=jnp.float32
+    )
+    frozen_backward = lax.psum_scatter(partial_term, "tensor", scatter_dimension=1, tiled=True)
     got = lax.all_to_all(send, "dp", split_axis=0, concat_axis=0, tiled=True)
     got_tok = got[:, :feature_portion]
     got_cot = got[:, feature_portion : feature_portion + query_portion]
@@ -80,12 +81,15 @@
     )
 
     back = jnp.concatenate([adapter_output, adapter_backward], axis=1)
+    back, tokens_late = lax.optimization_barrier((back, tokens_full))
     back = lax.all_to_all(back, "dp", split_axis=0, concat_axis=0, tiled=True)
+    frozen_output = lax.optimization_barrier(
+        jnp.dot(tokens_late, frozen_query_weight, preferred_element_type=jnp.float32)
+    )
     mine = jnp.einsum("st,sc->tc", pick, back, preferred_element_type=jnp.float32)
     mine_out = mine[:, :query_portion]
     mine_grad = mine[:, query_portion:]
 
-    frozen_output = jnp.dot(tokens_full, frozen_query_weight, preferred_element_type=jnp.float32)
     projected = (frozen_output + mine_out).astype(jnp.bfloat16)
     input_gradient = (frozen_backward + mine_grad).astype(jnp.bfloat16)
     return (projected, input_gradient, down_grad, up_grad)

time: 208 us -> 195 us (0.938)
  waiting for transfers between devices: 37.8 us -> 29.6 us
  matrix products: 53.6 us -> 47.1 us
  other arithmetic: 5.9 us -> 8.9 us
    dot_general x2, matrix products: 25.4 us -> 16.6 us  [the longest x1 8.65 us: per_device(): lax.dot_general(cot_late, weight_late, (((1,), (1,)), ((), ())), preferre...]
    all_to_all x1, waiting for transfers between devices: 37.1 us -> 28.9 us  [per_device(): back = lax.all_to_all(back, 'dp', split_axis=0, concat_axis=0, tiled=True)]
    concatenate x1 -> x0, local copies, waits for them, and re-layouts: 2.95 us -> none  [per_device(): back = jnp.concatenate([adapter_output, adapter_backward], axis=1)]
    optimization_barrier x0 -> x1, local copies, waits for them, and re-layouts: none -> 2.95 us  [per_device(): back, tokens_late = lax.optimization_barrier((back, tokens_full))]
    convert_element_type x0 -> x1, other arithmetic: none -> 2.34 us  [per_device(): projected = (frozen_output + mine_out).astype(jnp.bfloat16)]
    dot_general x1, matrix products: 3.34 us -> 5.43 us  [per_device(): jnp.dot(pick, payload, preferred_element_type=jnp.float32)]
  transfers between devices with their start and end apart: 3 -> 3, of which waited for: 1 -> 1; matrix products, arithmetic and copies ran while one was open for 29% -> 30% of each run, Pallas kernels for 0% -> 0%
where the time goes in v1:
time: 195 us
  blocking collectives  85 us (44%)
  matrix products  47.1 us (24%)
  waiting for transfers between devices  29.6 us (15%)
  between operations  14.3 us (7%)
  other arithmetic  8.9 us (5%)
  local copies, waits for them, and re-layouts  5.81 us (3%)
  starting transfers between devices  3.83 us (2%)
    all_to_all x1, blocking collectives, per_device(): got = lax.all_to_all(send, 'dp', split_axis=0, concat_axis=0, tiled=True)  50.6 us
    all_to_all x1, waiting for transfers between devices, per_device(): back = lax.all_to_all(back, 'dp', split_axis=0, concat_axis=0, tiled=True)  28.9 us
    all_to_all x1, blocking collectives, tensor_sum(): lax.all_to_all(parts, 'tensor', split_axis=0, concat_axis=0, tiled=True)  18.6 us
    all_to_all x1, blocking collectives, tensor_sum(): lax.all_to_all(spread, 'tensor', split_axis=0, concat_axis=0, tiled=True)  15.9 us
    dot_general x1, matrix products, per_device(): lax.dot_general(cot_late, weight_late, (((1,), (1,)), ((), ())), preferre...  8.65 us
    dot_general x1, matrix products, per_device(): jnp.dot(tokens_late, frozen_query_weight, preferred_element_type=jnp.floa...  7.99 us
    dot_general x1, matrix products, per_device(): jnp.einsum('sd,sar->adr', got_tok, grad_spread, preferred_element_type=jn...  6.08 us
    dot_general x1, matrix products, per_device(): jnp.dot(pick, payload, preferred_element_type=jnp.float32)  5.43 us
  transfers between devices with their start and end apart: 3, of which 1 were waited for; matrix products, arithmetic and copies ran while one was open for 30% of the time, Pallas kernels for 0%

profile of v1, /device:TPU:1, one launch (start us, length us, event | category | flops | bytes accessed | tf_op | source)
XLA Modules:
  0.0 194.5 jit_solution(16128141705799195118)
XLA Ops:
  7.2 0.7 all-gather.2.cloned.1.call-update
  8.0 0.7 add_select_fusion.1
  8.7 1.2 reduce-window.6
  9.8 0.2 slice_reduce_fusion
  10.2 0.1 fusion.41
  10.4 5.4 %convolution_convert_fusion = bf16[1024,1664]{1,0:T(8,128)(2,1)} fusion(bf16[512,128]{1,0:T(8,128)(2,1)S(1)} %fusion.41, bf16[512,512]{1,0:T(8,128)(2,1)} %param.7, bf16[512,1024]{1,0:T(8,128)(2,1)} %param.6, s32[512]{0:T(512)S(1)} %multiply_add_fusion), kind=kOutput, calls=%fused_computation.3 | convolution fusion | flops 1752170496 | bytes 5113856 | tf_op jit(solution)/shard_map/dot_general | solution.py:45
  15.8 8.6 %fusion.49 = f32[512,8192]{1,0:T(8,128)} fusion(bf16[512,512]{1,0:T(8,128)(2,1)S(1)} %copy-done.4, bf16[8192,512]{1,0:T(8,128)(2,1)S(1)} %copy-done.2), kind=kOutput, calls=%fused_computation.69 | convolution fusion | flops 4294967296 | bytes 25690112 | tf_op jit(solution)/shard_map/dot_general | solution.py:47
  24.5 50.6 %all_to_all.34 = bf16[16,64,1664]{2,1,0:T(8,128)(2,1)} all-to-all(bf16[16,64,1664]{2,1,0:T(8,128)(2,1)} %bitcast.62), channel_id=1, replica_groups=mesh['dp'=16,'tensor'=8] {'dp'}, dimensions={0} | all-to-all | bytes 6815744 | tf_op jit(solution)/shard_map/all_to_all | solution.py:51
  75.1 1.0 slice.38
  76.0 0.1 copy.53
  76.2 4.0 %fusion.18 = f32[1024,1024]{0,1:S(1)} fusion(bf16[1024,1024]{0,1:T(8,128)(2,1)S(1)} %bitcast.58, bf16[1024,1664]{1,0:T(8,128)(2,1)} %bitcast.3), kind=kOutput, calls=%fused_computation.22 | convolution fusion | flops 2147483648 | bytes 8388608
  80.2 0.5 multiply_reduce_fusion.1
  80.7 0.7 copy-done.7
  81.4 2.6 %multiply_reduce_fusion = f32[1024,64]{0,1:T(8,128)S(1)} fusion(bf16[16,64,512]{2,1,0:T(8,128)(2,1)S(1)} %copy-done.7, f32[1024,16]{0,1:T(8,128)S(1)} %convert_element_type.37, bf16[1024,1664]{1,0:T(8,128)(2,1)} %bitcast.3), kind=kOutput, calls=%fused_computation.1 | convolution fusion | flops 1075773440 | bytes 2424832 | tf_op jit(solution)/shard_map/sq,arq->sar/dot_general | solution.py:60
  84.0 18.6 %all_to_all.35 = f32[8,128,128]{1,2,0:T(8,128)S(1)} all-to-all(f32[8,128,128]{1,2,0:T(8,128)S(1)} %copy_bitcast_fusion), channel_id=1, replica_groups=mesh['dp'=16,'tensor'=8] {'tensor'}, dimensions={0} | all-to-all | bytes 1048576 | tf_op jit(solution)/shard_map/all_to_all | solution.py:13
  102.7 15.9 %all_to_all.36 = f32[8,128,128]{1,2,0:T(8,128)S(1)} all-to-all(f32[8,128,128]{1,2,0:T(8,128)S(1)} %broadcast_in_dim.2), channel_id=1, replica_groups=mesh['dp'=16,'tensor'=8] {'tensor'}, dimensions={0} | all-to-all | bytes 1048576 | tf_op jit(solution)/shard_map/all_to_all | solution.py:16
  118.5 0.2 copy.49
  118.8 0.2 slice.42
  119.0 0.2 copy.54
  119.2 0.1 copy.50
  119.3 2.6 %fusion.13 = bf16[1024,512]{0,1:T(8,128)(2,1)S(1)} fusion(bf16[16,64,512]{2,1,0:T(8,128)(2,1)} %param.10, bf16[1024,64]{0,1:T(8,128)(2,1)S(1)} %copy.50, bf16[1024,16]{0,1:T(8,128)(2,1)} %copy-done.5), kind=kOutput, calls=%fused_computation.18 | convolution fusion | flops 1075838976 | bytes 2260992 | tf_op jit(solution)/shard_map/sar,arq->sq/dot_general | solution.py:73
  121.9 2.4 %bitcast_convert_fusion = bf16[1024,1024]{0,1:T(8,128)(2,1)S(1)} fusion(bf16[16,1024,64]{1,2,0:T(8,128)(2,1)S(1)} %copy-done, bf16[1024,64]{0,1:T(8,128)(2,1)S(1)} %multiply_convert_fusion, bf16[1024,16]{0,1:T(8,128)(2,1)S(1)} %copy-done.6), kind=kOutput, calls=%fused_computation | convolution fusion | flops 2149580800 | bytes 4358144 | tf_op jit(solution)/shard_map/sar,adr->sd/dot_general | solution.py:75
  124.3 0.3 pad_maximum_fusion
  124.7 3.0 %copy.52 = bf16[1024,1536]{1,0:T(8,128)(2,1)} copy(bf16[1024,1536]{0,1:T(8,128)(2,1)S(1)} %pad_maximum_fusion) | data formatting | bytes 6291456 | tf_op jit(solution)/shard_map/optimization_barrier | solution.py:84
  127.6 3.8 %all-to-all-start.3 = ((bf16[16,64,1536]{2,1,0:T(8,128)(2,1)}), bf16[16,64,1536]{2,1,0:T(8,128)(2,1)S(1)}, u32[]{:S(2)}, u32[]{:S(2)}) async-start(bf16[16,64,1536]{2,1,0:T(8,128)(2,1)} %bitcast.11), calls=%async_computation.3 | async-start | bytes 6291456 | tf_op jit(solution)/shard_map/all_to_all | solution.py:85
  131.4 4.0 %fusion.27 = f32[16,64,512]{2,1,0:T(8,128)} fusion(bf16[1024,64]{0,1:T(8,128)(2,1)S(1)} %copy.50, bf16[1024,16]{0,1:T(8,128)(2,1)S(1)} %copy-done.6, bf16[1024,1664]{1,0:T(8,128)(2,1)} %bitcast.3), kind=kOutput, calls=%fused_computation.29 | convolution fusion | flops 1075314688 | bytes 3309568 | tf_op jit(solution)/shard_map/sar,sq->arq/dot_general | solution.py:79
  135.4 6.1 %fusion.8 = f32[16,1024,64]{1,2,0:T(8,128)} fusion(bf16[1024,1664]{1,0:T(8,128)(2,1)} %bitcast.3, bf16[1024,64]{0,1:T(8,128)(2,1)S(1)} %multiply_convert_fusion, bf16[1024,16]{0,1:T(8,128)(2,1)S(1)} %copy-done.6), kind=kOutput, calls=%fused_computation.13 | convolution fusion | flops 2148532224 | bytes 6455296 | tf_op jit(solution)/shard_map/sd,sar->adr/dot_general | solution.py:78
  141.5 8.0 %fusion.48 = f32[512,512]{1,0:T(8,128)} fusion(bf16[512,8192]{1,0:T(8,128)(2,1)} %all-gather.2.cloned.1.call-done, bf16[8192,512]{1,0:T(8,128)(2,1)S(1)} %bitcast.60), kind=kOutput, calls=%fused_computation.68 | convolution fusion | flops 4294967296 | bytes 17825792 | tf_op jit(solution)/shard_map/dot_general | solution.py:87
  149.4 28.9 %all-to-all-done.3 = bf16[16,64,1536]{2,1,0:T(8,128)(2,1)S(1)} async-done(((bf16[16,64,1536]{2,1,0:T(8,128)(2,1)}), bf16[16,64,1536]{2,1,0:T(8,128)(2,1)S(1)}, u32[]{:S(2)}, u32[]{:S(2)}) %all-to-all-start.3) | async-done | bytes 3145760 | tf_op jit(solution)/shard_map/all_to_all | solution.py:85
  178.3 3.5 %fusion.14 = f32[512,1536]{1,0:T(8,128)} fusion(bf16[1024,1536]{1,0:T(8,128)(2,1)S(1)} %bitcast.65, s32[512]{0:T(512)S(1)} %multiply_add_fusion), kind=kOutput, calls=%fused_computation.20 | convolution fusion | flops 1611137024 | bytes 6293504 | tf_op jit(solution)/shard_map/st,sc->tc/dot_general | solution.py:89
  181.8 2.3 %fusion.30 = bf16[512,512]{1,0:T(8,128)(2,1)} fusion(f32[512,512]{1,0:T(8,128)S(1)} %copy-done.3, f32[512,1536]{1,0:T(8,128)} %fusion.14), kind=kLoop, calls=%fused_computation.31 | loop fusion | flops 524288 | bytes 2621440 | tf_op jit(solution)/shard_map/convert_element_type | solution.py:93
  184.2 3.5 %fusion.11 = bf16[512,1024]{1,0:T(8,128)(2,1)} fusion(f32[512,1024]{1,0:T(8,128)} %reduce-scatter.2.cloned.1.call-done, f32[512,1536]{1,0:T(8,128)} %fusion.14), kind=kLoop, calls=%fused_computation.15 | loop fusion | flops 1048576 | bytes 5242880 | tf_op jit(solution)/shard_map/convert_element_type | solution.py:94
  (36 shorter events, 0.5 us)
Async XLA Ops:
  7.2 69.0 %copy-start = (bf16[16,1024,64]{1,2,0:T(8,128)(2,1)S(1)}, bf16[16,1024,64]{1,2,0:T(8,128)(2,1)}, u32[]{:S(2)}) copy-start(bf16[16,1024,64]{1,2,0:T(8,128)(2,1)} %param.9) | copy-start | bytes 6291460
  7.2 117.5 %all-gather.2.cloned.1.call-start = ((), (), s32[]{:S(2)}) async-start(), calls=%async_computation.5 | async-start | bytes 9437184 | tf_op jit(solution)/shard_map/all_gather | solution.py:32
  7.9 176.3 %reduce-scatter.2.cloned.1.call-start = ((), (), s32[]{:S(2)}) async-start(), calls=%async_computation.6 | async-start | bytes 18874368 | tf_op jit(solution)/shard_map/reduce_scatter | solution.py:50
  10.3 5.5 %copy-start.2 = (bf16[8192,512]{1,0:T(8,128)(2,1)S(1)}, bf16[8192,512]{1,0:T(8,128)(2,1)}, u32[]{:S(2)}) copy-start(bf16[8192,512]{1,0:T(8,128)(2,1)} %param.8) | copy-start | bytes 25165828
  10.3 5.4 %copy-start.4 = (bf16[512,512]{1,0:T(8,128)(2,1)S(1)}, bf16[512,512]{1,0:T(8,128)(2,1)}, u32[]{:S(2)}) copy-start(bf16[512,512]{1,0:T(8,128)(2,1)} %param.7) | copy-start | bytes 1572868
  76.1 4.0 %copy-start.5 = (bf16[1024,16]{0,1:T(8,128)(2,1)}, bf16[1024,16]{0,1:T(8,128)(2,1)S(1)}, u32[]{:S(2)}) copy-start(bf16[1024,16]{0,1:T(8,128)(2,1)S(1)} %copy.53) | copy-start | bytes 98308
  80.1 1.3 copy-start.7
  119.3 2.6 %copy-start.6 = (bf16[1024,16]{0,1:T(8,128)(2,1)S(1)}, bf16[1024,16]{0,1:T(8,128)(2,1)}, u32[]{:S(2)}) copy-start(bf16[1024,16]{0,1:T(8,128)(2,1)} %copy-done.5) | copy-start | bytes 98308
  127.6 50.7 %all-to-all-start.3 = ((bf16[16,64,1536]{2,1,0:T(8,128)(2,1)}), bf16[16,64,1536]{2,1,0:T(8,128)(2,1)S(1)}, u32[]{:S(2)}, u32[]{:S(2)}) async-start(bf16[16,64,1536]{2,1,0:T(8,128)(2,1)} %bitcast.11), calls=%async_computation.3 | async-start | bytes 6291456 | tf_op jit(solution)/shard_map/all_to_all | solution.py:85
  131.4 10.1 %slice-start = ((s8[8388608]{0:T(1024)(128)(4,1)}), s8[4194304]{0:T(1024)(128)(4,1)S(1)}, s32[]{:S(2)}) async-start(s8[8388608]{0:T(1024)(128)(4,1)} %bitcast.59), calls=%async_computation.7 | async-start | bytes 8388608
  135.4 6.1 %slice-start.1 = ((s8[8388608]{0:T(1024)(128)(4,1)}), s8[4194304]{0:T(1024)(128)(4,1)S(1)}, s32[]{:S(2)}) async-start(s8[8388608]{0:T(1024)(128)(4,1)} %bitcast.59), calls=%async_computation.8 | async-start | bytes 8388608
  178.3 3.5 %copy-start.3 = (f32[512,512]{1,0:T(8,128)S(1)}, f32[512,512]{1,0:T(8,128)}, u32[]{:S(2)}) copy-start(f32[512,512]{1,0:T(8,128)} %fusion.48) | copy-start | bytes 3145732
  181.8 5.9 %copy-start.1 = (bf16[16,1024,64]{1,2,0:T(8,128)(2,1)S(1)}, bf16[16,1024,64]{1,2,0:T(8,128)(2,1)}, u32[]{:S(2)}) copy-start(bf16[16,1024,64]{1,2,0:T(8,128)(2,1)} %param.9) | copy-start | bytes 6291460
Sparse Core Ops, SparseCore 0:
  9.7 53.2 all-gather.1
  65.5 102.2 reduce-scatter.1

commit v2 on v1

--- a/solution.py
+++ b/solution.py
@@ -8,13 +8,12 @@
 
 def tensor_sum(x):
     n = lax.axis_size("tensor")
-    rows = x.shape[0]
-    parts = x.reshape(n, rows // n, *x.shape[1:])
-    got = lax.all_to_all(parts, "tensor", split_axis=0, concat_axis=0, tiled=True)
-    mine = jnp.sum(got, axis=0)
-    spread = jnp.broadcast_to(mine[None], (n,) + mine.shape)
-    full = lax.all_to_all(spread, "tensor", split_axis=0, concat_axis=0, tiled=True)
-    return full.reshape(x.shape)
+    step = 1
+    while step < n:
+        perm = [(t, t ^ step) for t in range(n)]
+        x = x + lax.ppermute(x, "tensor", perm)
+        step *= 2
+    return x
 
 
 def per_device(

time: 195 us -> 201 us (1.031)
  blocking collectives: 85 us -> 50.6 us
  waiting for transfers between devices: 29.6 us -> 63.6 us
  starting transfers between devices: 3.83 us -> 10.4 us
    ppermute x0 -> x3, waiting for transfers between devices: none -> 37 us  [tensor_sum(): x = x + lax.ppermute(x, 'tensor', perm)]
    all_to_all x2 -> x0, blocking collectives: 34.4 us -> none  [the longest x1 18.6 us: tensor_sum(): lax.all_to_all(parts, 'tensor', split_axis=0, concat_axis=0, tiled=True)]
    ppermute x0 -> x3, starting transfers between devices: none -> 6.53 us  [tensor_sum(): x = x + lax.ppermute(x, 'tensor', perm)]
    all_to_all x1, waiting for transfers between devices: 28.9 us -> 25.8 us  [per_device(): back = lax.all_to_all(back, 'dp', split_axis=0, concat_axis=0, tiled=True)]
  transfers between devices with their start and end apart: 3 -> 6, of which waited for: 1 -> 4; matrix products, arithmetic and copies ran while one was open for 30% -> 28% of each run, Pallas kernels for 0% -> 0%
where the time goes in v2:
time: 201 us; the launch traced here: 199 us
  waiting for transfers between devices  63.6 us (32%)
  blocking collectives  50.6 us (25%)
  matrix products  46 us (23%)
  between operations  14.2 us (7%)
  starting transfers between devices  10.4 us (5%)
  other arithmetic  9.08 us (5%)
  local copies, waits for them, and re-layouts  5.05 us (3%)
    all_to_all x1, blocking collectives, per_device(): got = lax.all_to_all(send, 'dp', split_axis=0, concat_axis=0, tiled=True)  50.6 us
    ppermute x3, waiting for transfers between devices, tensor_sum(): x = x + lax.ppermute(x, 'tensor', perm)  37 us
    all_to_all x1, waiting for transfers between devices, per_device(): back = lax.all_to_all(back, 'dp', split_axis=0, concat_axis=0, tiled=True)  25.8 us
    dot_general x1, matrix products, per_device(): lax.dot_general(cot_late, weight_late, (((1,), (1,)), ((), ())), preferre...  8.65 us
    dot_general x1, matrix products, per_device(): jnp.dot(tokens_late, frozen_query_weight, preferred_element_type=jnp.floa...  7.97 us
    ppermute x3, starting transfers between devices, tensor_sum(): x = x + lax.ppermute(x, 'tensor', perm)  6.53 us
    dot_general x1, matrix products, per_device(): jnp.einsum('sd,sar->adr', got_tok, grad_spread, preferred_element_type=jn...  6.12 us
    dot_general x1, matrix products, per_device(): jnp.dot(pick, payload, preferred_element_type=jnp.float32)  5.43 us
  transfers between devices with their start and end apart: 6, of which 4 were waited for; matrix products, arithmetic and copies ran while one was open for 28% of the time, Pallas kernels for 0%

profile of v2, /device:TPU:1, one launch (start us, length us, event | category | flops | bytes accessed | tf_op | source)
XLA Modules:
  0.0 198.9 jit_solution(16574011863889636476)
XLA Ops:
  7.2 0.7 all-gather.2.cloned.1.call-update
  8.0 0.7 add_select_fusion.1
  8.7 1.2 reduce-window.6
  9.8 0.2 slice_reduce_fusion
  10.2 0.1 fusion.42
  10.4 5.4 %convolution_convert_fusion = bf16[1024,1664]{1,0:T(8,128)(2,1)} fusion(bf16[512,128]{1,0:T(8,128)(2,1)S(1)} %fusion.42, bf16[512,512]{1,0:T(8,128)(2,1)} %param.7, bf16[512,1024]{1,0:T(8,128)(2,1)} %param.6, s32[512]{0:T(512)S(1)} %multiply_add_fusion), kind=kOutput, calls=%fused_computation.3 | convolution fusion | flops 1752170496 | bytes 5113856 | tf_op jit(solution)/shard_map/dot_general | solution.py:44
  15.8 8.6 %fusion.51 = f32[512,8192]{1,0:T(8,128)} fusion(bf16[512,512]{1,0:T(8,128)(2,1)S(1)} %copy-done.4, bf16[8192,512]{1,0:T(8,128)(2,1)S(1)} %copy-done.2), kind=kOutput, calls=%fused_computation.70 | convolution fusion | flops 4294967296 | bytes 25690112 | tf_op jit(solution)/shard_map/dot_general | solution.py:46
  24.5 50.6 %all_to_all.24 = bf16[16,64,1664]{2,1,0:T(8,128)(2,1)} all-to-all(bf16[16,64,1664]{2,1,0:T(8,128)(2,1)} %bitcast.56), channel_id=1, replica_groups=mesh['dp'=16,'tensor'=8] {'dp'}, dimensions={0} | all-to-all | bytes 6815744 | tf_op jit(solution)/shard_map/all_to_all | solution.py:50
  75.1 1.0 slice.38
  76.0 0.1 copy.26
  76.2 4.0 %fusion.18 = f32[1024,1024]{0,1:S(1)} fusion(bf16[1024,1024]{0,1:T(8,128)(2,1)S(1)} %bitcast.52, bf16[1024,1664]{1,0:T(8,128)(2,1)} %bitcast.3), kind=kOutput, calls=%fused_computation.22 | convolution fusion | flops 2147483648 | bytes 8388608
  80.2 0.5 multiply_reduce_fusion.1
  80.7 0.7 copy-done.5
  81.4 2.6 %multiply_reduce_fusion = f32[1024,64]{0,1:T(8,128)S(1)} fusion(bf16[16,64,512]{2,1,0:T(8,128)(2,1)S(1)} %copy-done.5, f32[1024,16]{0,1:T(8,128)S(1)} %convert_element_type.37, bf16[1024,1664]{1,0:T(8,128)(2,1)} %bitcast.3), kind=kOutput, calls=%fused_computation.1 | convolution fusion | flops 1075773440 | bytes 2424832 | tf_op jit(solution)/shard_map/sq,arq->sar/dot_general | solution.py:59
  84.0 1.8 collective-permute-start
  85.8 1.5 collective-permute-done
  87.4 1.4 collective-permute-start.1
  88.9 18.0 %collective-permute-done.1 = f32[1024,128]{0,1:T(8,128)S(1)} collective-permute-done((f32[1024,128]{0,1:T(8,128)S(1)}, f32[1024,128]{0,1:T(8,128)S(1)}, u32[]{:S(2)}, u32[]{:S(2)}) %collective-permute-start.1) | collective-permute-done | bytes 524320 | tf_op jit(solution)/shard_map/ppermute | solution.py:14
  107.0 3.3 %collective-permute-start.2 = (f32[1024,128]{0,1:T(8,128)S(1)}, f32[1024,128]{0,1:T(8,128)S(1)}, u32[]{:S(2)}, u32[]{:S(2)}) collective-permute-start(f32[1024,128]{0,1:T(8,128)S(1)} %add.30), channel_id=1, source_target_pairs={{0,4},{1,5},{2,6},{3,7},{4,0},{5,1},{6,2},{7,3},{8,12},{9,13},{10,... | collective-permute-start | bytes 1572872 | tf_op jit(solution)/shard_map/ppermute | solution.py:14
  110.3 17.5 %collective-permute-done.2 = f32[1024,128]{0,1:T(8,128)S(1)} collective-permute-done((f32[1024,128]{0,1:T(8,128)S(1)}, f32[1024,128]{0,1:T(8,128)S(1)}, u32[]{:S(2)}, u32[]{:S(2)}) %collective-permute-start.2) | collective-permute-done | bytes 524320 | tf_op jit(solution)/shard_map/ppermute | solution.py:14
  127.8 1.3 fusion.13
  129.1 2.4 %bitcast_convert_fusion = bf16[1024,1024]{0,1:T(8,128)(2,1)S(1)} fusion(bf16[16,1024,64]{1,2,0:T(8,128)(2,1)S(1)} %copy-done, bf16[1024,64]{0,1:T(8,128)(2,1)S(1)} %fusion.41, bf16[1024,16]{0,1:T(8,128)(2,1)S(1)} %copy.26), kind=kOutput, calls=%fused_computation | convolution fusion | flops 2149580800 | bytes 4358144 | tf_op jit(solution)/shard_map/sar,adr->sd/dot_general | solution.py:74
  131.5 0.3 pad_maximum_fusion
  131.9 3.0 %copy.25 = bf16[1024,1536]{1,0:T(8,128)(2,1)} copy(bf16[1024,1536]{0,1:T(8,128)(2,1)S(1)} %pad_maximum_fusion) | data formatting | bytes 6291456 | tf_op jit(solution)/shard_map/optimization_barrier | solution.py:83
  134.8 3.8 %all-to-all-start.1 = ((bf16[16,64,1536]{2,1,0:T(8,128)(2,1)}), bf16[16,64,1536]{2,1,0:T(8,128)(2,1)S(1)}, u32[]{:S(2)}, u32[]{:S(2)}) async-start(bf16[16,64,1536]{2,1,0:T(8,128)(2,1)} %bitcast.10), calls=%async_computation.1 | async-start | bytes 6291456 | tf_op jit(solution)/shard_map/all_to_all | solution.py:84
  138.6 4.2 %fusion.27 = f32[16,64,512]{2,1,0:T(8,128)} fusion(bf16[1024,64]{0,1:T(8,128)(2,1)S(1)} %slice.65, bf16[1024,16]{0,1:T(8,128)(2,1)S(1)} %copy.26, bf16[1024,1664]{1,0:T(8,128)(2,1)} %bitcast.3), kind=kOutput, calls=%fused_computation.29 | convolution fusion | flops 1075314688 | bytes 3309568 | tf_op jit(solution)/shard_map/sar,sq->arq/dot_general | solution.py:78
  142.8 6.1 %fusion.8 = f32[16,1024,64]{1,2,0:T(8,128)} fusion(bf16[1024,1664]{1,0:T(8,128)(2,1)} %bitcast.3, bf16[1024,64]{0,1:T(8,128)(2,1)S(1)} %fusion.41, bf16[1024,16]{0,1:T(8,128)(2,1)S(1)} %copy.26), kind=kOutput, calls=%fused_computation.13 | convolution fusion | flops 2148532224 | bytes 6455296 | tf_op jit(solution)/shard_map/sd,sar->adr/dot_general | solution.py:77
  148.9 8.0 %fusion.50 = f32[512,512]{1,0:T(8,128)} fusion(bf16[512,8192]{1,0:T(8,128)(2,1)} %all-gather.2.cloned.1.call-done, bf16[8192,512]{1,0:T(8,128)(2,1)S(1)} %bitcast.54), kind=kOutput, calls=%fused_computation.69 | convolution fusion | flops 4294967296 | bytes 17825792 | tf_op jit(solution)/shard_map/dot_general | solution.py:86
  156.9 25.8 %all-to-all-done.1 = bf16[16,64,1536]{2,1,0:T(8,128)(2,1)S(1)} async-done(((bf16[16,64,1536]{2,1,0:T(8,128)(2,1)}), bf16[16,64,1536]{2,1,0:T(8,128)(2,1)S(1)}, u32[]{:S(2)}, u32[]{:S(2)}) %all-to-all-start.1) | async-done | bytes 3145760 | tf_op jit(solution)/shard_map/all_to_all | solution.py:84
  182.7 3.5 %fusion.14 = f32[512,1536]{1,0:T(8,128)} fusion(bf16[1024,1536]{1,0:T(8,128)(2,1)S(1)} %bitcast.57, s32[512]{0:T(512)S(1)} %multiply_add_fusion), kind=kOutput, calls=%fused_computation.20 | convolution fusion | flops 1611137024 | bytes 6293504 | tf_op jit(solution)/shard_map/st,sc->tc/dot_general | solution.py:88
  186.2 2.3 %fusion.30 = bf16[512,512]{1,0:T(8,128)(2,1)} fusion(f32[512,512]{1,0:T(8,128)S(1)} %copy-done.3, f32[512,1536]{1,0:T(8,128)} %fusion.14), kind=kLoop, calls=%fused_computation.31 | loop fusion | flops 524288 | bytes 2621440 | tf_op jit(solution)/shard_map/convert_element_type | solution.py:92
  188.5 3.5 %fusion.11 = bf16[512,1024]{1,0:T(8,128)(2,1)} fusion(f32[512,1024]{1,0:T(8,128)} %reduce-scatter.2.cloned.1.call-done, f32[512,1536]{1,0:T(8,128)} %fusion.14), kind=kLoop, calls=%fused_computation.15 | loop fusion | flops 1048576 | bytes 5242880 | tf_op jit(solution)/shard_map/convert_element_type | solution.py:93
  (33 shorter events, 0.6 us)
Async XLA Ops:
  7.2 69.0 %copy-start = (bf16[16,1024,64]{1,2,0:T(8,128)(2,1)S(1)}, bf16[16,1024,64]{1,2,0:T(8,128)(2,1)}, u32[]{:S(2)}) copy-start(bf16[16,1024,64]{1,2,0:T(8,128)(2,1)} %param.9) | copy-start | bytes 6291460
  7.2 124.7 %all-gather.2.cloned.1.call-start = ((), (), s32[]{:S(2)}) async-start(), calls=%async_computation.3 | async-start | bytes 9437184 | tf_op jit(solution)/shard_map/all_gather | solution.py:31
  7.9 180.6 %reduce-scatter.2.cloned.1.call-start = ((), (), s32[]{:S(2)}) async-start(), calls=%async_computation.4 | async-start | bytes 18874368 | tf_op jit(solution)/shard_map/reduce_scatter | solution.py:49
  10.3 5.5 %copy-start.2 = (bf16[8192,512]{1,0:T(8,128)(2,1)S(1)}, bf16[8192,512]{1,0:T(8,128)(2,1)}, u32[]{:S(2)}) copy-start(bf16[8192,512]{1,0:T(8,128)(2,1)} %param.8) | copy-start | bytes 25165828
  10.3 5.4 %copy-start.4 = (bf16[512,512]{1,0:T(8,128)(2,1)S(1)}, bf16[512,512]{1,0:T(8,128)(2,1)}, u32[]{:S(2)}) copy-start(bf16[512,512]{1,0:T(8,128)(2,1)} %param.7) | copy-start | bytes 1572868
  80.1 1.3 copy-start.5
  84.0 3.4 %collective-permute-start = (f32[1024,128]{0,1:T(8,128)S(1)}, f32[1024,128]{0,1:T(8,128)S(1)}, u32[]{:S(2)}, u32[]{:S(2)}) collective-permute-start(f32[1024,128]{0,1:T(8,128)S(1)} %pad_maximum_fusion.1), channel_id=1, source_target_pairs={{0,1},{1,0},{2,3},{3,2},{4,5},{5,4},{6,7},{7,6},{8,9},{9,8},{10,11... | collective-permute-start | bytes 1572872 | tf_op jit(solution)/shard_map/ppermute | solution.py:14
  87.4 19.4 %collective-permute-start.1 = (f32[1024,128]{0,1:T(8,128)S(1)}, f32[1024,128]{0,1:T(8,128)S(1)}, u32[]{:S(2)}, u32[]{:S(2)}) collective-permute-start(f32[1024,128]{0,1:T(8,128)S(1)} %fusion.49), channel_id=1, source_target_pairs={{0,2},{1,3},{2,0},{3,1},{4,6},{5,7},{6,4},{7,5},{8,10},{9,11},{10,... | collective-permute-start | bytes 1572872 | tf_op jit(solution)/shard_map/ppermute | solution.py:14
  107.0 20.8 %collective-permute-start.2 = (f32[1024,128]{0,1:T(8,128)S(1)}, f32[1024,128]{0,1:T(8,128)S(1)}, u32[]{:S(2)}, u32[]{:S(2)}) collective-permute-start(f32[1024,128]{0,1:T(8,128)S(1)} %add.30), channel_id=1, source_target_pairs={{0,4},{1,5},{2,6},{3,7},{4,0},{5,1},{6,2},{7,3},{8,12},{9,13},{10,... | collective-permute-start | bytes 1572872 | tf_op jit(solution)/shard_map/ppermute | solution.py:14
  134.8 47.8 %all-to-all-start.1 = ((bf16[16,64,1536]{2,1,0:T(8,128)(2,1)}), bf16[16,64,1536]{2,1,0:T(8,128)(2,1)S(1)}, u32[]{:S(2)}, u32[]{:S(2)}) async-start(bf16[16,64,1536]{2,1,0:T(8,128)(2,1)} %bitcast.10), calls=%async_computation.1 | async-start | bytes 6291456 | tf_op jit(solution)/shard_map/all_to_all | solution.py:84
  138.6 10.3 %slice-start = ((s8[8388608]{0:T(1024)(128)(4,1)}), s8[4194304]{0:T(1024)(128)(4,1)S(1)}, s32[]{:S(2)}) async-start(s8[8388608]{0:T(1024)(128)(4,1)} %bitcast.53), calls=%async_computation.5 | async-start | bytes 8388608
  142.8 6.1 %slice-start.1 = ((s8[8388608]{0:T(1024)(128)(4,1)}), s8[4194304]{0:T(1024)(128)(4,1)S(1)}, s32[]{:S(2)}) async-start(s8[8388608]{0:T(1024)(128)(4,1)} %bitcast.53), calls=%async_computation.6 | async-start | bytes 8388608
  182.7 3.5 %copy-start.3 = (f32[512,512]{1,0:T(8,128)S(1)}, f32[512,512]{1,0:T(8,128)}, u32[]{:S(2)}) copy-start(f32[512,512]{1,0:T(8,128)} %fusion.50) | copy-start | bytes 3145732
  186.2 5.9 %copy-start.1 = (bf16[16,1024,64]{1,2,0:T(8,128)(2,1)S(1)}, bf16[16,1024,64]{1,2,0:T(8,128)(2,1)}, u32[]{:S(2)}) copy-start(bf16[16,1024,64]{1,2,0:T(8,128)(2,1)} %param.9) | copy-start | bytes 6291460
Sparse Core Ops, SparseCore 0:
  9.7 53.2 all-gather.1
  65.5 113.3 reduce-scatter.1

commit v3 on v2

--- a/solution.py
+++ b/solution.py
@@ -8,12 +8,21 @@
 
 def tensor_sum(x):
     n = lax.axis_size("tensor")
-    step = 1
+    half = x.shape[0] // 2
+    core = lax.axis_index("tensor") % 2
+    keep = lax.dynamic_slice_in_dim(x, core * half, half, axis=0)
+    give = lax.dynamic_slice_in_dim(x, (1 - core) * half, half, axis=0)
+    pair = [(t, t ^ 1) for t in range(n)]
+    mine = keep + lax.ppermute(give, "tensor", pair)
+    step = 2
     while step < n:
         perm = [(t, t ^ step) for t in range(n)]
-        x = x + lax.ppermute(x, "tensor", perm)
+        mine = mine + lax.ppermute(mine, "tensor", perm)
         step *= 2
-    return x
+    other = lax.ppermute(mine, "tensor", pair)
+    first = jnp.where(core == 0, mine, other)
+    second = jnp.where(core == 0, other, mine)
+    return jnp.concatenate([first, second], axis=0)
 
 
 def per_device(

time: 201 us -> 200 us (level)
  blocking collectives: 50.6 us -> 0 us
  waiting for transfers between devices: 63.6 us -> 102 us
  starting transfers between devices: 10.4 us -> 21.6 us
    all_to_all x0 -> x1, waiting for transfers between devices: none -> 50.7 us  [per_device(): got = lax.all_to_all(send, 'dp', split_axis=0, concat_axis=0, tiled=True)]
    all_to_all x1 -> x0, blocking collectives: 50.6 us -> none  [per_device(): got = lax.all_to_all(send, 'dp', split_axis=0, concat_axis=0, tiled=True)]
    ppermute x3 -> x4, waiting for transfers between devices: 37 us -> 21.1 us  [the longest x2 18.7 us: tensor_sum(): mine = mine + lax.ppermute(mine, 'tensor', perm)]
    all_to_all x0 -> x1, starting transfers between devices: none -> 8.92 us  [per_device(): got = lax.all_to_all(send, 'dp', split_axis=0, concat_axis=0, tiled=True)]
    all_to_all x1, waiting for transfers between devices: 25.8 us -> 29.5 us  [per_device(): back = lax.all_to_all(back, 'dp', split_axis=0, concat_axis=0, tiled=True)]
    ppermute x3 -> x4, starting transfers between devices: 6.53 us -> 8.38 us  [the longest x2 4.35 us: tensor_sum(): mine = mine + lax.ppermute(mine, 'tensor', perm)]
  transfers between devices with their start and end apart: 6 -> 8, of which waited for: 4 -> 6; matrix products, arithmetic and copies ran while one was open for 28% -> 29% of each run, Pallas kernels for 0% -> 0%
where the time goes in v3:
time: 200 us; the launch traced here: 199 us
  waiting for transfers between devices  102 us (51%)
  matrix products  47.1 us (24%)
  starting transfers between devices  21.6 us (11%)
  between operations  14.3 us (7%)
  other arithmetic  9.02 us (5%)
  local copies, waits for them, and re-layouts  5.05 us (3%)
    all_to_all x1, waiting for transfers between devices, per_device(): got = lax.all_to_all(send, 'dp', split_axis=0, concat_axis=0, tiled=True)  50.7 us
    all_to_all x1, waiting for transfers between devices, per_device(): back = lax.all_to_all(back, 'dp', split_axis=0, concat_axis=0, tiled=True)  29.5 us
    ppermute x2, waiting for transfers between devices, tensor_sum(): mine = mine + lax.ppermute(mine, 'tensor', perm)  18.7 us
    all_to_all x1, starting transfers between devices, per_device(): got = lax.all_to_all(send, 'dp', split_axis=0, concat_axis=0, tiled=True)  8.92 us
    dot_general x1, matrix products, per_device(): lax.dot_general(cot_late, weight_late, (((1,), (1,)), ((), ())), preferre...  8.65 us
    dot_general x1, matrix products, per_device(): jnp.dot(tokens_late, frozen_query_weight, preferred_element_type=jnp.floa...  8 us
    dot_general x1, matrix products, per_device(): jnp.einsum('sd,sar->adr', got_tok, grad_spread, preferred_element_type=jn...  6.13 us
    dot_general x1, matrix products, per_device(): jnp.dot(pick, payload, preferred_element_type=jnp.float32)  5.43 us
  transfers between devices with their start and end apart: 8, of which 6 were waited for; matrix products, arithmetic and copies ran while one was open for 29% of the time, Pallas kernels for 0%

profile of v3, /device:TPU:1, one launch (start us, length us, event | category | flops | bytes accessed | tf_op | source)
XLA Modules:
  0.0 199.1 jit_solution(10571462115131809670)
XLA Ops:
  7.2 0.7 all-gather.2.cloned.1.call-update
  8.0 0.7 add_select_fusion.1
  8.7 1.2 reduce-window.6
  10.4 5.4 %convolution_convert_fusion = bf16[1024,1664]{1,0:T(8,128)(2,1)} fusion(bf16[512,128]{1,0:T(8,128)(2,1)S(1)} %fusion.48, bf16[512,512]{1,0:T(8,128)(2,1)} %param.7, bf16[512,1024]{1,0:T(8,128)(2,1)} %param.6, s32[512]{0:T(512)S(1)} %multiply_add_fusion), kind=kOutput, calls=%fused_computation.3 | convolution fusion | flops 1752170496 | bytes 5113856 | tf_op jit(solution)/shard_map/dot_general | solution.py:53
  15.8 8.6 %fusion.56 = f32[512,8192]{1,0:T(8,128)} fusion(bf16[512,512]{1,0:T(8,128)(2,1)S(1)} %copy-done.4, bf16[8192,512]{1,0:T(8,128)(2,1)S(1)} %copy-done.2), kind=kOutput, calls=%fused_computation.81 | convolution fusion | flops 4294967296 | bytes 25690112 | tf_op jit(solution)/shard_map/dot_general | solution.py:55
  24.5 8.9 %all-to-all-start = ((bf16[16,64,1664]{2,1,0:T(8,128)(2,1)}), bf16[16,64,1664]{2,1,0:T(8,128)(2,1)}, u32[]{:S(2)}, u32[]{:S(2)}) async-start(bf16[16,64,1664]{2,1,0:T(8,128)(2,1)} %bitcast.56), calls=%async_computation | async-start | bytes 6815744 | tf_op jit(solution)/shard_map/all_to_all | solution.py:59
  33.4 50.7 %all-to-all-done = bf16[16,64,1664]{2,1,0:T(8,128)(2,1)} async-done(((bf16[16,64,1664]{2,1,0:T(8,128)(2,1)}), bf16[16,64,1664]{2,1,0:T(8,128)(2,1)}, u32[]{:S(2)}, u32[]{:S(2)}) %all-to-all-start) | async-done | bytes 3407904 | tf_op jit(solution)/shard_map/all_to_all | solution.py:59
  84.1 1.0 slice.38
  85.2 4.0 %fusion.18 = f32[1024,1024]{0,1:S(1)} fusion(bf16[1024,1024]{0,1:T(8,128)(2,1)S(1)} %bitcast.52, bf16[1024,1664]{1,0:T(8,128)(2,1)} %bitcast.3), kind=kOutput, calls=%fused_computation.22 | convolution fusion | flops 2147483648 | bytes 8388608
  89.2 0.5 multiply_reduce_fusion.1
  89.8 0.7 copy-done.5
  90.4 2.6 %multiply_reduce_fusion = f32[1024,64]{0,1:T(8,128)S(1)} fusion(bf16[16,64,512]{2,1,0:T(8,128)(2,1)S(1)} %copy-done.5, f32[1024,16]{0,1:T(8,128)S(1)} %convert_element_type.37, bf16[1024,1664]{1,0:T(8,128)(2,1)} %bitcast.3), kind=kOutput, calls=%fused_computation.1 | convolution fusion | flops 1075773440 | bytes 2424832 | tf_op jit(solution)/shard_map/sq,arq->sar/dot_general | solution.py:68
  93.1 1.9 collective-permute-start
  95.0 1.2 collective-permute-done
  96.2 1.5 collective-permute-start.1
  97.7 9.5 %collective-permute-done.1 = f32[512,128]{0,1:T(8,128)S(1)} collective-permute-done((f32[512,128]{0,1:T(8,128)S(1)}, f32[512,128]{0,1:T(8,128)S(1)}, u32[]{:S(2)}, u32[]{:S(2)}) %collective-permute-start.1) | collective-permute-done | bytes 262176 | tf_op jit(solution)/shard_map/ppermute | solution.py:20
  107.3 2.9 %collective-permute-start.2 = (f32[512,128]{0,1:T(8,128)S(1)}, f32[512,128]{0,1:T(8,128)S(1)}, u32[]{:S(2)}, u32[]{:S(2)}) collective-permute-start(f32[512,128]{0,1:T(8,128)S(1)} %add.43), channel_id=1, source_target_pairs={{0,4},{1,5},{2,6},{3,7},{4,0},{5,1},{6,2},{7,3},{8,12},{9,13},{10,... | collective-permute-start | bytes 786440 | tf_op jit(solution)/shard_map/ppermute | solution.py:20
  110.2 9.2 %collective-permute-done.2 = f32[512,128]{0,1:T(8,128)S(1)} collective-permute-done((f32[512,128]{0,1:T(8,128)S(1)}, f32[512,128]{0,1:T(8,128)S(1)}, u32[]{:S(2)}, u32[]{:S(2)}) %collective-permute-start.2) | collective-permute-done | bytes 262176 | tf_op jit(solution)/shard_map/ppermute | solution.py:20
  119.3 2.1 %collective-permute-start.3 = (f32[512,128]{0,1:T(8,128)S(1)}, f32[512,128]{0,1:T(8,128)S(1)}, u32[]{:S(2)}, u32[]{:S(2)}) collective-permute-start(f32[512,128]{0,1:T(8,128)S(1)} %add.44), channel_id=1, source_target_pairs={{0,1},{1,0},{2,3},{3,2},{4,5},{5,4},{6,7},{7,6},{8,9},{9,8},{10,11... | collective-permute-start | bytes 786440 | tf_op jit(solution)/shard_map/ppermute | solution.py:22
  121.5 1.2 collective-permute-done.3
  122.8 2.5 %fusion.13 = bf16[1024,512]{0,1:T(8,128)(2,1)S(1)} fusion(bf16[16,64,512]{2,1,0:T(8,128)(2,1)} %param.10, bf16[1024,64]{0,1:T(8,128)(2,1)S(1)} %fusion.42, bf16[1024,16]{0,1:T(8,128)(2,1)S(1)} %copy.26), kind=kOutput, calls=%fused_computation.18 | convolution fusion | flops 1075838976 | bytes 2260992 | tf_op jit(solution)/shard_map/sar,arq->sq/dot_general | solution.py:81
  125.3 2.4 %bitcast_convert_fusion = bf16[1024,1024]{0,1:T(8,128)(2,1)S(1)} fusion(bf16[16,1024,64]{1,2,0:T(8,128)(2,1)S(1)} %copy-done, bf16[1024,64]{0,1:T(8,128)(2,1)S(1)} %fusion.47, bf16[1024,16]{0,1:T(8,128)(2,1)S(1)} %copy.26), kind=kOutput, calls=%fused_computation | convolution fusion | flops 2149580800 | bytes 4358144 | tf_op jit(solution)/shard_map/sar,adr->sd/dot_general | solution.py:83
  127.7 0.3 pad_maximum_fusion
  128.0 3.0 %copy.25 = bf16[1024,1536]{1,0:T(8,128)(2,1)} copy(bf16[1024,1536]{0,1:T(8,128)(2,1)S(1)} %pad_maximum_fusion) | data formatting | bytes 6291456 | tf_op jit(solution)/shard_map/optimization_barrier | solution.py:92
  131.1 4.3 %all-to-all-start.1 = ((bf16[16,64,1536]{2,1,0:T(8,128)(2,1)}), bf16[16,64,1536]{2,1,0:T(8,128)(2,1)S(1)}, u32[]{:S(2)}, u32[]{:S(2)}) async-start(bf16[16,64,1536]{2,1,0:T(8,128)(2,1)} %bitcast.10), calls=%async_computation.1 | async-start | bytes 6291456 | tf_op jit(solution)/shard_map/all_to_all | solution.py:93
  135.3 4.0 %fusion.27 = f32[16,64,512]{2,1,0:T(8,128)} fusion(bf16[1024,64]{0,1:T(8,128)(2,1)S(1)} %fusion.42, bf16[1024,16]{0,1:T(8,128)(2,1)S(1)} %copy.26, bf16[1024,1664]{1,0:T(8,128)(2,1)} %bitcast.3), kind=kOutput, calls=%fused_computation.29 | convolution fusion | flops 1075314688 | bytes 3309568 | tf_op jit(solution)/shard_map/sar,sq->arq/dot_general | solution.py:87
  139.3 6.1 %fusion.8 = f32[16,1024,64]{1,2,0:T(8,128)} fusion(bf16[1024,1664]{1,0:T(8,128)(2,1)} %bitcast.3, bf16[1024,64]{0,1:T(8,128)(2,1)S(1)} %fusion.47, bf16[1024,16]{0,1:T(8,128)(2,1)S(1)} %copy.26), kind=kOutput, calls=%fused_computation.13 | convolution fusion | flops 2148532224 | bytes 6455296 | tf_op jit(solution)/shard_map/sd,sar->adr/dot_general | solution.py:86
  145.4 8.0 %fusion.55 = f32[512,512]{1,0:T(8,128)} fusion(bf16[512,8192]{1,0:T(8,128)(2,1)} %all-gather.2.cloned.1.call-done, bf16[8192,512]{1,0:T(8,128)(2,1)S(1)} %bitcast.54), kind=kOutput, calls=%fused_computation.80 | convolution fusion | flops 4294967296 | bytes 17825792 | tf_op jit(solution)/shard_map/dot_general | solution.py:95
  153.4 29.5 %all-to-all-done.1 = bf16[16,64,1536]{2,1,0:T(8,128)(2,1)S(1)} async-done(((bf16[16,64,1536]{2,1,0:T(8,128)(2,1)}), bf16[16,64,1536]{2,1,0:T(8,128)(2,1)S(1)}, u32[]{:S(2)}, u32[]{:S(2)}) %all-to-all-start.1) | async-done | bytes 3145760 | tf_op jit(solution)/shard_map/all_to_all | solution.py:93
  182.9 3.5 %fusion.14 = f32[512,1536]{1,0:T(8,128)} fusion(bf16[1024,1536]{1,0:T(8,128)(2,1)S(1)} %bitcast.57, s32[512]{0:T(512)S(1)} %multiply_add_fusion), kind=kOutput, calls=%fused_computation.20 | convolution fusion | flops 1611137024 | bytes 6293504 | tf_op jit(solution)/shard_map/st,sc->tc/dot_general | solution.py:97
  186.4 2.3 %fusion.30 = bf16[512,512]{1,0:T(8,128)(2,1)} fusion(f32[512,512]{1,0:T(8,128)S(1)} %copy-done.3, f32[512,1536]{1,0:T(8,128)} %fusion.14), kind=kLoop, calls=%fused_computation.31 | loop fusion | flops 524288 | bytes 2621440 | tf_op jit(solution)/shard_map/convert_element_type | solution.py:101
  188.8 3.5 %fusion.11 = bf16[512,1024]{1,0:T(8,128)(2,1)} fusion(f32[512,1024]{1,0:T(8,128)} %reduce-scatter.2.cloned.1.call-done, f32[512,1536]{1,0:T(8,128)} %fusion.14), kind=kLoop, calls=%fused_computation.15 | loop fusion | flops 1048576 | bytes 5242880 | tf_op jit(solution)/shard_map/convert_element_type | solution.py:102
  (37 shorter events, 1.0 us)
Async XLA Ops:
  7.2 78.0 %copy-start = (bf16[16,1024,64]{1,2,0:T(8,128)(2,1)S(1)}, bf16[16,1024,64]{1,2,0:T(8,128)(2,1)}, u32[]{:S(2)}) copy-start(bf16[16,1024,64]{1,2,0:T(8,128)(2,1)} %param.9) | copy-start | bytes 6291460
  7.2 120.9 %all-gather.2.cloned.1.call-start = ((), (), s32[]{:S(2)}) async-start(), calls=%async_computation.3 | async-start | bytes 9437184 | tf_op jit(solution)/shard_map/all_gather | solution.py:40
  7.9 180.9 %reduce-scatter.2.cloned.1.call-start = ((), (), s32[]{:S(2)}) async-start(), calls=%async_computation.4 | async-start | bytes 18874368 | tf_op jit(solution)/shard_map/reduce_scatter | solution.py:58
  10.3 5.5 %copy-start.2 = (bf16[8192,512]{1,0:T(8,128)(2,1)S(1)}, bf16[8192,512]{1,0:T(8,128)(2,1)}, u32[]{:S(2)}) copy-start(bf16[8192,512]{1,0:T(8,128)(2,1)} %param.8) | copy-start | bytes 25165828
  10.3 5.4 %copy-start.4 = (bf16[512,512]{1,0:T(8,128)(2,1)S(1)}, bf16[512,512]{1,0:T(8,128)(2,1)}, u32[]{:S(2)}) copy-start(bf16[512,512]{1,0:T(8,128)(2,1)} %param.7) | copy-start | bytes 1572868
  24.5 59.6 %all-to-all-start = ((bf16[16,64,1664]{2,1,0:T(8,128)(2,1)}), bf16[16,64,1664]{2,1,0:T(8,128)(2,1)}, u32[]{:S(2)}, u32[]{:S(2)}) async-start(bf16[16,64,1664]{2,1,0:T(8,128)(2,1)} %bitcast.56), calls=%async_computation | async-start | bytes 6815744 | tf_op jit(solution)/shard_map/all_to_all | solution.py:59
  89.2 1.2 copy-start.5
  93.1 3.1 %collective-permute-start = (f32[512,128]{0,1:T(8,128)S(1)}, f32[512,128]{0,1:T(8,128)S(1)}, u32[]{:S(2)}, u32[]{:S(2)}) collective-permute-start(f32[512,128]{0,1:T(8,128)S(1)} %fusion.43), channel_id=1, source_target_pairs={{0,1},{1,0},{2,3},{3,2},{4,5},{5,4},{6,7},{7,6},{8,9},{9,8},{10,11... | collective-permute-start | bytes 786440 | tf_op jit(solution)/shard_map/ppermute | solution.py:16
  96.2 11.0 %collective-permute-start.1 = (f32[512,128]{0,1:T(8,128)S(1)}, f32[512,128]{0,1:T(8,128)S(1)}, u32[]{:S(2)}, u32[]{:S(2)}) collective-permute-start(f32[512,128]{0,1:T(8,128)S(1)} %fusion.45), channel_id=1, source_target_pairs={{0,2},{1,3},{2,0},{3,1},{4,6},{5,7},{6,4},{7,5},{8,10},{9,11},{10,... | collective-permute-start | bytes 786440 | tf_op jit(solution)/shard_map/ppermute | solution.py:20
  107.3 12.1 %collective-permute-start.2 = (f32[512,128]{0,1:T(8,128)S(1)}, f32[512,128]{0,1:T(8,128)S(1)}, u32[]{:S(2)}, u32[]{:S(2)}) collective-permute-start(f32[512,128]{0,1:T(8,128)S(1)} %add.43), channel_id=1, source_target_pairs={{0,4},{1,5},{2,6},{3,7},{4,0},{5,1},{6,2},{7,3},{8,12},{9,13},{10,... | collective-permute-start | bytes 786440 | tf_op jit(solution)/shard_map/ppermute | solution.py:20
  119.3 3.3 %collective-permute-start.3 = (f32[512,128]{0,1:T(8,128)S(1)}, f32[512,128]{0,1:T(8,128)S(1)}, u32[]{:S(2)}, u32[]{:S(2)}) collective-permute-start(f32[512,128]{0,1:T(8,128)S(1)} %add.44), channel_id=1, source_target_pairs={{0,1},{1,0},{2,3},{3,2},{4,5},{5,4},{6,7},{7,6},{8,9},{9,8},{10,11... | collective-permute-start | bytes 786440 | tf_op jit(solution)/shard_map/ppermute | solution.py:22
  131.1 51.9 %all-to-all-start.1 = ((bf16[16,64,1536]{2,1,0:T(8,128)(2,1)}), bf16[16,64,1536]{2,1,0:T(8,128)(2,1)S(1)}, u32[]{:S(2)}, u32[]{:S(2)}) async-start(bf16[16,64,1536]{2,1,0:T(8,128)(2,1)} %bitcast.10), calls=%async_computation.1 | async-start | bytes 6291456 | tf_op jit(solution)/shard_map/all_to_all | solution.py:93
  135.3 10.1 %slice-start = ((s8[8388608]{0:T(1024)(128)(4,1)}), s8[4194304]{0:T(1024)(128)(4,1)S(1)}, s32[]{:S(2)}) async-start(s8[8388608]{0:T(1024)(128)(4,1)} %bitcast.53), calls=%async_computation.5 | async-start | bytes 8388608
  139.3 6.1 %slice-start.1 = ((s8[8388608]{0:T(1024)(128)(4,1)}), s8[4194304]{0:T(1024)(128)(4,1)S(1)}, s32[]{:S(2)}) async-start(s8[8388608]{0:T(1024)(128)(4,1)} %bitcast.53), calls=%async_computation.6 | async-start | bytes 8388608
  182.9 3.5 %copy-start.3 = (f32[512,512]{1,0:T(8,128)S(1)}, f32[512,512]{1,0:T(8,128)}, u32[]{:S(2)}) copy-start(f32[512,512]{1,0:T(8,128)} %fusion.55) | copy-start | bytes 3145732
  186.4 5.9 %copy-start.1 = (bf16[16,1024,64]{1,2,0:T(8,128)(2,1)S(1)}, bf16[16,1024,64]{1,2,0:T(8,128)(2,1)}, u32[]{:S(2)}) copy-start(bf16[16,1024,64]{1,2,0:T(8,128)(2,1)} %param.9) | copy-start | bytes 6291460
Sparse Core Ops, SparseCore 0:
  9.7 53.2 all-gather.1
  65.5 102.0 reduce-scatter.1

commit v4 on v3

--- a/solution.py
+++ b/solution.py
@@ -6,12 +6,11 @@
 adapter_factor = 0.5
 
 
-def tensor_sum(x):
+def tensor_sum(x, keep_first):
     n = lax.axis_size("tensor")
     half = x.shape[0] // 2
-    core = lax.axis_index("tensor") % 2
-    keep = lax.dynamic_slice_in_dim(x, core * half, half, axis=0)
-    give = lax.dynamic_slice_in_dim(x, (1 - core) * half, half, axis=0)
+    keep = jnp.where(keep_first, x[:half], x[half:])
+    give = jnp.where(keep_first, x[half:], x[:half])
     pair = [(t, t ^ 1) for t in range(n)]
     mine = keep + lax.ppermute(give, "tensor", pair)
     step = 2
@@ -20,8 +19,8 @@
         mine = mine + lax.ppermute(mine, "tensor", perm)
         step *= 2
     other = lax.ppermute(mine, "tensor", pair)
-    first = jnp.where(core == 0, mine, other)
-    second = jnp.where(core == 0, other, mine)
+    first = jnp.where(keep_first, mine, other)
+    second = jnp.where(keep_first, other, mine)
     return jnp.concatenate([first, second], axis=0)
 
 
@@ -51,7 +50,10 @@
     )
     payload = jnp.concatenate([tokens, cotangent, local_hot], axis=1)
     send = jnp.dot(pick, payload, preferred_element_type=jnp.float32).astype(jnp.bfloat16)
-    send, cot_late, weight_late = lax.optimization_barrier((send, cotangent, frozen_query_weight))
+    keep_first = lax.axis_index("tensor") % 2 == 0
+    send, cot_late, weight_late, keep_first = lax.optimization_barrier(
+        (send, cotangent, frozen_query_weight, keep_first)
+    )
     partial_term = lax.dot_general(
         cot_late, weight_late, (((1,), (1,)), ((), ())), preferred_element_type=jnp.float32
     )
@@ -70,7 +72,7 @@
     )
     hidden_part = jnp.sum(hidden_all * hot_f[:, :, None], axis=1)
     grad_part = jnp.sum(grad_all * hot_f[:, :, None], axis=1)
-    joined = tensor_sum(jnp.concatenate([hidden_part, grad_part], axis=1))
+    joined = tensor_sum(jnp.concatenate([hidden_part, grad_part], axis=1), keep_first)
     lowrank_round = joined[:, :rank_columns].astype(jnp.bfloat16)
     gradient_round = (adapter_factor * joined[:, rank_columns:]).astype(jnp.bfloat16)
     low_spread = got_hot[:, :, None] * lowrank_round[:, None, :]

time: 200 us -> 189 us (0.945)
  blocking collectives: 0 us -> 50.6 us
  waiting for transfers between devices: 102 us -> 51.4 us
  starting transfers between devices: 21.6 us -> 12.2 us
    all_to_all x1 -> x0, waiting for transfers between devices: 50.7 us -> none  [per_device(): got = lax.all_to_all(send, 'dp', split_axis=0, concat_axis=0, tiled=True)]
    all_to_all x0 -> x1, blocking collectives: none -> 50.6 us  [per_device(): got = lax.all_to_all(send, 'dp', split_axis=0, concat_axis=0, tiled=True)]
    all_to_all x1 -> x0, starting transfers between devices: 8.92 us -> none  [per_device(): got = lax.all_to_all(send, 'dp', split_axis=0, concat_axis=0, tiled=True)]
  transfers between devices with their start and end apart: 8 -> 7, of which waited for: 6 -> 5; matrix products, arithmetic and copies ran while one was open for 29% -> 30% of each run, Pallas kernels for 0% -> 0%
where the time goes in v4:
time: 189 us; the launch traced here: 188 us
  waiting for transfers between devices  51.4 us (27%)
  blocking collectives  50.6 us (27%)
  matrix products  45.9 us (24%)
  between operations  14.2 us (8%)
  starting transfers between devices  12.2 us (6%)
  other arithmetic  9.06 us (5%)
  local copies, waits for them, and re-layouts  5.05 us (3%)
    all_to_all x1, blocking collectives, per_device(): got = lax.all_to_all(send, 'dp', split_axis=0, concat_axis=0, tiled=True)  50.6 us
    all_to_all x1, waiting for transfers between devices, per_device(): back = lax.all_to_all(back, 'dp', split_axis=0, concat_axis=0, tiled=True)  29.7 us
    ppermute x2, waiting for transfers between devices, tensor_sum(): mine = mine + lax.ppermute(mine, 'tensor', perm)  18.6 us
    dot_general x1, matrix products, per_device(): lax.dot_general(cot_late, weight_late, (((1,), (1,)), ((), ())), preferre...  8.65 us
    dot_general x1, matrix products, per_device(): jnp.dot(tokens_late, frozen_query_weight, preferred_element_type=jnp.floa...  7.99 us
    dot_general x1, matrix products, per_device(): jnp.einsum('sd,sar->adr', got_tok, grad_spread, preferred_element_type=jn...  6.12 us
    dot_general x1, matrix products, per_device(): jnp.dot(pick, payload, preferred_element_type=jnp.float32)  5.43 us
    ppermute x2, starting transfers between devices, tensor_sum(): mine = mine + lax.ppermute(mine, 'tensor', perm)  4.45 us
  transfers between devices with their start and end apart: 7, of which 5 were waited for; matrix products, arithmetic and copies ran while one was open for 30% of the time, Pallas kernels for 0%

profile of v4, /device:TPU:1, one launch (start us, length us, event | category | flops | bytes accessed | tf_op | source)
XLA Modules:
  0.0 188.4 jit_solution(11189232899646032693)
XLA Ops:
  7.2 0.7 all-gather.2.cloned.1.call-update
  8.0 0.7 add_select_fusion.1
  8.7 1.2 reduce-window.6
  9.8 0.2 slice_reduce_fusion
  10.4 5.4 %convolution_convert_fusion = bf16[1024,1664]{1,0:T(8,128)(2,1)} fusion(bf16[512,128]{1,0:T(8,128)(2,1)S(1)} %fusion.46, bf16[512,512]{1,0:T(8,128)(2,1)} %param.7, bf16[512,1024]{1,0:T(8,128)(2,1)} %param.6, s32[512]{0:T(512)S(1)} %multiply_add_fusion), kind=kOutput, calls=%fused_computation.3 | convolution fusion | flops 1752170496 | bytes 5113856 | tf_op jit(solution)/shard_map/dot_general | solution.py:52
  15.8 8.7 %fusion.54 = f32[512,8192]{1,0:T(8,128)} fusion(bf16[512,512]{1,0:T(8,128)(2,1)S(1)} %copy-done.4, bf16[8192,512]{1,0:T(8,128)(2,1)S(1)} %copy-done.2), kind=kOutput, calls=%fused_computation.80 | convolution fusion | flops 4294967296 | bytes 25690112 | tf_op jit(solution)/shard_map/dot_general | solution.py:57
  24.5 50.6 %all_to_all.24 = bf16[16,64,1664]{2,1,0:T(8,128)(2,1)} all-to-all(bf16[16,64,1664]{2,1,0:T(8,128)(2,1)} %bitcast.56), channel_id=1, replica_groups=mesh['dp'=16,'tensor'=8] {'dp'}, dimensions={0} | all-to-all | bytes 6815744 | tf_op jit(solution)/shard_map/all_to_all | solution.py:61
  75.1 1.0 slice.48
  76.2 4.0 %fusion.18 = f32[1024,1024]{0,1:S(1)} fusion(bf16[1024,1024]{0,1:T(8,128)(2,1)S(1)} %bitcast.52, bf16[1024,1664]{1,0:T(8,128)(2,1)} %bitcast.3), kind=kOutput, calls=%fused_computation.22 | convolution fusion | flops 2147483648 | bytes 8388608
  80.2 0.5 multiply_reduce_fusion.1
  80.7 0.7 copy-done.5
  81.4 2.6 %multiply_reduce_fusion = f32[1024,64]{0,1:T(8,128)S(1)} fusion(bf16[16,64,512]{2,1,0:T(8,128)(2,1)S(1)} %copy-done.5, f32[1024,16]{0,1:T(8,128)S(1)} %convert_element_type.37, bf16[1024,1664]{1,0:T(8,128)(2,1)} %bitcast.3), kind=kOutput, calls=%fused_computation.1 | convolution fusion | flops 1075773440 | bytes 2424832 | tf_op jit(solution)/shard_map/sq,arq->sar/dot_general | solution.py:70
  84.0 1.8 collective-permute-start
  85.8 1.2 collective-permute-done
  87.1 1.4 collective-permute-start.1
  88.5 9.6 %collective-permute-done.1 = f32[512,128]{0,1:T(8,128)S(1)} collective-permute-done((f32[512,128]{0,1:T(8,128)S(1)}, f32[512,128]{0,1:T(8,128)S(1)}, u32[]{:S(2)}, u32[]{:S(2)}) %collective-permute-start.1) | collective-permute-done | bytes 262176 | tf_op jit(solution)/shard_map/ppermute | solution.py:19
  98.1 3.0 %collective-permute-start.2 = (f32[512,128]{0,1:T(8,128)S(1)}, f32[512,128]{0,1:T(8,128)S(1)}, u32[]{:S(2)}, u32[]{:S(2)}) collective-permute-start(f32[512,128]{0,1:T(8,128)S(1)} %add.35), channel_id=1, source_target_pairs={{0,4},{1,5},{2,6},{3,7},{4,0},{5,1},{6,2},{7,3},{8,12},{9,13},{10,... | collective-permute-start | bytes 786440 | tf_op jit(solution)/shard_map/ppermute | solution.py:19
  101.2 9.0 %collective-permute-done.2 = f32[512,128]{0,1:T(8,128)S(1)} collective-permute-done((f32[512,128]{0,1:T(8,128)S(1)}, f32[512,128]{0,1:T(8,128)S(1)}, u32[]{:S(2)}, u32[]{:S(2)}) %collective-permute-start.2) | collective-permute-done | bytes 262176 | tf_op jit(solution)/shard_map/ppermute | solution.py:19
  110.2 2.1 %collective-permute-start.3 = (f32[512,128]{0,1:T(8,128)S(1)}, f32[512,128]{0,1:T(8,128)S(1)}, u32[]{:S(2)}, u32[]{:S(2)}) collective-permute-start(f32[512,128]{0,1:T(8,128)S(1)} %add.36), channel_id=1, source_target_pairs={{0,1},{1,0},{2,3},{3,2},{4,5},{5,4},{6,7},{7,6},{8,9},{9,8},{10,11... | collective-permute-start | bytes 786440 | tf_op jit(solution)/shard_map/ppermute | solution.py:21
  112.3 1.2 collective-permute-done.3
  113.6 1.3 fusion.13
  114.9 2.4 %bitcast_convert_fusion = bf16[1024,1024]{0,1:T(8,128)(2,1)S(1)} fusion(bf16[16,1024,64]{1,2,0:T(8,128)(2,1)S(1)} %copy-done, bf16[1024,64]{0,1:T(8,128)(2,1)S(1)} %fusion.45, bf16[1024,16]{0,1:T(8,128)(2,1)S(1)} %copy.26), kind=kOutput, calls=%fused_computation | convolution fusion | flops 2149580800 | bytes 4358144 | tf_op jit(solution)/shard_map/sar,adr->sd/dot_general | solution.py:85
  117.3 0.3 pad_maximum_fusion
  117.6 3.0 %copy.25 = bf16[1024,1536]{1,0:T(8,128)(2,1)} copy(bf16[1024,1536]{0,1:T(8,128)(2,1)S(1)} %pad_maximum_fusion) | data formatting | bytes 6291456 | tf_op jit(solution)/shard_map/optimization_barrier | solution.py:94
  120.6 3.7 %all-to-all-start.1 = ((bf16[16,64,1536]{2,1,0:T(8,128)(2,1)}), bf16[16,64,1536]{2,1,0:T(8,128)(2,1)S(1)}, u32[]{:S(2)}, u32[]{:S(2)}) async-start(bf16[16,64,1536]{2,1,0:T(8,128)(2,1)} %bitcast.10), calls=%async_computation.1 | async-start | bytes 6291456 | tf_op jit(solution)/shard_map/all_to_all | solution.py:95
  124.4 4.0 %fusion.27 = f32[16,64,512]{2,1,0:T(8,128)} fusion(bf16[1024,64]{0,1:T(8,128)(2,1)S(1)} %fusion.42, bf16[1024,16]{0,1:T(8,128)(2,1)S(1)} %copy.26, bf16[1024,1664]{1,0:T(8,128)(2,1)} %bitcast.3), kind=kOutput, calls=%fused_computation.29 | convolution fusion | flops 1075314688 | bytes 3309568 | tf_op jit(solution)/shard_map/sar,sq->arq/dot_general | solution.py:89
  128.4 6.1 %fusion.8 = f32[16,1024,64]{1,2,0:T(8,128)} fusion(bf16[1024,1664]{1,0:T(8,128)(2,1)} %bitcast.3, bf16[1024,64]{0,1:T(8,128)(2,1)S(1)} %fusion.45, bf16[1024,16]{0,1:T(8,128)(2,1)S(1)} %copy.26), kind=kOutput, calls=%fused_computation.13 | convolution fusion | flops 2148532224 | bytes 6455296 | tf_op jit(solution)/shard_map/sd,sar->adr/dot_general | solution.py:88
  134.5 8.0 %fusion.53 = f32[512,512]{1,0:T(8,128)} fusion(bf16[512,8192]{1,0:T(8,128)(2,1)} %all-gather.2.cloned.1.call-done, bf16[8192,512]{1,0:T(8,128)(2,1)S(1)} %bitcast.54), kind=kOutput, calls=%fused_computation.79 | convolution fusion | flops 4294967296 | bytes 17825792 | tf_op jit(solution)/shard_map/dot_general | solution.py:97
  142.5 29.7 %all-to-all-done.1 = bf16[16,64,1536]{2,1,0:T(8,128)(2,1)S(1)} async-done(((bf16[16,64,1536]{2,1,0:T(8,128)(2,1)}), bf16[16,64,1536]{2,1,0:T(8,128)(2,1)S(1)}, u32[]{:S(2)}, u32[]{:S(2)}) %all-to-all-start.1) | async-done | bytes 3145760 | tf_op jit(solution)/shard_map/all_to_all | solution.py:95
  172.2 3.5 %fusion.14 = f32[512,1536]{1,0:T(8,128)} fusion(bf16[1024,1536]{1,0:T(8,128)(2,1)S(1)} %bitcast.57, s32[512]{0:T(512)S(1)} %multiply_add_fusion), kind=kOutput, calls=%fused_computation.20 | convolution fusion | flops 1611137024 | bytes 6293504 | tf_op jit(solution)/shard_map/st,sc->tc/dot_general | solution.py:99
  175.7 2.3 %fusion.30 = bf16[512,512]{1,0:T(8,128)(2,1)} fusion(f32[512,512]{1,0:T(8,128)S(1)} %copy-done.3, f32[512,1536]{1,0:T(8,128)} %fusion.14), kind=kLoop, calls=%fused_computation.31 | loop fusion | flops 524288 | bytes 2621440 | tf_op jit(solution)/shard_map/convert_element_type | solution.py:103
  178.1 3.5 %fusion.11 = bf16[512,1024]{1,0:T(8,128)(2,1)} fusion(f32[512,1024]{1,0:T(8,128)} %reduce-scatter.2.cloned.1.call-done, f32[512,1536]{1,0:T(8,128)} %fusion.14), kind=kLoop, calls=%fused_computation.15 | loop fusion | flops 1048576 | bytes 5242880 | tf_op jit(solution)/shard_map/convert_element_type | solution.py:104
  (36 shorter events, 0.8 us)
Async XLA Ops:
  7.2 69.0 %copy-start = (bf16[16,1024,64]{1,2,0:T(8,128)(2,1)S(1)}, bf16[16,1024,64]{1,2,0:T(8,128)(2,1)}, u32[]{:S(2)}) copy-start(bf16[16,1024,64]{1,2,0:T(8,128)(2,1)} %param.9) | copy-start | bytes 6291460
  7.2 110.4 %all-gather.2.cloned.1.call-start = ((), (), s32[]{:S(2)}) async-start(), calls=%async_computation.3 | async-start | bytes 9437184 | tf_op jit(solution)/shard_map/all_gather | solution.py:39
  7.9 170.2 %reduce-scatter.2.cloned.1.call-start = ((), (), s32[]{:S(2)}) async-start(), calls=%async_computation.4 | async-start | bytes 18874368 | tf_op jit(solution)/shard_map/reduce_scatter | solution.py:60
  10.3 5.5 %copy-start.2 = (bf16[8192,512]{1,0:T(8,128)(2,1)S(1)}, bf16[8192,512]{1,0:T(8,128)(2,1)}, u32[]{:S(2)}) copy-start(bf16[8192,512]{1,0:T(8,128)(2,1)} %param.8) | copy-start | bytes 25165828
  10.3 5.4 %copy-start.4 = (bf16[512,512]{1,0:T(8,128)(2,1)S(1)}, bf16[512,512]{1,0:T(8,128)(2,1)}, u32[]{:S(2)}) copy-start(bf16[512,512]{1,0:T(8,128)(2,1)} %param.7) | copy-start | bytes 1572868
  80.1 1.3 copy-start.5
  84.0 3.0 %collective-permute-start = (f32[512,128]{0,1:T(8,128)S(1)}, f32[512,128]{0,1:T(8,128)S(1)}, u32[]{:S(2)}, u32[]{:S(2)}) collective-permute-start(f32[512,128]{0,1:T(8,128)S(1)} %broadcast_select_fusion.2), channel_id=1, source_target_pairs={{0,1},{1,0},{2,3},{3,2},{4,5},{5,4},{6,7},{7,6},{8,9},{9,8},{10,11... | collective-permute-start | bytes 786440 | tf_op jit(solution)/shard_map/ppermute | solution.py:15
  87.1 11.0 %collective-permute-start.1 = (f32[512,128]{0,1:T(8,128)S(1)}, f32[512,128]{0,1:T(8,128)S(1)}, u32[]{:S(2)}, u32[]{:S(2)}) collective-permute-start(f32[512,128]{0,1:T(8,128)S(1)} %select_add_fusion), channel_id=1, source_target_pairs={{0,2},{1,3},{2,0},{3,1},{4,6},{5,7},{6,4},{7,5},{8,10},{9,11},{10,... | collective-permute-start | bytes 786440 | tf_op jit(solution)/shard_map/ppermute | solution.py:19
  98.1 12.1 %collective-permute-start.2 = (f32[512,128]{0,1:T(8,128)S(1)}, f32[512,128]{0,1:T(8,128)S(1)}, u32[]{:S(2)}, u32[]{:S(2)}) collective-permute-start(f32[512,128]{0,1:T(8,128)S(1)} %add.35), channel_id=1, source_target_pairs={{0,4},{1,5},{2,6},{3,7},{4,0},{5,1},{6,2},{7,3},{8,12},{9,13},{10,... | collective-permute-start | bytes 786440 | tf_op jit(solution)/shard_map/ppermute | solution.py:19
  110.2 3.3 %collective-permute-start.3 = (f32[512,128]{0,1:T(8,128)S(1)}, f32[512,128]{0,1:T(8,128)S(1)}, u32[]{:S(2)}, u32[]{:S(2)}) collective-permute-start(f32[512,128]{0,1:T(8,128)S(1)} %add.36), channel_id=1, source_target_pairs={{0,1},{1,0},{2,3},{3,2},{4,5},{5,4},{6,7},{7,6},{8,9},{9,8},{10,11... | collective-permute-start | bytes 786440 | tf_op jit(solution)/shard_map/ppermute | solution.py:21
  120.6 51.6 %all-to-all-start.1 = ((bf16[16,64,1536]{2,1,0:T(8,128)(2,1)}), bf16[16,64,1536]{2,1,0:T(8,128)(2,1)S(1)}, u32[]{:S(2)}, u32[]{:S(2)}) async-start(bf16[16,64,1536]{2,1,0:T(8,128)(2,1)} %bitcast.10), calls=%async_computation.1 | async-start | bytes 6291456 | tf_op jit(solution)/shard_map/all_to_all | solution.py:95
  124.3 10.2 %slice-start = ((s8[8388608]{0:T(1024)(128)(4,1)}), s8[4194304]{0:T(1024)(128)(4,1)S(1)}, s32[]{:S(2)}) async-start(s8[8388608]{0:T(1024)(128)(4,1)} %bitcast.53), calls=%async_computation.5 | async-start | bytes 8388608
  128.4 6.1 %slice-start.1 = ((s8[8388608]{0:T(1024)(128)(4,1)}), s8[4194304]{0:T(1024)(128)(4,1)S(1)}, s32[]{:S(2)}) async-start(s8[8388608]{0:T(1024)(128)(4,1)} %bitcast.53), calls=%async_computation.6 | async-start | bytes 8388608
  172.2 3.5 %copy-start.3 = (f32[512,512]{1,0:T(8,128)S(1)}, f32[512,512]{1,0:T(8,128)}, u32[]{:S(2)}) copy-start(f32[512,512]{1,0:T(8,128)} %fusion.53) | copy-start | bytes 3145732
  175.7 5.9 %copy-start.1 = (bf16[16,1024,64]{1,2,0:T(8,128)(2,1)S(1)}, bf16[16,1024,64]{1,2,0:T(8,128)(2,1)}, u32[]{:S(2)}) copy-start(bf16[16,1024,64]{1,2,0:T(8,128)(2,1)} %param.9) | copy-start | bytes 6291460
Sparse Core Ops, SparseCore 0:
  9.7 53.2 all-gather.1
  65.5 102.0 reduce-scatter.1

commit v5 on v4

v5 whole, which is shorter than its diff:
```python
import jax
import jax.numpy as jnp
from jax import lax
from jax.sharding import PartitionSpec as P

adapter_factor = 0.5


def tensor_sum(x, keep_first):
    n = lax.axis_size("tensor")
    half = x.shape[0] // 2
    keep = jnp.where(keep_first, x[:half], x[half:])
    give = jnp.where(keep_first, x[half:], x[:half])
    pair = [(t, t ^ 1) for t in range(n)]
    mine = keep + lax.ppermute(give, "tensor", pair)
    step = 2
    while step < n:
        perm = [(t, t ^ step) for t in range(n)]
        mine = mine + lax.ppermute(mine, "tensor", perm)
        step *= 2
    other = lax.ppermute(mine, "tensor", pair)
    first = jnp.where(keep_first, mine, other)
    second = jnp.where(keep_first, other, mine)
    return jnp.concatenate([first, second], axis=0)


def adapter_low_parts(got, adapter_down_weight, adapter_up_weight, feature_portion, query_portion):
    local_adapters = adapter_down_weight.shape[0]
    got_tok = got[:, :feature_portion]
    got_cot = got[:, feature_portion : feature_portion + query_portion]
    got_hot = got[:, feature_portion + query_portion : feature_portion + query_portion + local_adapters]
    hot_f = got_hot.astype(jnp.float32)
    hidden_all = jnp.einsum(
        "sd,adr->sar", got_tok, adapter_down_weight, preferred_element_type=jnp.float32
    )
    grad_all = jnp.einsum(
        "sq,arq->sar", got_cot, adapter_up_weight, preferred_element_type=jnp.float32
    )
    hidden_part = jnp.sum(hidden_all * hot_f[:, :, None], axis=1)
    grad_part = jnp.sum(grad_all * hot_f[:, :, None], axis=1)
    return jnp.concatenate([hidden_part, grad_part], axis=1)


def adapter_results(got, joined, adapter_down_weight, adapter_up_weight, feature_portion, query_portion):
    local_adapters, _, rank_columns = adapter_down_weight.shape
    got_tok = got[:, :feature_portion]
    got_cot = got[:, feature_portion : feature_portion + query_portion]
    got_hot = got[:, feature_portion + query_portion : feature_portion + query_portion + local_adapters]
    lowrank_round = joined[:, :rank_columns].astype(jnp.bfloat16)
    gradient_round = (adapter_factor * joined[:, rank_columns:]).astype(jnp.bfloat16)
    low_spread = got_hot[:, :, None] * lowrank_round[:, None, :]
    grad_spread = got_hot[:, :, None] * gradient_round[:, None, :]
    adapter_output = (
        adapter_factor
        * jnp.einsum("sar,arq->sq", low_spread, adapter_up_weight, preferred_element_type=jnp.float32)
    ).astype(jnp.bfloat16)
    adapter_backward = jnp.einsum(
        "sar,adr->sd", grad_spread, adapter_down_weight, preferred_element_type=jnp.float32
    ).astype(jnp.bfloat16)
    down_terms = jnp.einsum("sd,sar->adr", got_tok, grad_spread, preferred_element_type=jnp.float32)
    up_terms = jnp.einsum("sar,sq->arq", low_spread, got_cot, preferred_element_type=jnp.float32)
    back = jnp.concatenate([adapter_output, adapter_backward], axis=1)
    return back, down_terms, up_terms


def per_device(
    tokens, cotangent, frozen_query_weight, adapter_down_weight, adapter_up_weight, token_adapter
):
    tok_rows, feature_portion = tokens.shape
    query_portion = cotangent.shape[1]
    local_adapters = adapter_down_weight.shape[0]
    dp_size = lax.axis_size("dp")
    capacity = tok_rows // dp_size * 2
    capacity = min(capacity, tok_rows)
    chunks = 2 if capacity % 16 == 0 else 1
    oh_width = 128
    dims = (adapter_down_weight, adapter_up_weight, feature_portion, query_portion)

    tokens_full = lax.all_gather(tokens, "tensor", axis=1, tiled=True)

    owners = token_adapter // local_adapters
    local_ids = token_adapter % local_adapters
    owner_hits = (owners[:, None] == jnp.arange(dp_size, dtype=jnp.int32)[None, :]).astype(jnp.int32)
    earlier = jnp.cumsum(owner_hits, axis=0) - owner_hits
    rank_in = jnp.sum(earlier * owner_hits, axis=1)
    slot_of = owners * capacity + rank_in
    per_chunk = capacity // chunks
    slot_ids = jnp.arange(dp_size * capacity, dtype=jnp.int32).reshape(dp_size, chunks, per_chunk)
    local_hot = (local_ids[:, None] == jnp.arange(oh_width, dtype=jnp.int32)[None, :]).astype(
        jnp.bfloat16
    )
    payload = jnp.concatenate([tokens, cotangent, local_hot], axis=1)
    picks, sends = [], []
    for c in range(chunks):
        ids = slot_ids[:, c, :].reshape(dp_size * per_chunk)
        pick = (ids[:, None] == slot_of[None, :]).astype(jnp.bfloat16)
        picks.append(pick)
        sends.append(jnp.dot(pick, payload, preferred_element_type=jnp.float32).astype(jnp.bfloat16))
    keep_first = lax.axis_index("tensor") % 2 == 0
    sends, cot_late, weight_late, keep_first = lax.optimization_barrier(
        (sends, cotangent, frozen_query_weight, keep_first)
    )
    partial_term = lax.dot_general(
        cot_late, weight_late, (((1,), (1,)), ((), ())), preferred_element_type=jnp.float32
    )
    frozen_backward = lax.psum_scatter(partial_term, "tensor", scatter_dimension=1, tiled=True)

    gots, lows = [], []
    for c in range(chunks):
        send = sends[c]
        if lows:
            send, lows[-1] = lax.optimization_barrier((send, lows[-1]))
        got = lax.all_to_all(send, "dp", split_axis=0, concat_axis=0, tiled=True)
        gots.append(got)
        lows.append(adapter_low_parts(got, *dims))

    backs, down_grad, up_sum = [], None, None
    for c in range(chunks):
        joined = tensor_sum(lows[c], keep_first)
        back, down_terms, up_terms = adapter_results(gots[c], joined, *dims)
        down_grad = down_terms if down_grad is None else down_grad + down_terms
        up_sum = up_terms if up_sum is None else up_sum + up_terms
        if c == chunks - 1:
            back, tokens_full = lax.optimization_barrier((back, tokens_full))
        backs.append(lax.all_to_all(back, "dp", split_axis=0, concat_axis=0, tiled=True))
    up_grad = adapter_factor * up_sum
    frozen_output = lax.optimization_barrier(
        jnp.dot(tokens_full, frozen_query_weight, preferred_element_type=jnp.float32)
    )
    mine = None
    for c in range(chunks):
        part = jnp.einsum("st,sc->tc", picks[c], backs[c], preferred_element_type=jnp.float32)
        mine = part if mine is None else mine + part
    mine_out = mine[:, :query_portion]
    mine_grad = mine[:, query_portion:]

    projected = (frozen_output + mine_out).astype(jnp.bfloat16)
    input_gradient = (frozen_backward + mine_grad).astype(jnp.bfloat16)
    return (projected, input_gradient, down_grad, up_grad)


def solution(mesh):
    in_specs = (
        P("dp", "tensor"),
        P("dp", "tensor"),
        P(None, "tensor"),
        P("dp", "tensor", None),
        P("dp", None, "tensor"),
        P("dp"),
    )
    out_specs = (
        P("dp", "tensor"),
        P("dp", "tensor"),
        P("dp", "tensor", None),
        P("dp", None, "tensor"),
    )
    return jax.shard_map(
        per_device, mesh=mesh, in_specs=in_specs, out_specs=out_specs, check_vma=False
    )
```

time: 189 us -> 211 us (1.12)
  starting transfers between devices: 12.2 us -> 32.2 us
  blocking collectives: 50.6 us -> 31.5 us
  matrix products: 45.9 us -> 59.8 us
  waiting for transfers between devices: 51.4 us -> 54.6 us
  local copies, waits for them, and re-layouts: 5.05 us -> 7.66 us
    all_to_all x1, blocking collectives: 50.6 us -> 31.5 us  [per_device(): got = lax.all_to_all(send, 'dp', split_axis=0, concat_axis=0, tiled=True)]
    all_to_all x1 -> x3, starting transfers between devices: 3.74 us -> 15.9 us  [the longest x2 11.4 us: per_device(): lax.all_to_all(back, 'dp', split_axis=0, concat_axis=0, tiled=True)]
    dot_general x7 -> x13, matrix products: 27.9 us -> 39.4 us  [the longest x1 9.46 us: per_device(): jnp.dot(tokens_full, frozen_query_weight, preferred_element_type=jnp.floa...]
    all_to_all x1 -> x3, waiting for transfers between devices: 29.7 us -> 39.5 us  [the longest x1 23.5 us: per_device(): got = lax.all_to_all(send, 'dp', split_axis=0, concat_axis=0, tiled=True)]
    ppermute x2 -> x4, waiting for transfers between devices: 18.6 us -> 12.4 us  [tensor_sum(): mine = mine + lax.ppermute(mine, 'tensor', perm)]
    unnamed x17 -> x26, local copies, waits for them, and re-layouts: 0.88 us -> 5.88 us
    ppermute x2 -> x4, starting transfers between devices: 4.45 us -> 9.39 us  [tensor_sum(): mine = mine + lax.ppermute(mine, 'tensor', perm)]
    optimization_barrier x1 -> x0, local copies, waits for them, and re-layouts: 2.97 us -> none  [per_device(): back, tokens_late = lax.optimization_barrier((back, tokens_full))]
  transfers between devices with their start and end apart: 7 -> 13, of which waited for: 5 -> 8; matrix products, arithmetic and copies ran while one was open for 30% -> 32% of each run, Pallas kernels for 0% -> 0%
where the time goes in v5:
time: 211 us; the launch traced here: 210 us
  matrix products  59.8 us (28%)
  waiting for transfers between devices  54.6 us (26%)
  starting transfers between devices  32.2 us (15%)
  blocking collectives  31.5 us (15%)
  between operations  14.4 us (7%)
  other arithmetic  9.98 us (5%)
  local copies, waits for them, and re-layouts  7.66 us (4%)
    all_to_all x1, blocking collectives, per_device(): got = lax.all_to_all(send, 'dp', split_axis=0, concat_axis=0, tiled=True)  31.5 us
    all_to_all x1, waiting for transfers between devices, per_device(): got = lax.all_to_all(send, 'dp', split_axis=0, concat_axis=0, tiled=True)  23.5 us
    all_to_all x2, waiting for transfers between devices, per_device(): lax.all_to_all(back, 'dp', split_axis=0, concat_axis=0, tiled=True)  16 us
    ppermute x4, waiting for transfers between devices, tensor_sum(): mine = mine + lax.ppermute(mine, 'tensor', perm)  12.4 us
    all_to_all x2, starting transfers between devices, per_device(): lax.all_to_all(back, 'dp', split_axis=0, concat_axis=0, tiled=True)  11.4 us
    dot_general x1, matrix products, per_device(): jnp.dot(tokens_full, frozen_query_weight, preferred_element_type=jnp.floa...  9.46 us
    ppermute x4, starting transfers between devices, tensor_sum(): mine = mine + lax.ppermute(mine, 'tensor', perm)  9.39 us
    dot_general x1, matrix products, per_device(): lax.dot_general(cot_late, weight_late, (((1,), (1,)), ((), ())), preferre...  9.1 us
  transfers between devices with their start and end apart: 13, of which 8 were waited for; matrix products, arithmetic and copies ran while one was open for 32% of the time, Pallas kernels for 0%

profile of v5, /device:TPU:1, one launch (start us, length us, event | category | flops | bytes accessed | tf_op | source)
XLA Modules:
  0.0 210.1 jit_solution(15551166135306091791)
XLA Ops:
  10.6 3.9 %convolution_convert_fusion.1 = bf16[512,1664]{1,0:T(8,128)(2,1)} fusion(bf16[512,128]{1,0:T(8,128)(2,1)S(1)} %fusion.69, bf16[512,512]{1,0:T(8,128)(2,1)} %param.7, bf16[512,1024]{1,0:T(8,128)(2,1)} %param.6, s32[512]{0:T(512)S(1)} %multiply_add_fusion.1, s32[512]{0:T(512)S(1)} %eq.71), kind=kOutput, calls=%fused_computation.3 | convolution fusion | flops 878641152 | bytes 3411968 | tf_op jit(solution)/shard_map/dot_general | solution.py:98
  14.5 2.4 %convolution_convert_fusion = bf16[512,1664]{1,0:T(8,128)(2,1)} fusion(bf16[512,128]{1,0:T(8,128)(2,1)S(1)} %fusion.69, bf16[512,512]{1,0:T(8,128)(2,1)S(1)} %copy-done.8, bf16[512,1024]{1,0:T(8,128)(2,1)S(1)} %copy-done.7, s32[512]{0:T(512)S(1)} %multiply_add_fusion.1, s32[512]{0:T(512)S(1)} %eq.85), kind=kOutput, calls=%fused_computation.2 | convolution fusion | flops 878641152 | bytes 3411968 | tf_op jit(solution)/shard_map/dot_general | solution.py:98
  16.9 9.1 %fusion.87 = f32[512,8192]{1,0:T(8,128)} fusion(bf16[512,512]{1,0:T(8,128)(2,1)S(1)} %copy-done.8, bf16[8192,512]{1,0:T(8,128)(2,1)S(1)} %copy-done.2), kind=kOutput, calls=%fused_computation.128 | convolution fusion | flops 4294967296 | bytes 25690112 | tf_op jit(solution)/shard_map/dot_general | solution.py:103
  26.0 31.5 %all_to_all.48 = bf16[16,32,1664]{2,1,0:T(8,128)(2,1)S(1)} all-to-all(bf16[16,32,1664]{2,1,0:T(8,128)(2,1)} %bitcast.93), channel_id=1, replica_groups=mesh['dp'=16,'tensor'=8] {'dp'}, dimensions={0} | all-to-all | bytes 3407872 | tf_op jit(solution)/shard_map/all_to_all | solution.py:113
  58.8 2.5 %fusion.43 = f32[512,1024]{0,1:S(1)} fusion(bf16[1024,1024]{0,1:T(8,128)(2,1)S(1)} %bitcast.81, bf16[512,1664]{1,0:T(8,128)(2,1)} %bitcast.88), kind=kOutput, calls=%fused_computation.47 | convolution fusion | flops 1073741824 | bytes 5242880
  62.6 1.8 multiply_reduce_fusion.2
  64.4 2.0 collective-permute-start.4
  68.8 3.4 %collective-permute-done.5 = f32[256,128]{0,1:T(8,128)S(1)} collective-permute-done((f32[256,128]{0,1:T(8,128)S(1)}, f32[256,128]{0,1:T(8,128)S(1)}, u32[]{:S(2)}, u32[]{:S(2)}) %collective-permute-start.5) | collective-permute-done | bytes 131104 | tf_op jit(solution)/shard_map/ppermute | solution.py:19
  72.2 3.0 %collective-permute-start.6 = (f32[256,128]{0,1:T(8,128)S(1)}, f32[256,128]{0,1:T(8,128)S(1)}, u32[]{:S(2)}, u32[]{:S(2)}) collective-permute-start(f32[256,128]{0,1:T(8,128)S(1)} %add.61), channel_id=1, source_target_pairs={{0,4},{1,5},{2,6},{3,7},{4,0},{5,1},{6,2},{7,3},{8,12},{9,13},{10,... | collective-permute-start | bytes 393224 | tf_op jit(solution)/shard_map/ppermute | solution.py:19
  75.2 4.0 %collective-permute-done.6 = f32[256,128]{0,1:T(8,128)S(1)} collective-permute-done((f32[256,128]{0,1:T(8,128)S(1)}, f32[256,128]{0,1:T(8,128)S(1)}, u32[]{:S(2)}, u32[]{:S(2)}) %collective-permute-start.6) | collective-permute-done | bytes 131104 | tf_op jit(solution)/shard_map/ppermute | solution.py:19
  79.2 2.3 %collective-permute-start.7 = (f32[256,128]{0,1:T(8,128)S(1)}, f32[256,128]{0,1:T(8,128)S(1)}, u32[]{:S(2)}, u32[]{:S(2)}) collective-permute-start(f32[256,128]{0,1:T(8,128)S(1)} %add.62), channel_id=1, source_target_pairs={{0,1},{1,0},{2,3},{3,2},{4,5},{5,4},{6,7},{7,6},{8,9},{9,8},{10,11... | collective-permute-start | bytes 393224 | tf_op jit(solution)/shard_map/ppermute | solution.py:21
  81.6 4.4 %all-to-all-start.1 = ((bf16[16,32,1664]{2,1,0:T(8,128)(2,1)}), bf16[16,32,1664]{2,1,0:T(8,128)(2,1)}, u32[]{:S(2)}, u32[]{:S(2)}) async-start(bf16[16,32,1664]{2,1,0:T(8,128)(2,1)} %bitcast.92), calls=%async_computation.1 | async-start | bytes 3407872 | tf_op jit(solution)/shard_map/all_to_all | solution.py:113
  86.0 2.0 fusion.33
  90.9 23.5 %all-to-all-done.1 = bf16[16,32,1664]{2,1,0:T(8,128)(2,1)} async-done(((bf16[16,32,1664]{2,1,0:T(8,128)(2,1)}), bf16[16,32,1664]{2,1,0:T(8,128)(2,1)}, u32[]{:S(2)}, u32[]{:S(2)}) %all-to-all-start.1) | async-done | bytes 1703968 | tf_op jit(solution)/shard_map/all_to_all | solution.py:113
  114.4 4.6 %all-to-all-start.2 = ((bf16[16,32,1536]{2,1,0:T(8,128)(2,1)}), bf16[16,32,1536]{2,1,0:T(8,128)(2,1)}, u32[]{:S(2)}, u32[]{:S(2)}) async-start(bf16[16,32,1536]{2,1,0:T(8,128)(2,1)} %bitcast.83), calls=%async_computation.2 | async-start | bytes 3145728 | tf_op jit(solution)/shard_map/all_to_all | solution.py:125
  120.0 2.5 %fusion.40 = f32[512,1024]{0,1:S(1)} fusion(bf16[1024,1024]{0,1:T(8,128)(2,1)S(1)} %bitcast.82, bf16[512,1664]{1,0:T(8,128)(2,1)} %bitcast.9), kind=kOutput, calls=%fused_computation.44 | convolution fusion | flops 1073741824 | bytes 5242880
  123.8 1.9 multiply_reduce_fusion
  127.8 1.6 collective-permute-start.1
  129.4 3.3 %fusion.1 = f32[16,64,1024]{2,1,0:T(8,128)} fusion(bf16[512,1664]{1,0:T(8,128)(2,1)S(1)} %bitcast.90, bf16[512,64]{0,1:T(8,128)(2,1)S(1)} %fusion.76, bf16[512,16]{0,1:T(8,128)(2,1)S(1)} %copy.41), kind=kOutput, calls=%fused_computation.16 | convolution fusion | flops 1074266112 | bytes 5324800 | tf_op jit(solution)/shard_map/sd,sar->adr/dot_general | solution.py:60
  132.7 2.0 collective-permute-done.1
  134.7 3.4 %collective-permute-start.2 = (f32[256,128]{0,1:T(8,128)S(1)}, f32[256,128]{0,1:T(8,128)S(1)}, u32[]{:S(2)}, u32[]{:S(2)}) collective-permute-start(f32[256,128]{0,1:T(8,128)S(1)} %add.58), channel_id=1, source_target_pairs={{0,4},{1,5},{2,6},{3,7},{4,0},{5,1},{6,2},{7,3},{8,12},{9,13},{10,... | collective-permute-start | bytes 393224 | tf_op jit(solution)/shard_map/ppermute | solution.py:19
  138.1 2.0 fusion.4
  140.1 3.0 %collective-permute-done.2 = f32[256,128]{0,1:T(8,128)S(1)} collective-permute-done((f32[256,128]{0,1:T(8,128)S(1)}, f32[256,128]{0,1:T(8,128)S(1)}, u32[]{:S(2)}, u32[]{:S(2)}) %collective-permute-start.2) | collective-permute-done | bytes 131104 | tf_op jit(solution)/shard_map/ppermute | solution.py:19
  144.7 4.3 %fusion.27 = f32[512,1536]{1,0:T(8,128)} fusion(bf16[512,1536]{1,0:T(8,128)(2,1)} %bitcast.19, s32[512]{0:T(512)S(1)} %multiply_add_fusion.1, s32[512]{0:T(512)S(1)} %eq.71), kind=kOutput, calls=%fused_computation.34 | convolution fusion | flops 805568512 | bytes 4722688 | tf_op jit(solution)/shard_map/st,sc->tc/dot_general | solution.py:132
  153.6 3.2 %add_multiply_fusion = f32[16,64,512]{2,1,0:T(8,128)} fusion(f32[16,64,512]{2,1,0:T(8,128)S(1)} %copy-done.4, bf16[512,64]{0,1:T(8,128)(2,1)S(1)} %fusion.73, bf16[512,16]{0,1:T(8,128)(2,1)S(1)} %copy.42, bf16[512,1664]{1,0:T(8,128)(2,1)} %bitcast.9), kind=kOutput, calls=%fused_computation.8 | convolution fusion | flops 538443776 | bytes 4800512 | tf_op jit(solution)/shard_map/sar,sq->arq/dot_general | solution.py:61
  156.8 4.5 %add_bitcast_fusion = f32[16,1024,64]{1,2,0:T(8,128)} fusion(f32[16,64,1024]{2,1,0:T(8,128)S(1)} %copy-done.3, bf16[512,1664]{1,0:T(8,128)(2,1)} %bitcast.9, bf16[512,64]{0,1:T(8,128)(2,1)S(1)} %fusion.78, bf16[512,16]{0,1:T(8,128)(2,1)S(1)} %copy.42), kind=kOutput, calls=%fused_computation | convolution fusion | flops 1075314688 | bytes 9519104 | tf_op jit(solution)/shard_map/sd,sar->adr/dot_general | solution.py:60
  161.3 6.9 %all-to-all-start.3 = ((bf16[16,32,1536]{2,1,0:T(8,128)(2,1)}), bf16[16,32,1536]{2,1,0:T(8,128)(2,1)}, u32[]{:S(2)}, u32[]{:S(2)}) async-start(bf16[16,32,1536]{2,1,0:T(8,128)(2,1)} %bitcast.84), calls=%async_computation.3 | async-start | bytes 3145728 | tf_op jit(solution)/shard_map/all_to_all | solution.py:125
  168.2 9.5 %fusion.86 = f32[512,512]{1,0:T(8,128)S(1)} fusion(bf16[512,8192]{1,0:T(8,128)(2,1)} %all-gather.2.cloned.1.call-done, bf16[8192,512]{1,0:T(8,128)(2,1)} %param.8), kind=kOutput, calls=%fused_computation.127 | convolution fusion | flops 4294967296 | bytes 17825792 | tf_op jit(solution)/shard_map/dot_general | solution.py:128
  177.7 16.0 %all-to-all-done.3 = bf16[16,32,1536]{2,1,0:T(8,128)(2,1)} async-done(((bf16[16,32,1536]{2,1,0:T(8,128)(2,1)}), bf16[16,32,1536]{2,1,0:T(8,128)(2,1)}, u32[]{:S(2)}, u32[]{:S(2)}) %all-to-all-start.3) | async-done | bytes 1572896 | tf_op jit(solution)/shard_map/all_to_all | solution.py:125
  193.6 3.5 %convolution_add_fusion = f32[512,1536]{1,0:T(8,128)S(1)} fusion(f32[512,1536]{1,0:T(8,128)} %fusion.27, bf16[512,1536]{1,0:T(8,128)(2,1)} %bitcast.21, s32[512]{0:T(512)S(1)} %multiply_add_fusion.1, s32[512]{0:T(512)S(1)} %eq.85), kind=kOutput, calls=%fused_computation.1 | convolution fusion | flops 806354944 | bytes 7868416 | tf_op jit(solution)/shard_map/st,sc->tc/dot_general | solution.py:132
  197.1 1.6 copy-done.1
  199.7 3.5 %fusion = bf16[512,1024]{1,0:T(8,128)(2,1)} fusion(f32[512,1024]{1,0:T(8,128)} %reduce-scatter.2.cloned.1.call-done, f32[512,1536]{1,0:T(8,128)} %copy-done.1), kind=kLoop, calls=%fused_computation.5 | loop fusion | flops 1048576 | bytes 5242880 | tf_op jit(solution)/shard_map/convert_element_type | solution.py:138
  (81 shorter events, 22.4 us)
Async XLA Ops:
  7.2 51.6 %copy-start = (bf16[16,1024,64]{1,2,0:T(8,128)(2,1)S(1)}, bf16[16,1024,64]{1,2,0:T(8,128)(2,1)}, u32[]{:S(2)}) copy-start(bf16[16,1024,64]{1,2,0:T(8,128)(2,1)} %param.9) | copy-start | bytes 6291460
  7.2 154.2 %all-gather.2.cloned.1.call-start = ((), (), s32[]{:S(2)}) async-start(), calls=%async_computation.5 | async-start | bytes 9437184 | tf_op jit(solution)/shard_map/all_gather | solution.py:79
  7.9 191.8 %reduce-scatter.2.cloned.1.call-start = ((), (), s32[]{:S(2)}) async-start(), calls=%async_computation.6 | async-start | bytes 18874368 | tf_op jit(solution)/shard_map/reduce_scatter | solution.py:106
  10.4 4.1 %copy-start.7 = (bf16[512,1024]{1,0:T(8,128)(2,1)S(1)}, bf16[512,1024]{1,0:T(8,128)(2,1)}, u32[]{:S(2)}) copy-start(bf16[512,1024]{1,0:T(8,128)(2,1)} %param.6) | copy-start | bytes 3145732
  10.4 4.1 %copy-start.8 = (bf16[512,512]{1,0:T(8,128)(2,1)S(1)}, bf16[512,512]{1,0:T(8,128)(2,1)}, u32[]{:S(2)}) copy-start(bf16[512,512]{1,0:T(8,128)(2,1)} %param.7) | copy-start | bytes 1572868
  10.6 6.3 %copy-start.2 = (bf16[8192,512]{1,0:T(8,128)(2,1)S(1)}, bf16[8192,512]{1,0:T(8,128)(2,1)}, u32[]{:S(2)}) copy-start(bf16[8192,512]{1,0:T(8,128)(2,1)} %param.8) | copy-start | bytes 25165828
  57.5 1.2 copy-start.5
  61.3 1.2 copy-start.9
  64.4 3.0 %collective-permute-start.4 = (f32[256,128]{0,1:T(8,128)S(1)}, f32[256,128]{0,1:T(8,128)S(1)}, u32[]{:S(2)}, u32[]{:S(2)}) collective-permute-start(f32[256,128]{0,1:T(8,128)S(1)} %slice_select_fusion), channel_id=1, source_target_pairs={{0,1},{1,0},{2,3},{3,2},{4,5},{5,4},{6,7},{7,6},{8,9},{9,8},{10,11... | collective-permute-start | bytes 393224 | tf_op jit(solution)/shard_map/ppermute | solution.py:15
  67.5 4.8 %collective-permute-start.5 = (f32[256,128]{0,1:T(8,128)S(1)}, f32[256,128]{0,1:T(8,128)S(1)}, u32[]{:S(2)}, u32[]{:S(2)}) collective-permute-start(f32[256,128]{0,1:T(8,128)S(1)} %select_add_fusion), channel_id=1, source_target_pairs={{0,2},{1,3},{2,0},{3,1},{4,6},{5,7},{6,4},{7,5},{8,10},{9,11},{10,... | collective-permute-start | bytes 393224 | tf_op jit(solution)/shard_map/ppermute | solution.py:19
  72.2 7.0 %collective-permute-start.6 = (f32[256,128]{0,1:T(8,128)S(1)}, f32[256,128]{0,1:T(8,128)S(1)}, u32[]{:S(2)}, u32[]{:S(2)}) collective-permute-start(f32[256,128]{0,1:T(8,128)S(1)} %add.61), channel_id=1, source_target_pairs={{0,4},{1,5},{2,6},{3,7},{4,0},{5,1},{6,2},{7,3},{8,12},{9,13},{10,... | collective-permute-start | bytes 393224 | tf_op jit(solution)/shard_map/ppermute | solution.py:19
  79.2 6.7 %collective-permute-start.7 = (f32[256,128]{0,1:T(8,128)S(1)}, f32[256,128]{0,1:T(8,128)S(1)}, u32[]{:S(2)}, u32[]{:S(2)}) collective-permute-start(f32[256,128]{0,1:T(8,128)S(1)} %add.62), channel_id=1, source_target_pairs={{0,1},{1,0},{2,3},{3,2},{4,5},{5,4},{6,7},{7,6},{8,9},{9,8},{10,11... | collective-permute-start | bytes 393224 | tf_op jit(solution)/shard_map/ppermute | solution.py:21
  81.6 32.8 %all-to-all-start.1 = ((bf16[16,32,1664]{2,1,0:T(8,128)(2,1)}), bf16[16,32,1664]{2,1,0:T(8,128)(2,1)}, u32[]{:S(2)}, u32[]{:S(2)}) async-start(bf16[16,32,1664]{2,1,0:T(8,128)(2,1)} %bitcast.92), calls=%async_computation.1 | async-start | bytes 3407872 | tf_op jit(solution)/shard_map/all_to_all | solution.py:113
  114.4 30.3 %all-to-all-start.2 = ((bf16[16,32,1536]{2,1,0:T(8,128)(2,1)}), bf16[16,32,1536]{2,1,0:T(8,128)(2,1)}, u32[]{:S(2)}, u32[]{:S(2)}) async-start(bf16[16,32,1536]{2,1,0:T(8,128)(2,1)} %bitcast.83), calls=%async_computation.2 | async-start | bytes 3145728 | tf_op jit(solution)/shard_map/all_to_all | solution.py:125
  122.6 1.3 copy-start.10
  123.8 5.6 %copy-start.6 = (bf16[16,32,1664]{2,1,0:T(8,128)(2,1)S(1)}, bf16[16,32,1664]{2,1,0:T(8,128)(2,1)}, u32[]{:S(2)}) copy-start(bf16[16,32,1664]{2,1,0:T(8,128)(2,1)} %copy-done.5) | copy-start | bytes 5111812
  125.8 1.9 collective-permute-start
  127.8 6.9 %collective-permute-start.1 = (f32[256,128]{0,1:T(8,128)S(1)}, f32[256,128]{0,1:T(8,128)S(1)}, u32[]{:S(2)}, u32[]{:S(2)}) collective-permute-start(f32[256,128]{0,1:T(8,128)S(1)} %select_add_fusion.1), channel_id=1, source_target_pairs={{0,2},{1,3},{2,0},{3,1},{4,6},{5,7},{6,4},{7,5},{8,10},{9,11},{10,... | collective-permute-start | bytes 393224 | tf_op jit(solution)/shard_map/ppermute | solution.py:19
  134.7 8.5 %collective-permute-start.2 = (f32[256,128]{0,1:T(8,128)S(1)}, f32[256,128]{0,1:T(8,128)S(1)}, u32[]{:S(2)}, u32[]{:S(2)}) collective-permute-start(f32[256,128]{0,1:T(8,128)S(1)} %add.58), channel_id=1, source_target_pairs={{0,4},{1,5},{2,6},{3,7},{4,0},{5,1},{6,2},{7,3},{8,12},{9,13},{10,... | collective-permute-start | bytes 393224 | tf_op jit(solution)/shard_map/ppermute | solution.py:19
  143.2 5.9 %collective-permute-start.3 = (f32[256,128]{0,1:T(8,128)S(1)}, f32[256,128]{0,1:T(8,128)S(1)}, u32[]{:S(2)}, u32[]{:S(2)}) collective-permute-start(f32[256,128]{0,1:T(8,128)S(1)} %add.59), channel_id=1, source_target_pairs={{0,1},{1,0},{2,3},{3,2},{4,5},{5,4},{6,7},{7,6},{8,9},{9,8},{10,11... | collective-permute-start | bytes 393224 | tf_op jit(solution)/shard_map/ppermute | solution.py:21
  144.7 4.4 %copy-start.11 = (bf16[16,64,512]{2,1,0:T(8,128)(2,1)S(1)}, bf16[16,64,512]{2,1,0:T(8,128)(2,1)}, u32[]{:S(2)}) copy-start(bf16[16,64,512]{2,1,0:T(8,128)(2,1)} %param.10) | copy-start | bytes 3145732
  151.4 2.2 %copy-start.4 = (f32[16,64,512]{2,1,0:T(8,128)S(1)}, f32[16,64,512]{2,1,0:T(8,128)}, u32[]{:S(2)}) copy-start(f32[16,64,512]{2,1,0:T(8,128)} %fusion.4) | copy-start | bytes 6291460
  153.6 3.2 %copy-start.3 = (f32[16,64,1024]{2,1,0:T(8,128)S(1)}, f32[16,64,1024]{2,1,0:T(8,128)}, u32[]{:S(2)}) copy-start(f32[16,64,1024]{2,1,0:T(8,128)} %fusion.1) | copy-start | bytes 12582916
  161.3 32.3 %all-to-all-start.3 = ((bf16[16,32,1536]{2,1,0:T(8,128)(2,1)}), bf16[16,32,1536]{2,1,0:T(8,128)(2,1)}, u32[]{:S(2)}, u32[]{:S(2)}) async-start(bf16[16,32,1536]{2,1,0:T(8,128)(2,1)} %bitcast.84), calls=%async_computation.3 | async-start | bytes 3145728 | tf_op jit(solution)/shard_map/all_to_all | solution.py:125
  197.1 1.6 copy-start.1
Sparse Core Ops, SparseCore 0:
  9.7 53.2 all-gather.1
  65.5 99.1 reduce-scatter.1

commit v6 on v4

--- a/solution.py
+++ b/solution.py
@@ -15,7 +15,8 @@
     mine = keep + lax.ppermute(give, "tensor", pair)
     step = 2
     while step < n:
-        perm = [(t, t ^ step) for t in range(n)]
+        flip = 2 * step - 2 if step * 2 == n else step
+        perm = [(t, t ^ flip) for t in range(n)]
         mine = mine + lax.ppermute(mine, "tensor", perm)
         step *= 2
     other = lax.ppermute(mine, "tensor", pair)
@@ -96,9 +97,12 @@
     frozen_output = lax.optimization_barrier(
         jnp.dot(tokens_late, frozen_query_weight, preferred_element_type=jnp.float32)
     )
-    mine = jnp.einsum("st,sc->tc", pick, back, preferred_element_type=jnp.float32)
-    mine_out = mine[:, :query_portion]
-    mine_grad = mine[:, query_portion:]
+    mine_out = jnp.einsum(
+        "st,sc->tc", pick, back[:, :query_portion], preferred_element_type=jnp.float32
+    )
+    mine_grad = jnp.einsum(
+        "st,sc->tc", pick, back[:, query_portion:], preferred_element_type=jnp.float32
+    )
 
     projected = (frozen_output + mine_out).astype(jnp.bfloat16)
     input_gradient = (frozen_backward + mine_grad).astype(jnp.bfloat16)

time: 189 us -> 188 us (level)
  other arithmetic: 9.06 us -> 3.21 us
  matrix products: 45.9 us -> 49 us
    convert_element_type x2 -> x0, other arithmetic: 5.85 us -> none  [the longest x1 3.51 us: per_device(): input_gradient = (frozen_backward + mine_grad).astype(jnp.bfloat16)]
    dot_general x1 -> x2, matrix products: 3.49 us -> 7.42 us  [the longest x1 4.49 us: per_device(): jnp.einsum('st,sc->tc', pick, back[:, query_portion:], preferred_element_...]
  transfers between devices with their start and end apart: 7 -> 7, of which waited for: 5 -> 5; matrix products, arithmetic and copies ran while one was open for 30% -> 28% of each run, Pallas kernels for 0% -> 0%
where the time goes in v6:
time: 188 us
  waiting for transfers between devices  53.1 us (28%)
  blocking collectives  50.6 us (27%)
  matrix products  49 us (26%)
  between operations  14.2 us (8%)
  starting transfers between devices  12.6 us (7%)
  local copies, waits for them, and re-layouts  5.07 us (3%)
  other arithmetic  3.21 us (2%)
    all_to_all x1, blocking collectives, per_device(): got = lax.all_to_all(send, 'dp', split_axis=0, concat_axis=0, tiled=True)  50.6 us
    all_to_all x1, waiting for transfers between devices, per_device(): back = lax.all_to_all(back, 'dp', split_axis=0, concat_axis=0, tiled=True)  31.1 us
    ppermute x2, waiting for transfers between devices, tensor_sum(): mine = mine + lax.ppermute(mine, 'tensor', perm)  18.8 us
    dot_general x1, matrix products, per_device(): lax.dot_general(cot_late, weight_late, (((1,), (1,)), ((), ())), preferre...  8.67 us
    dot_general x1, matrix products, per_device(): jnp.dot(tokens_late, frozen_query_weight, preferred_element_type=jnp.floa...  7.13 us
    dot_general x1, matrix products, per_device(): jnp.einsum('sd,sar->adr', got_tok, grad_spread, preferred_element_type=jn...  6.14 us
    dot_general x1, matrix products, per_device(): jnp.dot(pick, payload, preferred_element_type=jnp.float32)  5.43 us
    all_to_all x1, starting transfers between devices, per_device(): back = lax.all_to_all(back, 'dp', split_axis=0, concat_axis=0, tiled=True)  4.56 us
  transfers between devices with their start and end apart: 7, of which 5 were waited for; matrix products, arithmetic and copies ran while one was open for 28% of the time, Pallas kernels for 0%

profile of v6, /device:TPU:1, one launch (start us, length us, event | category | flops | bytes accessed | tf_op | source)
XLA Modules:
  0.0 187.8 jit_solution(10621117777105811948)
XLA Ops:
  7.2 0.7 all-gather.2.cloned.1.call-update
  8.0 0.7 add_select_fusion.1
  8.7 1.2 reduce-window.6
  9.8 0.2 slice_reduce_fusion
  10.2 0.1 fusion.52
  10.4 5.4 %convolution_convert_fusion = bf16[1024,1664]{1,0:T(8,128)(2,1)} fusion(bf16[512,128]{1,0:T(8,128)(2,1)S(1)} %fusion.52, bf16[512,512]{1,0:T(8,128)(2,1)} %param.7, bf16[512,1024]{1,0:T(8,128)(2,1)} %param.6, s32[512]{0:T(512)S(1)} %multiply_add_fusion), kind=kOutput, calls=%fused_computation.3 | convolution fusion | flops 1752170496 | bytes 5113856 | tf_op jit(solution)/shard_map/dot_general | solution.py:53
  15.8 8.7 %fusion.60 = f32[512,8192]{1,0:T(8,128)} fusion(bf16[512,512]{1,0:T(8,128)(2,1)S(1)} %copy-done.3, bf16[8192,512]{1,0:T(8,128)(2,1)S(1)} %copy-done.2), kind=kOutput, calls=%fused_computation.83 | convolution fusion | flops 4294967296 | bytes 25690112 | tf_op jit(solution)/shard_map/dot_general | solution.py:58
  24.5 50.6 %all_to_all.24 = bf16[16,64,1664]{2,1,0:T(8,128)(2,1)} all-to-all(bf16[16,64,1664]{2,1,0:T(8,128)(2,1)} %bitcast.55), channel_id=1, replica_groups=mesh['dp'=16,'tensor'=8] {'dp'}, dimensions={0} | all-to-all | bytes 6815744 | tf_op jit(solution)/shard_map/all_to_all | solution.py:62
  75.1 1.0 slice.48
  76.2 4.0 %fusion.19 = f32[1024,1024]{0,1:S(1)} fusion(bf16[1024,1024]{0,1:T(8,128)(2,1)S(1)} %bitcast.51, bf16[1024,1664]{1,0:T(8,128)(2,1)} %bitcast.3), kind=kOutput, calls=%fused_computation.23 | convolution fusion | flops 2147483648 | bytes 8388608
  80.2 0.5 multiply_reduce_fusion.1
  80.7 0.7 copy-done.4
  81.4 2.6 %multiply_reduce_fusion = f32[1024,64]{0,1:T(8,128)S(1)} fusion(bf16[16,64,512]{2,1,0:T(8,128)(2,1)S(1)} %copy-done.4, f32[1024,16]{0,1:T(8,128)S(1)} %convert_element_type.37, bf16[1024,1664]{1,0:T(8,128)(2,1)} %bitcast.3), kind=kOutput, calls=%fused_computation.1 | convolution fusion | flops 1075773440 | bytes 2424832 | tf_op jit(solution)/shard_map/sq,arq->sar/dot_general | solution.py:71
  84.0 1.8 collective-permute-start
  85.8 1.2 collective-permute-done
  87.1 1.4 collective-permute-start.1
  88.5 9.6 %collective-permute-done.1 = f32[512,128]{0,1:T(8,128)S(1)} collective-permute-done((f32[512,128]{0,1:T(8,128)S(1)}, f32[512,128]{0,1:T(8,128)S(1)}, u32[]{:S(2)}, u32[]{:S(2)}) %collective-permute-start.1) | collective-permute-done | bytes 262176 | tf_op jit(solution)/shard_map/ppermute | solution.py:20
  98.1 2.9 %collective-permute-start.2 = (f32[512,128]{0,1:T(8,128)S(1)}, f32[512,128]{0,1:T(8,128)S(1)}, u32[]{:S(2)}, u32[]{:S(2)}) collective-permute-start(f32[512,128]{0,1:T(8,128)S(1)} %add.35), channel_id=1, source_target_pairs={{0,6},{1,7},{2,4},{3,5},{4,2},{5,3},{6,0},{7,1},{8,14},{9,15},{10,... | collective-permute-start | bytes 786440 | tf_op jit(solution)/shard_map/ppermute | solution.py:20
  101.0 9.2 %collective-permute-done.2 = f32[512,128]{0,1:T(8,128)S(1)} collective-permute-done((f32[512,128]{0,1:T(8,128)S(1)}, f32[512,128]{0,1:T(8,128)S(1)}, u32[]{:S(2)}, u32[]{:S(2)}) %collective-permute-start.2) | collective-permute-done | bytes 262176 | tf_op jit(solution)/shard_map/ppermute | solution.py:20
  110.2 1.9 collective-permute-start.3
  112.1 1.3 collective-permute-done.3
  113.5 1.3 fusion.14
  114.8 2.4 %bitcast_convert_fusion = bf16[1024,1024]{0,1:T(8,128)(2,1)S(1)} fusion(bf16[16,1024,64]{1,2,0:T(8,128)(2,1)S(1)} %copy-done, bf16[1024,64]{0,1:T(8,128)(2,1)S(1)} %fusion.51, bf16[1024,16]{0,1:T(8,128)(2,1)S(1)} %copy.26), kind=kOutput, calls=%fused_computation | convolution fusion | flops 2149580800 | bytes 4358144 | tf_op jit(solution)/shard_map/sar,adr->sd/dot_general | solution.py:86
  117.2 0.3 pad_maximum_fusion
  117.6 3.0 %copy.25 = bf16[1024,1536]{1,0:T(8,128)(2,1)} copy(bf16[1024,1536]{0,1:T(8,128)(2,1)S(1)} %pad_maximum_fusion) | data formatting | bytes 6291456 | tf_op jit(solution)/shard_map/optimization_barrier | solution.py:95
  120.6 4.6 %all-to-all-start.1 = ((bf16[16,64,1536]{2,1,0:T(8,128)(2,1)}), bf16[16,64,1536]{2,1,0:T(8,128)(2,1)}, u32[]{:S(2)}, u32[]{:S(2)}) async-start(bf16[16,64,1536]{2,1,0:T(8,128)(2,1)} %bitcast.10), calls=%async_computation.1 | async-start | bytes 6291456 | tf_op jit(solution)/shard_map/all_to_all | solution.py:96
  125.1 4.0 %fusion.28 = f32[16,64,512]{2,1,0:T(8,128)} fusion(bf16[1024,64]{0,1:T(8,128)(2,1)S(1)} %fusion.48, bf16[1024,16]{0,1:T(8,128)(2,1)S(1)} %copy.26, bf16[1024,1664]{1,0:T(8,128)(2,1)} %bitcast.3), kind=kOutput, calls=%fused_computation.30 | convolution fusion | flops 1075314688 | bytes 3309568 | tf_op jit(solution)/shard_map/sar,sq->arq/dot_general | solution.py:90
  129.1 6.1 %fusion.8 = f32[16,1024,64]{1,2,0:T(8,128)} fusion(bf16[1024,1664]{1,0:T(8,128)(2,1)} %bitcast.3, bf16[1024,64]{0,1:T(8,128)(2,1)S(1)} %fusion.51, bf16[1024,16]{0,1:T(8,128)(2,1)S(1)} %copy.26), kind=kOutput, calls=%fused_computation.13 | convolution fusion | flops 2148532224 | bytes 6455296 | tf_op jit(solution)/shard_map/sd,sar->adr/dot_general | solution.py:89
  135.3 7.1 %fusion.59 = f32[512,512]{1,0:T(8,128)S(1)} fusion(bf16[512,8192]{1,0:T(8,128)(2,1)} %all-gather.2.cloned.1.call-done, bf16[8192,512]{1,0:T(8,128)(2,1)S(1)} %bitcast.53), kind=kOutput, calls=%fused_computation.82 | convolution fusion | flops 4294967296 | bytes 17825792 | tf_op jit(solution)/shard_map/dot_general | solution.py:98
  142.4 31.1 %all-to-all-done.1 = bf16[16,64,1536]{2,1,0:T(8,128)(2,1)} async-done(((bf16[16,64,1536]{2,1,0:T(8,128)(2,1)}), bf16[16,64,1536]{2,1,0:T(8,128)(2,1)}, u32[]{:S(2)}, u32[]{:S(2)}) %all-to-all-start.1) | async-done | bytes 3145760 | tf_op jit(solution)/shard_map/all_to_all | solution.py:96
  173.5 2.9 %fusion.34 = bf16[512,512]{1,0:T(8,128)(2,1)} fusion(f32[512,512]{1,0:T(8,128)S(1)} %fusion.59, bf16[1024,1536]{1,0:T(8,128)(2,1)} %bitcast.11, s32[512]{0:T(512)S(1)} %multiply_add_fusion), kind=kOutput, calls=%fused_computation.32 | convolution fusion | flops 537919488 | bytes 2623488 | tf_op jit(solution)/shard_map/st,sc->tc/dot_general | solution.py:100
  176.5 4.5 %add_convert_fusion = bf16[512,1024]{1,0:T(8,128)(2,1)} fusion(f32[512,1024]{1,0:T(8,128)} %reduce-scatter.2.cloned.1.call-done, bf16[1024,1536]{1,0:T(8,128)(2,1)} %bitcast.11, s32[512]{0:T(512)S(1)} %multiply_add_fusion), kind=kOutput, calls=%fused_computation.19 | convolution fusion | flops 1075314688 | bytes 5244928 | tf_op jit(solution)/shard_map/st,sc->tc/dot_general | solution.py:103
  (33 shorter events, 0.7 us)
Async XLA Ops:
  7.2 69.0 %copy-start = (bf16[16,1024,64]{1,2,0:T(8,128)(2,1)S(1)}, bf16[16,1024,64]{1,2,0:T(8,128)(2,1)}, u32[]{:S(2)}) copy-start(bf16[16,1024,64]{1,2,0:T(8,128)(2,1)} %param.9) | copy-start | bytes 6291460
  7.2 110.4 %all-gather.2.cloned.1.call-start = ((), (), s32[]{:S(2)}) async-start(), calls=%async_computation.3 | async-start | bytes 9437184 | tf_op jit(solution)/shard_map/all_gather | solution.py:40
  7.9 168.6 %reduce-scatter.2.cloned.1.call-start = ((), (), s32[]{:S(2)}) async-start(), calls=%async_computation.4 | async-start | bytes 18874368 | tf_op jit(solution)/shard_map/reduce_scatter | solution.py:61
  10.3 5.5 %copy-start.2 = (bf16[8192,512]{1,0:T(8,128)(2,1)S(1)}, bf16[8192,512]{1,0:T(8,128)(2,1)}, u32[]{:S(2)}) copy-start(bf16[8192,512]{1,0:T(8,128)(2,1)} %param.8) | copy-start | bytes 25165828
  10.4 5.4 %copy-start.3 = (bf16[512,512]{1,0:T(8,128)(2,1)S(1)}, bf16[512,512]{1,0:T(8,128)(2,1)}, u32[]{:S(2)}) copy-start(bf16[512,512]{1,0:T(8,128)(2,1)} %param.7) | copy-start | bytes 1572868
  80.1 1.3 copy-start.4
  84.0 3.0 %collective-permute-start = (f32[512,128]{0,1:T(8,128)S(1)}, f32[512,128]{0,1:T(8,128)S(1)}, u32[]{:S(2)}, u32[]{:S(2)}) collective-permute-start(f32[512,128]{0,1:T(8,128)S(1)} %broadcast_select_fusion.2), channel_id=1, source_target_pairs={{0,1},{1,0},{2,3},{3,2},{4,5},{5,4},{6,7},{7,6},{8,9},{9,8},{10,11... | collective-permute-start | bytes 786440 | tf_op jit(solution)/shard_map/ppermute | solution.py:15
  87.1 11.0 %collective-permute-start.1 = (f32[512,128]{0,1:T(8,128)S(1)}, f32[512,128]{0,1:T(8,128)S(1)}, u32[]{:S(2)}, u32[]{:S(2)}) collective-permute-start(f32[512,128]{0,1:T(8,128)S(1)} %select_add_fusion), channel_id=1, source_target_pairs={{0,2},{1,3},{2,0},{3,1},{4,6},{5,7},{6,4},{7,5},{8,10},{9,11},{10,... | collective-permute-start | bytes 786440 | tf_op jit(solution)/shard_map/ppermute | solution.py:20
  98.1 12.1 %collective-permute-start.2 = (f32[512,128]{0,1:T(8,128)S(1)}, f32[512,128]{0,1:T(8,128)S(1)}, u32[]{:S(2)}, u32[]{:S(2)}) collective-permute-start(f32[512,128]{0,1:T(8,128)S(1)} %add.35), channel_id=1, source_target_pairs={{0,6},{1,7},{2,4},{3,5},{4,2},{5,3},{6,0},{7,1},{8,14},{9,15},{10,... | collective-permute-start | bytes 786440 | tf_op jit(solution)/shard_map/ppermute | solution.py:20
  110.2 3.2 %collective-permute-start.3 = (f32[512,128]{0,1:T(8,128)S(1)}, f32[512,128]{0,1:T(8,128)S(1)}, u32[]{:S(2)}, u32[]{:S(2)}) collective-permute-start(f32[512,128]{0,1:T(8,128)S(1)} %add.36), channel_id=1, source_target_pairs={{0,1},{1,0},{2,3},{3,2},{4,5},{5,4},{6,7},{7,6},{8,9},{9,8},{10,11... | collective-permute-start | bytes 786440 | tf_op jit(solution)/shard_map/ppermute | solution.py:22
  120.6 53.0 %all-to-all-start.1 = ((bf16[16,64,1536]{2,1,0:T(8,128)(2,1)}), bf16[16,64,1536]{2,1,0:T(8,128)(2,1)}, u32[]{:S(2)}, u32[]{:S(2)}) async-start(bf16[16,64,1536]{2,1,0:T(8,128)(2,1)} %bitcast.10), calls=%async_computation.1 | async-start | bytes 6291456 | tf_op jit(solution)/shard_map/all_to_all | solution.py:96
  125.1 10.1 %slice-start = ((s8[8388608]{0:T(1024)(128)(4,1)}), s8[4194304]{0:T(1024)(128)(4,1)S(1)}, s32[]{:S(2)}) async-start(s8[8388608]{0:T(1024)(128)(4,1)} %bitcast.52), calls=%async_computation.5 | async-start | bytes 8388608
  129.1 6.1 %slice-start.1 = ((s8[8388608]{0:T(1024)(128)(4,1)}), s8[4194304]{0:T(1024)(128)(4,1)S(1)}, s32[]{:S(2)}) async-start(s8[8388608]{0:T(1024)(128)(4,1)} %bitcast.52), calls=%async_computation.6 | async-start | bytes 8388608
  173.5 7.4 %copy-start.1 = (bf16[16,1024,64]{1,2,0:T(8,128)(2,1)S(1)}, bf16[16,1024,64]{1,2,0:T(8,128)(2,1)}, u32[]{:S(2)}) copy-start(bf16[16,1024,64]{1,2,0:T(8,128)(2,1)} %param.9) | copy-start | bytes 6291460
Sparse Core Ops, SparseCore 0:
  9.7 53.2 all-gather.1
  65.5 96.5 reduce-scatter.1

commit v7 on v6

--- a/solution.py
+++ b/solution.py
@@ -1,6 +1,7 @@
 import jax
 import jax.numpy as jnp
 from jax import lax
+from jax.experimental.layout import Layout, with_layout_constraint
 from jax.sharding import PartitionSpec as P
 
 adapter_factor = 0.5
@@ -91,6 +92,8 @@
         "sar,sq->arq", low_spread, got_cot, preferred_element_type=jnp.float32
     )
 
+    adapter_output = with_layout_constraint(adapter_output, Layout(major_to_minor=(0, 1)))
+    adapter_backward = with_layout_constraint(adapter_backward, Layout(major_to_minor=(0, 1)))
     back = jnp.concatenate([adapter_output, adapter_backward], axis=1)
     back, tokens_late = lax.optimization_barrier((back, tokens_full))
     back = lax.all_to_all(back, "dp", split_axis=0, concat_axis=0, tiled=True)

time: 188 us -> 187 us (level)
  matrix products: 49 us -> 46.3 us
    optimization_barrier x1 -> x0, local copies, waits for them, and re-layouts: 3 us -> none  [per_device(): back, tokens_late = lax.optimization_barrier((back, tokens_full))]
    dot_general x1, matrix products: 7.13 us -> 4.48 us  [per_device(): jnp.dot(tokens_late, frozen_query_weight, preferred_element_type=jnp.floa...]
    unnamed x15 -> x19, local copies, waits for them, and re-layouts: 0.88 us -> 3.11 us
  transfers between devices with their start and end apart: 7 -> 7, of which waited for: 5 -> 5; matrix products, arithmetic and copies ran while one was open for 28% -> 25% of each run, Pallas kernels for 0% -> 0%
where the time goes in v7:
time: 187 us
  waiting for transfers between devices  54.9 us (29%)
  blocking collectives  50.5 us (27%)
  matrix products  46.3 us (25%)
  between operations  14.2 us (8%)
  starting transfers between devices  12.5 us (7%)
  other arithmetic  4.78 us (3%)
  local copies, waits for them, and re-layouts  3.35 us (2%)
    all_to_all x1, blocking collectives, per_device(): got = lax.all_to_all(send, 'dp', split_axis=0, concat_axis=0, tiled=True)  50.5 us
    all_to_all x1, waiting for transfers between devices, per_device(): back = lax.all_to_all(back, 'dp', split_axis=0, concat_axis=0, tiled=True)  32.9 us
    ppermute x2, waiting for transfers between devices, tensor_sum(): mine = mine + lax.ppermute(mine, 'tensor', perm)  18.8 us
    dot_general x1, matrix products, per_device(): lax.dot_general(cot_late, weight_late, (((1,), (1,)), ((), ())), preferre...  8.65 us
    dot_general x1, matrix products, per_device(): jnp.einsum('sd,sar->adr', got_tok, grad_spread, preferred_element_type=jn...  6.15 us
    dot_general x1, matrix products, per_device(): jnp.dot(pick, payload, preferred_element_type=jnp.float32)  5.42 us
    dot_general x1, matrix products, per_device(): jnp.einsum('st,sc->tc', pick, back[:, query_portion:], preferred_element_...  4.49 us
    all_to_all x1, starting transfers between devices, per_device(): back = lax.all_to_all(back, 'dp', split_axis=0, concat_axis=0, tiled=True)  4.49 us
  transfers between devices with their start and end apart: 7, of which 5 were waited for; matrix products, arithmetic and copies ran while one was open for 25% of the time, Pallas kernels for 0%

profile of v7, /device:TPU:1, one launch (start us, length us, event | category | flops | bytes accessed | tf_op | source)
XLA Modules:
  0.0 186.5 jit_solution(17292204111207090636)
XLA Ops:
  7.2 0.7 all-gather.2.cloned.1.call-update
  8.0 0.7 add_select_fusion.1
  8.7 1.2 reduce-window.6
  9.8 0.2 slice_reduce_fusion
  10.2 0.1 fusion.52
  10.4 5.4 %convolution_convert_fusion = bf16[1024,1664]{1,0:T(8,128)(2,1)} fusion(bf16[512,128]{1,0:T(8,128)(2,1)S(1)} %fusion.52, bf16[512,512]{1,0:T(8,128)(2,1)} %param.7, bf16[512,1024]{1,0:T(8,128)(2,1)} %param.6, s32[512]{0:T(512)S(1)} %multiply_add_fusion), kind=kOutput, calls=%fused_computation.3 | convolution fusion | flops 1752170496 | bytes 5113856 | tf_op jit(solution)/shard_map/dot_general | solution.py:54
  15.8 8.7 %fusion.60 = f32[512,8192]{1,0:T(8,128)} fusion(bf16[512,512]{1,0:T(8,128)(2,1)S(1)} %copy-done.4, bf16[8192,512]{1,0:T(8,128)(2,1)S(1)} %copy-done.2), kind=kOutput, calls=%fused_computation.83 | convolution fusion | flops 4294967296 | bytes 25690112 | tf_op jit(solution)/shard_map/dot_general | solution.py:59
  24.5 50.5 %all_to_all.24 = bf16[16,64,1664]{2,1,0:T(8,128)(2,1)S(1)} all-to-all(bf16[16,64,1664]{2,1,0:T(8,128)(2,1)} %bitcast.60), channel_id=1, replica_groups=mesh['dp'=16,'tensor'=8] {'dp'}, dimensions={0} | all-to-all | bytes 6815744 | tf_op jit(solution)/shard_map/all_to_all | solution.py:63
  74.9 1.8 copy-done.3
  76.9 4.0 %fusion.19 = f32[1024,1024]{0,1:S(1)} fusion(bf16[1024,1024]{0,1:T(8,128)(2,1)S(1)} %bitcast.51, bf16[1024,1664]{1,0:T(8,128)(2,1)} %bitcast.56), kind=kOutput, calls=%fused_computation.23 | convolution fusion | flops 2147483648 | bytes 8388608
  80.9 0.5 multiply_reduce_fusion.1
  81.4 0.7 copy-done.6
  82.1 2.5 %multiply_reduce_fusion = f32[1024,64]{0,1:T(8,128)S(1)} fusion(bf16[16,64,512]{2,1,0:T(8,128)(2,1)S(1)} %copy-done.6, f32[1024,16]{0,1:T(8,128)S(1)} %convert_element_type.37, bf16[1024,1664]{1,0:T(8,128)(2,1)} %bitcast.57), kind=kOutput, calls=%fused_computation.1 | convolution fusion | flops 1075773440 | bytes 2424832 | tf_op jit(solution)/shard_map/sq,arq->sar/dot_general | solution.py:72
  84.7 1.9 %collective-permute-start = (f32[512,128]{0,1:T(8,128)S(1)}, f32[512,128]{0,1:T(8,128)S(1)}, u32[]{:S(2)}, u32[]{:S(2)}) collective-permute-start(f32[512,128]{0,1:T(8,128)S(1)} %broadcast_select_fusion.2), channel_id=1, source_target_pairs={{0,1},{1,0},{2,3},{3,2},{4,5},{5,4},{6,7},{7,6},{8,9},{9,8},{10,11... | collective-permute-start | bytes 786440 | tf_op jit(solution)/shard_map/ppermute | solution.py:16
  86.6 1.3 collective-permute-done
  88.0 1.4 collective-permute-start.1
  89.4 9.6 %collective-permute-done.1 = f32[512,128]{0,1:T(8,128)S(1)} collective-permute-done((f32[512,128]{0,1:T(8,128)S(1)}, f32[512,128]{0,1:T(8,128)S(1)}, u32[]{:S(2)}, u32[]{:S(2)}) %collective-permute-start.1) | collective-permute-done | bytes 262176 | tf_op jit(solution)/shard_map/ppermute | solution.py:21
  99.0 2.6 %collective-permute-start.2 = (f32[512,128]{0,1:T(8,128)S(1)}, f32[512,128]{0,1:T(8,128)S(1)}, u32[]{:S(2)}, u32[]{:S(2)}) collective-permute-start(f32[512,128]{0,1:T(8,128)S(1)} %add.35), channel_id=1, source_target_pairs={{0,6},{1,7},{2,4},{3,5},{4,2},{5,3},{6,0},{7,1},{8,14},{9,15},{10,... | collective-permute-start | bytes 786440 | tf_op jit(solution)/shard_map/ppermute | solution.py:21
  101.7 9.2 %collective-permute-done.2 = f32[512,128]{0,1:T(8,128)S(1)} collective-permute-done((f32[512,128]{0,1:T(8,128)S(1)}, f32[512,128]{0,1:T(8,128)S(1)}, u32[]{:S(2)}, u32[]{:S(2)}) %collective-permute-start.2) | collective-permute-done | bytes 262176 | tf_op jit(solution)/shard_map/ppermute | solution.py:21
  110.9 2.0 %collective-permute-start.3 = (f32[512,128]{0,1:T(8,128)S(1)}, f32[512,128]{0,1:T(8,128)S(1)}, u32[]{:S(2)}, u32[]{:S(2)}) collective-permute-start(f32[512,128]{0,1:T(8,128)S(1)} %add.36), channel_id=1, source_target_pairs={{0,1},{1,0},{2,3},{3,2},{4,5},{5,4},{6,7},{7,6},{8,9},{9,8},{10,11... | collective-permute-start | bytes 786440 | tf_op jit(solution)/shard_map/ppermute | solution.py:23
  112.9 1.2 collective-permute-done.3
  114.2 1.3 fusion.14
  115.5 2.4 %bitcast_convert_fusion = bf16[1024,1024]{1,0:T(8,128)(2,1)S(1)} fusion(bf16[16,1024,64]{1,2,0:T(8,128)(2,1)S(1)} %copy-done, bf16[1024,64]{0,1:T(8,128)(2,1)S(1)} %fusion.51, bf16[1024,16]{0,1:T(8,128)(2,1)S(1)} %copy.23), kind=kOutput, calls=%fused_computation | convolution fusion | flops 2149580800 | bytes 4358144 | tf_op jit(solution)/shard_map/sar,adr->sd/dot_general | solution.py:87
  117.9 1.9 %pad_maximum_fusion = bf16[1024,1536]{1,0:T(8,128)(2,1)} fusion(bf16[1024,1024]{1,0:T(8,128)(2,1)S(1)} %bitcast_convert_fusion, bf16[1024,512]{1,0:T(8,128)(2,1)S(1)} %fusion.14), kind=kLoop, calls=%fused_computation.4 | loop fusion | flops 6291456 | bytes 6291456 | tf_op jit(solution)/shard_map/concatenate | solution.py:97
  119.8 4.5 %all-to-all-start.1 = ((bf16[16,64,1536]{2,1,0:T(8,128)(2,1)}), bf16[16,64,1536]{2,1,0:T(8,128)(2,1)}, u32[]{:S(2)}, u32[]{:S(2)}) async-start(bf16[16,64,1536]{2,1,0:T(8,128)(2,1)} %bitcast.10), calls=%async_computation.1 | async-start | bytes 6291456 | tf_op jit(solution)/shard_map/all_to_all | solution.py:99
  124.3 4.0 %fusion.28 = f32[16,64,512]{2,1,0:T(8,128)} fusion(bf16[1024,64]{0,1:T(8,128)(2,1)S(1)} %fusion.48, bf16[1024,16]{0,1:T(8,128)(2,1)S(1)} %copy.23, bf16[1024,1664]{1,0:T(8,128)(2,1)} %bitcast.58), kind=kOutput, calls=%fused_computation.30 | convolution fusion | flops 1075314688 | bytes 3309568 | tf_op jit(solution)/shard_map/sar,sq->arq/dot_general | solution.py:91
  128.3 6.1 %fusion.8 = f32[16,1024,64]{1,2,0:T(8,128)} fusion(bf16[1024,1664]{1,0:T(8,128)(2,1)} %bitcast.59, bf16[1024,64]{0,1:T(8,128)(2,1)S(1)} %fusion.51, bf16[1024,16]{0,1:T(8,128)(2,1)S(1)} %copy.23), kind=kOutput, calls=%fused_computation.13 | convolution fusion | flops 2148532224 | bytes 6455296 | tf_op jit(solution)/shard_map/sd,sar->adr/dot_general | solution.py:90
  134.4 0.5 copy-done.5
  134.9 4.5 %fusion.59 = f32[512,512]{1,0:T(8,128)S(1)} fusion(bf16[512,8192]{1,0:T(8,128)(2,1)S(1)} %copy-done.5, bf16[8192,512]{1,0:T(8,128)(2,1)S(1)} %bitcast.53), kind=kOutput, calls=%fused_computation.82 | convolution fusion | flops 4294967296 | bytes 17825792 | tf_op jit(solution)/shard_map/dot_general | solution.py:101
  139.4 32.9 %all-to-all-done.1 = bf16[16,64,1536]{2,1,0:T(8,128)(2,1)} async-done(((bf16[16,64,1536]{2,1,0:T(8,128)(2,1)}), bf16[16,64,1536]{2,1,0:T(8,128)(2,1)}, u32[]{:S(2)}, u32[]{:S(2)}) %all-to-all-start.1) | async-done | bytes 3145760 | tf_op jit(solution)/shard_map/all_to_all | solution.py:99
  172.3 2.9 %fusion.34 = bf16[512,512]{1,0:T(8,128)(2,1)} fusion(f32[512,512]{1,0:T(8,128)S(1)} %fusion.59, bf16[1024,1536]{1,0:T(8,128)(2,1)} %bitcast.11, s32[512]{0:T(512)S(1)} %multiply_add_fusion), kind=kOutput, calls=%fused_computation.32 | convolution fusion | flops 537919488 | bytes 2623488 | tf_op jit(solution)/shard_map/st,sc->tc/dot_general | solution.py:103
  175.2 4.5 %add_convert_fusion = bf16[512,1024]{1,0:T(8,128)(2,1)} fusion(f32[512,1024]{1,0:T(8,128)} %reduce-scatter.2.cloned.1.call-done, bf16[1024,1536]{1,0:T(8,128)(2,1)} %bitcast.11, s32[512]{0:T(512)S(1)} %multiply_add_fusion), kind=kOutput, calls=%fused_computation.19 | convolution fusion | flops 1075314688 | bytes 5244928 | tf_op jit(solution)/shard_map/st,sc->tc/dot_general | solution.py:106
  (36 shorter events, 0.7 us)
Async XLA Ops:
  7.2 69.7 %copy-start = (bf16[16,1024,64]{1,2,0:T(8,128)(2,1)S(1)}, bf16[16,1024,64]{1,2,0:T(8,128)(2,1)}, u32[]{:S(2)}) copy-start(bf16[16,1024,64]{1,2,0:T(8,128)(2,1)} %param.9) | copy-start | bytes 6291460
  7.2 112.6 %all-gather.2.cloned.1.call-start = ((), (), s32[]{:S(2)}) async-start(), calls=%async_computation.3 | async-start | bytes 9437184 | tf_op jit(solution)/shard_map/all_gather | solution.py:41
  7.9 167.3 %reduce-scatter.2.cloned.1.call-start = ((), (), s32[]{:S(2)}) async-start(), calls=%async_computation.4 | async-start | bytes 18874368 | tf_op jit(solution)/shard_map/reduce_scatter | solution.py:62
  10.3 5.5 %copy-start.2 = (bf16[8192,512]{1,0:T(8,128)(2,1)S(1)}, bf16[8192,512]{1,0:T(8,128)(2,1)}, u32[]{:S(2)}) copy-start(bf16[8192,512]{1,0:T(8,128)(2,1)} %param.8) | copy-start | bytes 25165828
  10.4 5.4 %copy-start.4 = (bf16[512,512]{1,0:T(8,128)(2,1)S(1)}, bf16[512,512]{1,0:T(8,128)(2,1)}, u32[]{:S(2)}) copy-start(bf16[512,512]{1,0:T(8,128)(2,1)} %param.7) | copy-start | bytes 1572868
  74.9 1.8 copy-start.3
  80.9 1.2 copy-start.6
  84.7 3.2 %collective-permute-start = (f32[512,128]{0,1:T(8,128)S(1)}, f32[512,128]{0,1:T(8,128)S(1)}, u32[]{:S(2)}, u32[]{:S(2)}) collective-permute-start(f32[512,128]{0,1:T(8,128)S(1)} %broadcast_select_fusion.2), channel_id=1, source_target_pairs={{0,1},{1,0},{2,3},{3,2},{4,5},{5,4},{6,7},{7,6},{8,9},{9,8},{10,11... | collective-permute-start | bytes 786440 | tf_op jit(solution)/shard_map/ppermute | solution.py:16
  88.0 11.0 %collective-permute-start.1 = (f32[512,128]{0,1:T(8,128)S(1)}, f32[512,128]{0,1:T(8,128)S(1)}, u32[]{:S(2)}, u32[]{:S(2)}) collective-permute-start(f32[512,128]{0,1:T(8,128)S(1)} %select_add_fusion), channel_id=1, source_target_pairs={{0,2},{1,3},{2,0},{3,1},{4,6},{5,7},{6,4},{7,5},{8,10},{9,11},{10,... | collective-permute-start | bytes 786440 | tf_op jit(solution)/shard_map/ppermute | solution.py:21
  99.0 11.9 %collective-permute-start.2 = (f32[512,128]{0,1:T(8,128)S(1)}, f32[512,128]{0,1:T(8,128)S(1)}, u32[]{:S(2)}, u32[]{:S(2)}) collective-permute-start(f32[512,128]{0,1:T(8,128)S(1)} %add.35), channel_id=1, source_target_pairs={{0,6},{1,7},{2,4},{3,5},{4,2},{5,3},{6,0},{7,1},{8,14},{9,15},{10,... | collective-permute-start | bytes 786440 | tf_op jit(solution)/shard_map/ppermute | solution.py:21
  110.9 3.2 %collective-permute-start.3 = (f32[512,128]{0,1:T(8,128)S(1)}, f32[512,128]{0,1:T(8,128)S(1)}, u32[]{:S(2)}, u32[]{:S(2)}) collective-permute-start(f32[512,128]{0,1:T(8,128)S(1)} %add.36), channel_id=1, source_target_pairs={{0,1},{1,0},{2,3},{3,2},{4,5},{5,4},{6,7},{7,6},{8,9},{9,8},{10,11... | collective-permute-start | bytes 786440 | tf_op jit(solution)/shard_map/ppermute | solution.py:23
  119.8 52.5 %all-to-all-start.1 = ((bf16[16,64,1536]{2,1,0:T(8,128)(2,1)}), bf16[16,64,1536]{2,1,0:T(8,128)(2,1)}, u32[]{:S(2)}, u32[]{:S(2)}) async-start(bf16[16,64,1536]{2,1,0:T(8,128)(2,1)} %bitcast.10), calls=%async_computation.1 | async-start | bytes 6291456 | tf_op jit(solution)/shard_map/all_to_all | solution.py:99
  124.3 10.2 %slice-start = ((s8[8388608]{0:T(1024)(128)(4,1)}), s8[4194304]{0:T(1024)(128)(4,1)S(1)}, s32[]{:S(2)}) async-start(s8[8388608]{0:T(1024)(128)(4,1)} %bitcast.52), calls=%async_computation.5 | async-start | bytes 8388608
  128.3 6.2 %slice-start.1 = ((s8[8388608]{0:T(1024)(128)(4,1)}), s8[4194304]{0:T(1024)(128)(4,1)S(1)}, s32[]{:S(2)}) async-start(s8[8388608]{0:T(1024)(128)(4,1)} %bitcast.52), calls=%async_computation.6 | async-start | bytes 8388608
  128.3 6.6 %copy-start.5 = (bf16[512,8192]{1,0:T(8,128)(2,1)S(1)}, bf16[512,8192]{1,0:T(8,128)(2,1)}, u32[]{:S(2)}) copy-start(bf16[512,8192]{1,0:T(8,128)(2,1)} %all-gather.2.cloned.1.call-done) | copy-start | bytes 25165828
  172.3 7.4 %copy-start.1 = (bf16[16,1024,64]{1,2,0:T(8,128)(2,1)S(1)}, bf16[16,1024,64]{1,2,0:T(8,128)(2,1)}, u32[]{:S(2)}) copy-start(bf16[16,1024,64]{1,2,0:T(8,128)(2,1)} %param.9) | copy-start | bytes 6291460
Sparse Core Ops, SparseCore 0:
  9.7 53.2 all-gather.1
  65.5 96.5 reduce-scatter.1

commit v8 on v7

--- a/solution.py
+++ b/solution.py
@@ -100,12 +100,11 @@
     frozen_output = lax.optimization_barrier(
         jnp.dot(tokens_late, frozen_query_weight, preferred_element_type=jnp.float32)
     )
-    mine_out = jnp.einsum(
-        "st,sc->tc", pick, back[:, :query_portion], preferred_element_type=jnp.float32
+    pick_rows = (slot_of[:, None] == jnp.arange(slot_count, dtype=jnp.int32)[None, :]).astype(
+        jnp.bfloat16
     )
-    mine_grad = jnp.einsum(
-        "st,sc->tc", pick, back[:, query_portion:], preferred_element_type=jnp.float32
-    )
+    mine_out = jnp.dot(pick_rows, back[:, :query_portion], preferred_element_type=jnp.float32)
+    mine_grad = jnp.dot(pick_rows, back[:, query_portion:], preferred_element_type=jnp.float32)
 
     projected = (frozen_output + mine_out).astype(jnp.bfloat16)
     input_gradient = (frozen_backward + mine_grad).astype(jnp.bfloat16)

time: 187 us -> 187 us (level)
  no operation moved by 1% of the time
where the time goes in v8:
time: 187 us
  waiting for transfers between devices  54.9 us (29%)
  blocking collectives  50.5 us (27%)
  matrix products  46.3 us (25%)
  between operations  14.2 us (8%)
  starting transfers between devices  12.5 us (7%)
  other arithmetic  4.78 us (3%)
  local copies, waits for them, and re-layouts  3.35 us (2%)
    all_to_all x1, blocking collectives, per_device(): got = lax.all_to_all(send, 'dp', split_axis=0, concat_axis=0, tiled=True)  50.5 us
    all_to_all x1, waiting for transfers between devices, per_device(): back = lax.all_to_all(back, 'dp', split_axis=0, concat_axis=0, tiled=True)  32.9 us
    ppermute x2, waiting for transfers between devices, tensor_sum(): mine = mine + lax.ppermute(mine, 'tensor', perm)  18.8 us
    dot_general x1, matrix products, per_device(): lax.dot_general(cot_late, weight_late, (((1,), (1,)), ((), ())), preferre...  8.65 us
    dot_general x1, matrix products, per_device(): jnp.einsum('sd,sar->adr', got_tok, grad_spread, preferred_element_type=jn...  6.15 us
    dot_general x1, matrix products, per_device(): jnp.dot(pick, payload, preferred_element_type=jnp.float32)  5.42 us
    dot_general x1, matrix products, per_device(): jnp.dot(pick_rows, back[:, query_portion:], preferred_element_type=jnp.fl...  4.49 us
    all_to_all x1, starting transfers between devices, per_device(): back = lax.all_to_all(back, 'dp', split_axis=0, concat_axis=0, tiled=True)  4.49 us
  transfers between devices with their start and end apart: 7, of which 5 were waited for; matrix products, arithmetic and copies ran while one was open for 25% of the time, Pallas kernels for 0%

profile of v8, /device:TPU:1, one launch (start us, length us, event | category | flops | bytes accessed | tf_op | source)
XLA Modules:
  0.0 186.5 jit_solution(12525949183427099682)
XLA Ops:
  7.2 0.7 all-gather.2.cloned.1.call-update
  8.0 0.7 add_select_fusion.1
  8.7 1.2 reduce-window.6
  9.8 0.2 slice_reduce_fusion
  10.2 0.1 fusion.52
  10.4 5.4 %convolution_convert_fusion = bf16[1024,1664]{1,0:T(8,128)(2,1)} fusion(bf16[512,128]{1,0:T(8,128)(2,1)S(1)} %fusion.52, bf16[512,512]{1,0:T(8,128)(2,1)} %param.7, bf16[512,1024]{1,0:T(8,128)(2,1)} %param.6, s32[512]{0:T(512)S(1)} %multiply_add_fusion), kind=kOutput, calls=%fused_computation.3 | convolution fusion | flops 1752170496 | bytes 5113856 | tf_op jit(solution)/shard_map/dot_general | solution.py:54
  15.8 8.7 %fusion.60 = f32[512,8192]{1,0:T(8,128)} fusion(bf16[512,512]{1,0:T(8,128)(2,1)S(1)} %copy-done.4, bf16[8192,512]{1,0:T(8,128)(2,1)S(1)} %copy-done.2), kind=kOutput, calls=%fused_computation.84 | convolution fusion | flops 4294967296 | bytes 25690112 | tf_op jit(solution)/shard_map/dot_general | solution.py:59
  24.5 50.5 %all_to_all.24 = bf16[16,64,1664]{2,1,0:T(8,128)(2,1)S(1)} all-to-all(bf16[16,64,1664]{2,1,0:T(8,128)(2,1)} %bitcast.60), channel_id=1, replica_groups=mesh['dp'=16,'tensor'=8] {'dp'}, dimensions={0} | all-to-all | bytes 6815744 | tf_op jit(solution)/shard_map/all_to_all | solution.py:63
  74.9 1.8 copy-done.3
  76.9 4.0 %fusion.19 = f32[1024,1024]{0,1:S(1)} fusion(bf16[1024,1024]{0,1:T(8,128)(2,1)S(1)} %bitcast.51, bf16[1024,1664]{1,0:T(8,128)(2,1)} %bitcast.56), kind=kOutput, calls=%fused_computation.24 | convolution fusion | flops 2147483648 | bytes 8388608
  80.9 0.5 multiply_reduce_fusion.1
  81.4 0.7 copy-done.6
  82.1 2.5 %multiply_reduce_fusion = f32[1024,64]{0,1:T(8,128)S(1)} fusion(bf16[16,64,512]{2,1,0:T(8,128)(2,1)S(1)} %copy-done.6, f32[1024,16]{0,1:T(8,128)S(1)} %convert_element_type.38, bf16[1024,1664]{1,0:T(8,128)(2,1)} %bitcast.57), kind=kOutput, calls=%fused_computation.1 | convolution fusion | flops 1075773440 | bytes 2424832 | tf_op jit(solution)/shard_map/sq,arq->sar/dot_general | solution.py:72
  84.7 1.9 %collective-permute-start = (f32[512,128]{0,1:T(8,128)S(1)}, f32[512,128]{0,1:T(8,128)S(1)}, u32[]{:S(2)}, u32[]{:S(2)}) collective-permute-start(f32[512,128]{0,1:T(8,128)S(1)} %broadcast_select_fusion.2), channel_id=1, source_target_pairs={{0,1},{1,0},{2,3},{3,2},{4,5},{5,4},{6,7},{7,6},{8,9},{9,8},{10,11... | collective-permute-start | bytes 786440 | tf_op jit(solution)/shard_map/ppermute | solution.py:16
  86.6 1.3 collective-permute-done
  88.0 1.4 collective-permute-start.1
  89.4 9.6 %collective-permute-done.1 = f32[512,128]{0,1:T(8,128)S(1)} collective-permute-done((f32[512,128]{0,1:T(8,128)S(1)}, f32[512,128]{0,1:T(8,128)S(1)}, u32[]{:S(2)}, u32[]{:S(2)}) %collective-permute-start.1) | collective-permute-done | bytes 262176 | tf_op jit(solution)/shard_map/ppermute | solution.py:21
  99.0 2.6 %collective-permute-start.2 = (f32[512,128]{0,1:T(8,128)S(1)}, f32[512,128]{0,1:T(8,128)S(1)}, u32[]{:S(2)}, u32[]{:S(2)}) collective-permute-start(f32[512,128]{0,1:T(8,128)S(1)} %add.35), channel_id=1, source_target_pairs={{0,6},{1,7},{2,4},{3,5},{4,2},{5,3},{6,0},{7,1},{8,14},{9,15},{10,... | collective-permute-start | bytes 786440 | tf_op jit(solution)/shard_map/ppermute | solution.py:21
  101.7 9.2 %collective-permute-done.2 = f32[512,128]{0,1:T(8,128)S(1)} collective-permute-done((f32[512,128]{0,1:T(8,128)S(1)}, f32[512,128]{0,1:T(8,128)S(1)}, u32[]{:S(2)}, u32[]{:S(2)}) %collective-permute-start.2) | collective-permute-done | bytes 262176 | tf_op jit(solution)/shard_map/ppermute | solution.py:21
  110.9 2.0 %collective-permute-start.3 = (f32[512,128]{0,1:T(8,128)S(1)}, f32[512,128]{0,1:T(8,128)S(1)}, u32[]{:S(2)}, u32[]{:S(2)}) collective-permute-start(f32[512,128]{0,1:T(8,128)S(1)} %add.36), channel_id=1, source_target_pairs={{0,1},{1,0},{2,3},{3,2},{4,5},{5,4},{6,7},{7,6},{8,9},{9,8},{10,11... | collective-permute-start | bytes 786440 | tf_op jit(solution)/shard_map/ppermute | solution.py:23
  112.9 1.2 collective-permute-done.3
  114.2 1.3 fusion.14
  115.5 2.4 %bitcast_convert_fusion = bf16[1024,1024]{1,0:T(8,128)(2,1)S(1)} fusion(bf16[16,1024,64]{1,2,0:T(8,128)(2,1)S(1)} %copy-done, bf16[1024,64]{0,1:T(8,128)(2,1)S(1)} %fusion.51, bf16[1024,16]{0,1:T(8,128)(2,1)S(1)} %copy.23), kind=kOutput, calls=%fused_computation | convolution fusion | flops 2149580800 | bytes 4358144 | tf_op jit(solution)/shard_map/sar,adr->sd/dot_general | solution.py:87
  117.9 1.9 %pad_maximum_fusion = bf16[1024,1536]{1,0:T(8,128)(2,1)} fusion(bf16[1024,1024]{1,0:T(8,128)(2,1)S(1)} %bitcast_convert_fusion, bf16[1024,512]{1,0:T(8,128)(2,1)S(1)} %fusion.14), kind=kLoop, calls=%fused_computation.4 | loop fusion | flops 6291456 | bytes 6291456 | tf_op jit(solution)/shard_map/concatenate | solution.py:97
  119.8 4.5 %all-to-all-start.1 = ((bf16[16,64,1536]{2,1,0:T(8,128)(2,1)}), bf16[16,64,1536]{2,1,0:T(8,128)(2,1)}, u32[]{:S(2)}, u32[]{:S(2)}) async-start(bf16[16,64,1536]{2,1,0:T(8,128)(2,1)} %bitcast.10), calls=%async_computation.1 | async-start | bytes 6291456 | tf_op jit(solution)/shard_map/all_to_all | solution.py:99
  124.3 4.0 %fusion.28 = f32[16,64,512]{2,1,0:T(8,128)} fusion(bf16[1024,64]{0,1:T(8,128)(2,1)S(1)} %fusion.48, bf16[1024,16]{0,1:T(8,128)(2,1)S(1)} %copy.23, bf16[1024,1664]{1,0:T(8,128)(2,1)} %bitcast.58), kind=kOutput, calls=%fused_computation.31 | convolution fusion | flops 1075314688 | bytes 3309568 | tf_op jit(solution)/shard_map/sar,sq->arq/dot_general | solution.py:91
  128.3 6.1 %fusion.8 = f32[16,1024,64]{1,2,0:T(8,128)} fusion(bf16[1024,1664]{1,0:T(8,128)(2,1)} %bitcast.59, bf16[1024,64]{0,1:T(8,128)(2,1)S(1)} %fusion.51, bf16[1024,16]{0,1:T(8,128)(2,1)S(1)} %copy.23), kind=kOutput, calls=%fused_computation.13 | convolution fusion | flops 2148532224 | bytes 6455296 | tf_op jit(solution)/shard_map/sd,sar->adr/dot_general | solution.py:90
  134.4 0.5 copy-done.5
  134.9 4.5 %fusion.59 = f32[512,512]{1,0:T(8,128)S(1)} fusion(bf16[512,8192]{1,0:T(8,128)(2,1)S(1)} %copy-done.5, bf16[8192,512]{1,0:T(8,128)(2,1)S(1)} %bitcast.53), kind=kOutput, calls=%fused_computation.83 | convolution fusion | flops 4294967296 | bytes 17825792 | tf_op jit(solution)/shard_map/dot_general | solution.py:101
  139.4 32.9 %all-to-all-done.1 = bf16[16,64,1536]{2,1,0:T(8,128)(2,1)} async-done(((bf16[16,64,1536]{2,1,0:T(8,128)(2,1)}), bf16[16,64,1536]{2,1,0:T(8,128)(2,1)}, u32[]{:S(2)}, u32[]{:S(2)}) %all-to-all-start.1) | async-done | bytes 3145760 | tf_op jit(solution)/shard_map/all_to_all | solution.py:99
  172.3 2.9 %fusion.34 = bf16[512,512]{1,0:T(8,128)(2,1)} fusion(f32[512,512]{1,0:T(8,128)S(1)} %fusion.59, bf16[1024,1536]{1,0:T(8,128)(2,1)} %bitcast.11, s32[512]{0:T(512)S(1)} %multiply_add_fusion), kind=kOutput, calls=%fused_computation.33 | convolution fusion | flops 537919488 | bytes 2623488 | tf_op jit(solution)/shard_map/dot_general | solution.py:106
  175.2 4.5 %add_convert_fusion = bf16[512,1024]{1,0:T(8,128)(2,1)} fusion(f32[512,1024]{1,0:T(8,128)} %reduce-scatter.2.cloned.1.call-done, bf16[1024,1536]{1,0:T(8,128)(2,1)} %bitcast.11, s32[512]{0:T(512)S(1)} %multiply_add_fusion), kind=kOutput, calls=%fused_computation.19 | convolution fusion | flops 1075314688 | bytes 5244928 | tf_op jit(solution)/shard_map/dot_general | solution.py:107
  (36 shorter events, 0.7 us)
Async XLA Ops:
  7.2 69.7 %copy-start = (bf16[16,1024,64]{1,2,0:T(8,128)(2,1)S(1)}, bf16[16,1024,64]{1,2,0:T(8,128)(2,1)}, u32[]{:S(2)}) copy-start(bf16[16,1024,64]{1,2,0:T(8,128)(2,1)} %param.9) | copy-start | bytes 6291460
  7.2 112.6 %all-gather.2.cloned.1.call-start = ((), (), s32[]{:S(2)}) async-start(), calls=%async_computation.3 | async-start | bytes 9437184 | tf_op jit(solution)/shard_map/all_gather | solution.py:41
  7.9 167.3 %reduce-scatter.2.cloned.1.call-start = ((), (), s32[]{:S(2)}) async-start(), calls=%async_computation.4 | async-start | bytes 18874368 | tf_op jit(solution)/shard_map/reduce_scatter | solution.py:62
  10.3 5.5 %copy-start.2 = (bf16[8192,512]{1,0:T(8,128)(2,1)S(1)}, bf16[8192,512]{1,0:T(8,128)(2,1)}, u32[]{:S(2)}) copy-start(bf16[8192,512]{1,0:T(8,128)(2,1)} %param.8) | copy-start | bytes 25165828
  10.4 5.4 %copy-start.4 = (bf16[512,512]{1,0:T(8,128)(2,1)S(1)}, bf16[512,512]{1,0:T(8,128)(2,1)}, u32[]{:S(2)}) copy-start(bf16[512,512]{1,0:T(8,128)(2,1)} %param.7) | copy-start | bytes 1572868
  74.9 1.8 copy-start.3
  80.9 1.2 copy-start.6
  84.7 3.2 %collective-permute-start = (f32[512,128]{0,1:T(8,128)S(1)}, f32[512,128]{0,1:T(8,128)S(1)}, u32[]{:S(2)}, u32[]{:S(2)}) collective-permute-start(f32[512,128]{0,1:T(8,128)S(1)} %broadcast_select_fusion.2), channel_id=1, source_target_pairs={{0,1},{1,0},{2,3},{3,2},{4,5},{5,4},{6,7},{7,6},{8,9},{9,8},{10,11... | collective-permute-start | bytes 786440 | tf_op jit(solution)/shard_map/ppermute | solution.py:16
  88.0 11.0 %collective-permute-start.1 = (f32[512,128]{0,1:T(8,128)S(1)}, f32[512,128]{0,1:T(8,128)S(1)}, u32[]{:S(2)}, u32[]{:S(2)}) collective-permute-start(f32[512,128]{0,1:T(8,128)S(1)} %select_add_fusion), channel_id=1, source_target_pairs={{0,2},{1,3},{2,0},{3,1},{4,6},{5,7},{6,4},{7,5},{8,10},{9,11},{10,... | collective-permute-start | bytes 786440 | tf_op jit(solution)/shard_map/ppermute | solution.py:21
  99.0 11.9 %collective-permute-start.2 = (f32[512,128]{0,1:T(8,128)S(1)}, f32[512,128]{0,1:T(8,128)S(1)}, u32[]{:S(2)}, u32[]{:S(2)}) collective-permute-start(f32[512,128]{0,1:T(8,128)S(1)} %add.35), channel_id=1, source_target_pairs={{0,6},{1,7},{2,4},{3,5},{4,2},{5,3},{6,0},{7,1},{8,14},{9,15},{10,... | collective-permute-start | bytes 786440 | tf_op jit(solution)/shard_map/ppermute | solution.py:21
  110.9 3.2 %collective-permute-start.3 = (f32[512,128]{0,1:T(8,128)S(1)}, f32[512,128]{0,1:T(8,128)S(1)}, u32[]{:S(2)}, u32[]{:S(2)}) collective-permute-start(f32[512,128]{0,1:T(8,128)S(1)} %add.36), channel_id=1, source_target_pairs={{0,1},{1,0},{2,3},{3,2},{4,5},{5,4},{6,7},{7,6},{8,9},{9,8},{10,11... | collective-permute-start | bytes 786440 | tf_op jit(solution)/shard_map/ppermute | solution.py:23
  119.8 52.5 %all-to-all-start.1 = ((bf16[16,64,1536]{2,1,0:T(8,128)(2,1)}), bf16[16,64,1536]{2,1,0:T(8,128)(2,1)}, u32[]{:S(2)}, u32[]{:S(2)}) async-start(bf16[16,64,1536]{2,1,0:T(8,128)(2,1)} %bitcast.10), calls=%async_computation.1 | async-start | bytes 6291456 | tf_op jit(solution)/shard_map/all_to_all | solution.py:99
  124.3 10.2 %slice-start = ((s8[8388608]{0:T(1024)(128)(4,1)}), s8[4194304]{0:T(1024)(128)(4,1)S(1)}, s32[]{:S(2)}) async-start(s8[8388608]{0:T(1024)(128)(4,1)} %bitcast.52), calls=%async_computation.5 | async-start | bytes 8388608
  128.3 6.2 %slice-start.1 = ((s8[8388608]{0:T(1024)(128)(4,1)}), s8[4194304]{0:T(1024)(128)(4,1)S(1)}, s32[]{:S(2)}) async-start(s8[8388608]{0:T(1024)(128)(4,1)} %bitcast.52), calls=%async_computation.6 | async-start | bytes 8388608
  128.3 6.6 %copy-start.5 = (bf16[512,8192]{1,0:T(8,128)(2,1)S(1)}, bf16[512,8192]{1,0:T(8,128)(2,1)}, u32[]{:S(2)}) copy-start(bf16[512,8192]{1,0:T(8,128)(2,1)} %all-gather.2.cloned.1.call-done) | copy-start | bytes 25165828
  172.3 7.4 %copy-start.1 = (bf16[16,1024,64]{1,2,0:T(8,128)(2,1)S(1)}, bf16[16,1024,64]{1,2,0:T(8,128)(2,1)}, u32[]{:S(2)}) copy-start(bf16[16,1024,64]{1,2,0:T(8,128)(2,1)} %param.9) | copy-start | bytes 6291460
Sparse Core Ops, SparseCore 0:
  9.7 53.2 all-gather.1
  65.5 96.5 reduce-scatter.1

commit v9 on v7

--- a/solution.py
+++ b/solution.py
@@ -50,8 +50,16 @@
     local_hot = (local_ids[:, None] == jnp.arange(oh_width, dtype=jnp.int32)[None, :]).astype(
         jnp.bfloat16
     )
-    payload = jnp.concatenate([tokens, cotangent, local_hot], axis=1)
-    send = jnp.dot(pick, payload, preferred_element_type=jnp.float32).astype(jnp.bfloat16)
+    send = jnp.concatenate(
+        [
+            with_layout_constraint(
+                jnp.dot(pick, part, preferred_element_type=jnp.float32).astype(jnp.bfloat16),
+                Layout(major_to_minor=(0, 1)),
+            )
+            for part in (tokens, cotangent, local_hot)
+        ],
+        axis=1,
+    )
     keep_first = lax.axis_index("tensor") % 2 == 0
     send, cot_late, weight_late, keep_first = lax.optimization_barrier(
         (send, cotangent, frozen_query_weight, keep_first)

time: 187 us -> 187 us (level)
    concatenate x0 -> x1, other arithmetic: none -> 1.9 us  [per_device(): jnp.concatenate([with_layout_constraint(jnp.dot(pick, part, preferred_ele...]
    dot_general x1 -> x3, matrix products: 5.42 us -> 3.73 us  [per_device(): jnp.dot(pick, part, preferred_element_type=jnp.float32).astype(jnp.bfloat16)]
where the time goes in v9:
time: 187 us
  waiting for transfers between devices  54.8 us (29%)
  blocking collectives  50.2 us (27%)
  matrix products  44.9 us (24%)
  between operations  14.3 us (8%)
  starting transfers between devices  12.7 us (7%)
  other arithmetic  6.63 us (4%)
  local copies, waits for them, and re-layouts  3.4 us (2%)
    all_to_all x1, blocking collectives, per_device(): got = lax.all_to_all(send, 'dp', split_axis=0, concat_axis=0, tiled=True)  50.2 us
    all_to_all x1, waiting for transfers between devices, per_device(): back = lax.all_to_all(back, 'dp', split_axis=0, concat_axis=0, tiled=True)  32.9 us
    ppermute x2, waiting for transfers between devices, tensor_sum(): mine = mine + lax.ppermute(mine, 'tensor', perm)  18.8 us
    dot_general x1, matrix products, per_device(): lax.dot_general(cot_late, weight_late, (((1,), (1,)), ((), ())), preferre...  8.91 us
    dot_general x1, matrix products, per_device(): jnp.einsum('sd,sar->adr', got_tok, grad_spread, preferred_element_type=jn...  6.14 us
    dot_general x1, matrix products, per_device(): jnp.einsum('st,sc->tc', pick, back[:, query_portion:], preferred_element_...  4.49 us
    all_to_all x1, starting transfers between devices, per_device(): back = lax.all_to_all(back, 'dp', split_axis=0, concat_axis=0, tiled=True)  4.49 us
    dot_general x1, matrix products, per_device(): jnp.dot(tokens_late, frozen_query_weight, preferred_element_type=jnp.floa...  4.48 us
  transfers between devices with their start and end apart: 7, of which 5 were waited for; matrix products, arithmetic and copies ran while one was open for 25% of the time, Pallas kernels for 0%

profile of v9, /device:TPU:1, one launch (start us, length us, event | category | flops | bytes accessed | tf_op | source)
XLA Modules:
  0.0 186.8 jit_solution(11636710440365959551)
XLA Ops:
  7.2 0.7 all-gather.2.cloned.1.call-update
  8.0 0.8 add_select_fusion
  8.8 1.2 reduce-window.6
  10.3 0.6 fusion.35
  10.9 1.9 %fusion.30 = bf16[1024,512]{1,0:T(8,128)(2,1)S(1)} fusion(bf16[512,512]{1,0:T(8,128)(2,1)} %param.7, s32[512]{0:T(512)S(1)} %multiply_add_fusion), kind=kOutput, calls=%fused_computation.30 | convolution fusion | flops 537919488 | bytes 1574912 | tf_op jit(solution)/shard_map/dot_general | solution.py:56
  12.8 1.3 fusion.19
  14.1 1.9 %pad_maximum_fusion = bf16[1024,1664]{1,0:T(8,128)(2,1)} fusion(bf16[1024,128]{1,0:T(8,128)(2,1)S(1)} %fusion.35, bf16[1024,512]{1,0:T(8,128)(2,1)S(1)} %fusion.30, bf16[1024,1024]{1,0:T(8,128)(2,1)S(1)} %fusion.19), kind=kLoop, calls=%fused_computation.3 | loop fusion | flops 10223616 | bytes 6815744 | tf_op jit(solution)/shard_map/concatenate | solution.py:53
  16.0 8.9 %fusion.62 = f32[512,8192]{1,0:T(8,128)} fusion(bf16[512,512]{1,0:T(8,128)(2,1)S(1)} %copy-done.4, bf16[8192,512]{1,0:T(8,128)(2,1)S(1)} %bitcast.57), kind=kOutput, calls=%fused_computation.85 | convolution fusion | flops 4294967296 | bytes 25690112 | tf_op jit(solution)/shard_map/dot_general | solution.py:67
  24.9 50.2 %all_to_all.24 = bf16[16,64,1664]{2,1,0:T(8,128)(2,1)S(1)} all-to-all(bf16[16,64,1664]{2,1,0:T(8,128)(2,1)} %bitcast.54), channel_id=1, replica_groups=mesh['dp'=16,'tensor'=8] {'dp'}, dimensions={0} | all-to-all | bytes 6815744 | tf_op jit(solution)/shard_map/all_to_all | solution.py:71
  75.2 1.8 copy-done.2
  77.1 4.0 %fusion.23 = f32[1024,1024]{0,1:S(1)} fusion(bf16[1024,1024]{0,1:T(8,128)(2,1)S(1)} %bitcast.53, bf16[1024,1664]{1,0:T(8,128)(2,1)} %bitcast.62), kind=kOutput, calls=%fused_computation.27 | convolution fusion | flops 2147483648 | bytes 8388608
  81.1 0.5 multiply_reduce_fusion.1
  81.6 0.7 copy-done.6
  82.3 2.5 %multiply_reduce_fusion = f32[1024,64]{0,1:T(8,128)S(1)} fusion(bf16[16,64,512]{2,1,0:T(8,128)(2,1)S(1)} %copy-done.6, f32[1024,16]{0,1:T(8,128)S(1)} %convert_element_type.42, bf16[1024,1664]{1,0:T(8,128)(2,1)} %bitcast.63), kind=kOutput, calls=%fused_computation.1 | convolution fusion | flops 1075773440 | bytes 2424832 | tf_op jit(solution)/shard_map/sq,arq->sar/dot_general | solution.py:80
  84.9 1.9 %collective-permute-start = (f32[512,128]{0,1:T(8,128)S(1)}, f32[512,128]{0,1:T(8,128)S(1)}, u32[]{:S(2)}, u32[]{:S(2)}) collective-permute-start(f32[512,128]{0,1:T(8,128)S(1)} %broadcast_select_fusion.2), channel_id=1, source_target_pairs={{0,1},{1,0},{2,3},{3,2},{4,5},{5,4},{6,7},{7,6},{8,9},{9,8},{10,11... | collective-permute-start | bytes 786440 | tf_op jit(solution)/shard_map/ppermute | solution.py:16
  86.8 1.2 collective-permute-done
  88.1 1.5 collective-permute-start.1
  89.6 9.5 %collective-permute-done.1 = f32[512,128]{0,1:T(8,128)S(1)} collective-permute-done((f32[512,128]{0,1:T(8,128)S(1)}, f32[512,128]{0,1:T(8,128)S(1)}, u32[]{:S(2)}, u32[]{:S(2)}) %collective-permute-start.1) | collective-permute-done | bytes 262176 | tf_op jit(solution)/shard_map/ppermute | solution.py:21
  99.2 3.0 %collective-permute-start.2 = (f32[512,128]{0,1:T(8,128)S(1)}, f32[512,128]{0,1:T(8,128)S(1)}, u32[]{:S(2)}, u32[]{:S(2)}) collective-permute-start(f32[512,128]{0,1:T(8,128)S(1)} %add.35), channel_id=1, source_target_pairs={{0,6},{1,7},{2,4},{3,5},{4,2},{5,3},{6,0},{7,1},{8,14},{9,15},{10,... | collective-permute-start | bytes 786440 | tf_op jit(solution)/shard_map/ppermute | solution.py:21
  102.1 9.2 %collective-permute-done.2 = f32[512,128]{0,1:T(8,128)S(1)} collective-permute-done((f32[512,128]{0,1:T(8,128)S(1)}, f32[512,128]{0,1:T(8,128)S(1)}, u32[]{:S(2)}, u32[]{:S(2)}) %collective-permute-start.2) | collective-permute-done | bytes 262176 | tf_op jit(solution)/shard_map/ppermute | solution.py:21
  111.4 1.8 collective-permute-start.3
  113.2 1.2 collective-permute-done.3
  114.4 1.3 fusion.14
  115.7 2.4 %bitcast_convert_fusion = bf16[1024,1024]{1,0:T(8,128)(2,1)S(1)} fusion(bf16[16,1024,64]{1,2,0:T(8,128)(2,1)S(1)} %copy-done, bf16[1024,64]{0,1:T(8,128)(2,1)S(1)} %fusion.54, bf16[1024,16]{0,1:T(8,128)(2,1)S(1)} %copy.23), kind=kOutput, calls=%fused_computation | convolution fusion | flops 2149580800 | bytes 4358144 | tf_op jit(solution)/shard_map/sar,adr->sd/dot_general | solution.py:95
  118.1 1.9 %pad_maximum_fusion.1 = bf16[1024,1536]{1,0:T(8,128)(2,1)} fusion(bf16[1024,1024]{1,0:T(8,128)(2,1)S(1)} %bitcast_convert_fusion, bf16[1024,512]{1,0:T(8,128)(2,1)S(1)} %fusion.14), kind=kLoop, calls=%fused_computation.4 | loop fusion | flops 6291456 | bytes 6291456 | tf_op jit(solution)/shard_map/concatenate | solution.py:105
  120.0 4.5 %all-to-all-start.1 = ((bf16[16,64,1536]{2,1,0:T(8,128)(2,1)}), bf16[16,64,1536]{2,1,0:T(8,128)(2,1)}, u32[]{:S(2)}, u32[]{:S(2)}) async-start(bf16[16,64,1536]{2,1,0:T(8,128)(2,1)} %bitcast.55), calls=%async_computation.1 | async-start | bytes 6291456 | tf_op jit(solution)/shard_map/all_to_all | solution.py:107
  124.5 4.0 %fusion.27 = f32[16,64,512]{2,1,0:T(8,128)} fusion(bf16[1024,64]{0,1:T(8,128)(2,1)S(1)} %fusion.51, bf16[1024,16]{0,1:T(8,128)(2,1)S(1)} %copy.23, bf16[1024,1664]{1,0:T(8,128)(2,1)} %bitcast.64), kind=kOutput, calls=%fused_computation.29 | convolution fusion | flops 1075314688 | bytes 3309568 | tf_op jit(solution)/shard_map/sar,sq->arq/dot_general | solution.py:99
  128.5 6.1 %fusion.8 = f32[16,1024,64]{1,2,0:T(8,128)} fusion(bf16[1024,1664]{1,0:T(8,128)(2,1)} %bitcast.65, bf16[1024,64]{0,1:T(8,128)(2,1)S(1)} %fusion.54, bf16[1024,16]{0,1:T(8,128)(2,1)S(1)} %copy.23), kind=kOutput, calls=%fused_computation.13 | convolution fusion | flops 2148532224 | bytes 6455296 | tf_op jit(solution)/shard_map/sd,sar->adr/dot_general | solution.py:98
  135.2 4.5 %fusion.61 = f32[512,512]{1,0:T(8,128)S(1)} fusion(bf16[512,8192]{1,0:T(8,128)(2,1)S(1)} %copy-done.5, bf16[8192,512]{1,0:T(8,128)(2,1)S(1)} %bitcast.59), kind=kOutput, calls=%fused_computation.84 | convolution fusion | flops 4294967296 | bytes 17825792 | tf_op jit(solution)/shard_map/dot_general | solution.py:109
  139.6 32.9 %all-to-all-done.1 = bf16[16,64,1536]{2,1,0:T(8,128)(2,1)} async-done(((bf16[16,64,1536]{2,1,0:T(8,128)(2,1)}), bf16[16,64,1536]{2,1,0:T(8,128)(2,1)}, u32[]{:S(2)}, u32[]{:S(2)}) %all-to-all-start.1) | async-done | bytes 3145760 | tf_op jit(solution)/shard_map/all_to_all | solution.py:107
  172.6 2.9 %fusion.34 = bf16[512,512]{1,0:T(8,128)(2,1)} fusion(f32[512,512]{1,0:T(8,128)S(1)} %fusion.61, bf16[1024,1536]{1,0:T(8,128)(2,1)} %bitcast.11, s32[512]{0:T(512)S(1)} %multiply_add_fusion), kind=kOutput, calls=%fused_computation.32 | convolution fusion | flops 537919488 | bytes 2623488 | tf_op jit(solution)/shard_map/st,sc->tc/dot_general | solution.py:111
  175.5 4.5 %add_convert_fusion = bf16[512,1024]{1,0:T(8,128)(2,1)} fusion(f32[512,1024]{1,0:T(8,128)} %reduce-scatter.2.cloned.1.call-done, bf16[1024,1536]{1,0:T(8,128)(2,1)} %bitcast.11, s32[512]{0:T(512)S(1)} %multiply_add_fusion), kind=kOutput, calls=%fused_computation.19 | convolution fusion | flops 1075314688 | bytes 5244928 | tf_op jit(solution)/shard_map/st,sc->tc/dot_general | solution.py:114
  (43 shorter events, 1.4 us)
Async XLA Ops:
  7.2 70.0 %copy-start = (bf16[16,1024,64]{1,2,0:T(8,128)(2,1)S(1)}, bf16[16,1024,64]{1,2,0:T(8,128)(2,1)}, u32[]{:S(2)}) copy-start(bf16[16,1024,64]{1,2,0:T(8,128)(2,1)} %param.9) | copy-start | bytes 6291460
  7.2 112.8 %all-gather.2.cloned.1.call-start = ((), (), s32[]{:S(2)}) async-start(), calls=%async_computation.3 | async-start | bytes 9437184 | tf_op jit(solution)/shard_map/all_gather | solution.py:41
  7.9 167.6 %reduce-scatter.2.cloned.1.call-start = ((), (), s32[]{:S(2)}) async-start(), calls=%async_computation.4 | async-start | bytes 18874368 | tf_op jit(solution)/shard_map/reduce_scatter | solution.py:70
  8.0 4.8 %copy-start.3 = (bf16[512,1024]{1,0:T(8,128)(2,1)S(1)}, bf16[512,1024]{1,0:T(8,128)(2,1)}, u32[]{:S(2)}) copy-start(bf16[512,1024]{1,0:T(8,128)(2,1)} %param.6) | copy-start | bytes 3145732
  10.9 5.1 %slice-start = ((s8[8388608]{0:T(1024)(128)(4,1)}), s8[4194304]{0:T(1024)(128)(4,1)S(1)}, s32[]{:S(2)}) async-start(s8[8388608]{0:T(1024)(128)(4,1)} %bitcast.56), calls=%async_computation.5 | async-start | bytes 8388608
  12.8 3.2 %slice-start.1 = ((s8[8388608]{0:T(1024)(128)(4,1)}), s8[4194304]{0:T(1024)(128)(4,1)S(1)}, s32[]{:S(2)}) async-start(s8[8388608]{0:T(1024)(128)(4,1)} %bitcast.56), calls=%async_computation.6 | async-start | bytes 8388608
  14.1 1.9 %copy-start.4 = (bf16[512,512]{1,0:T(8,128)(2,1)S(1)}, bf16[512,512]{1,0:T(8,128)(2,1)}, u32[]{:S(2)}) copy-start(bf16[512,512]{1,0:T(8,128)(2,1)} %param.7) | copy-start | bytes 1572868
  75.2 1.8 copy-start.2
  81.1 1.2 copy-start.6
  84.9 3.1 %collective-permute-start = (f32[512,128]{0,1:T(8,128)S(1)}, f32[512,128]{0,1:T(8,128)S(1)}, u32[]{:S(2)}, u32[]{:S(2)}) collective-permute-start(f32[512,128]{0,1:T(8,128)S(1)} %broadcast_select_fusion.2), channel_id=1, source_target_pairs={{0,1},{1,0},{2,3},{3,2},{4,5},{5,4},{6,7},{7,6},{8,9},{9,8},{10,11... | collective-permute-start | bytes 786440 | tf_op jit(solution)/shard_map/ppermute | solution.py:16
  88.1 11.0 %collective-permute-start.1 = (f32[512,128]{0,1:T(8,128)S(1)}, f32[512,128]{0,1:T(8,128)S(1)}, u32[]{:S(2)}, u32[]{:S(2)}) collective-permute-start(f32[512,128]{0,1:T(8,128)S(1)} %select_add_fusion), channel_id=1, source_target_pairs={{0,2},{1,3},{2,0},{3,1},{4,6},{5,7},{6,4},{7,5},{8,10},{9,11},{10,... | collective-permute-start | bytes 786440 | tf_op jit(solution)/shard_map/ppermute | solution.py:21
  99.2 12.2 %collective-permute-start.2 = (f32[512,128]{0,1:T(8,128)S(1)}, f32[512,128]{0,1:T(8,128)S(1)}, u32[]{:S(2)}, u32[]{:S(2)}) collective-permute-start(f32[512,128]{0,1:T(8,128)S(1)} %add.35), channel_id=1, source_target_pairs={{0,6},{1,7},{2,4},{3,5},{4,2},{5,3},{6,0},{7,1},{8,14},{9,15},{10,... | collective-permute-start | bytes 786440 | tf_op jit(solution)/shard_map/ppermute | solution.py:21
  111.4 3.0 %collective-permute-start.3 = (f32[512,128]{0,1:T(8,128)S(1)}, f32[512,128]{0,1:T(8,128)S(1)}, u32[]{:S(2)}, u32[]{:S(2)}) collective-permute-start(f32[512,128]{0,1:T(8,128)S(1)} %add.36), channel_id=1, source_target_pairs={{0,1},{1,0},{2,3},{3,2},{4,5},{5,4},{6,7},{7,6},{8,9},{9,8},{10,11... | collective-permute-start | bytes 786440 | tf_op jit(solution)/shard_map/ppermute | solution.py:23
  120.0 52.6 %all-to-all-start.1 = ((bf16[16,64,1536]{2,1,0:T(8,128)(2,1)}), bf16[16,64,1536]{2,1,0:T(8,128)(2,1)}, u32[]{:S(2)}, u32[]{:S(2)}) async-start(bf16[16,64,1536]{2,1,0:T(8,128)(2,1)} %bitcast.55), calls=%async_computation.1 | async-start | bytes 6291456 | tf_op jit(solution)/shard_map/all_to_all | solution.py:107
  124.5 10.2 %slice-start.2 = ((s8[8388608]{0:T(1024)(128)(4,1)}), s8[4194304]{0:T(1024)(128)(4,1)S(1)}, s32[]{:S(2)}) async-start(s8[8388608]{0:T(1024)(128)(4,1)} %bitcast.58), calls=%async_computation.7 | async-start | bytes 8388608
  128.5 6.1 %slice-start.3 = ((s8[8388608]{0:T(1024)(128)(4,1)}), s8[4194304]{0:T(1024)(128)(4,1)S(1)}, s32[]{:S(2)}) async-start(s8[8388608]{0:T(1024)(128)(4,1)} %bitcast.58), calls=%async_computation.8 | async-start | bytes 8388608
  128.5 6.7 %copy-start.5 = (bf16[512,8192]{1,0:T(8,128)(2,1)S(1)}, bf16[512,8192]{1,0:T(8,128)(2,1)}, u32[]{:S(2)}) copy-start(bf16[512,8192]{1,0:T(8,128)(2,1)} %all-gather.2.cloned.1.call-done) | copy-start | bytes 25165828
  172.6 7.4 %copy-start.1 = (bf16[16,1024,64]{1,2,0:T(8,128)(2,1)S(1)}, bf16[16,1024,64]{1,2,0:T(8,128)(2,1)}, u32[]{:S(2)}) copy-start(bf16[16,1024,64]{1,2,0:T(8,128)(2,1)} %param.9) | copy-start | bytes 6291460
Sparse Core Ops, SparseCore 0:
  9.7 53.2 all-gather.1
  65.5 96.5 reduce-scatter.1

commit v10 on v7

--- a/solution.py
+++ b/solution.py
@@ -14,12 +14,15 @@
     give = jnp.where(keep_first, x[half:], x[:half])
     pair = [(t, t ^ 1) for t in range(n)]
     mine = keep + lax.ppermute(give, "tensor", pair)
-    step = 2
-    while step < n:
-        flip = 2 * step - 2 if step * 2 == n else step
-        perm = [(t, t ^ flip) for t in range(n)]
-        mine = mine + lax.ppermute(mine, "tensor", perm)
-        step *= 2
+    if n == 8:
+        got = [lax.ppermute(mine, "tensor", [(t, t ^ f) for t in range(n)]) for f in (2, 4, 6)]
+        mine = (mine + got[0]) + (got[1] + got[2])
+    else:
+        step = 2
+        while step < n:
+            perm = [(t, t ^ step) for t in range(n)]
+            mine = mine + lax.ppermute(mine, "tensor", perm)
+            step *= 2
     other = lax.ppermute(mine, "tensor", pair)
     first = jnp.where(keep_first, mine, other)
     second = jnp.where(keep_first, other, mine)

time: 187 us -> 185 us (0.989)
    ppermute x2 -> x3, waiting for transfers between devices: 18.8 us -> 17.7 us  [tensor_sum(): lax.ppermute(mine, 'tensor', [(t, t ^ f) for t in range(n)])]
    ppermute x2 -> x3, starting transfers between devices: 4.05 us -> 3.94 us  [tensor_sum(): lax.ppermute(mine, 'tensor', [(t, t ^ f) for t in range(n)])]
  transfers between devices with their start and end apart: 7 -> 8, of which waited for: 5 -> 5; matrix products, arithmetic and copies ran while one was open for 25% -> 25% of each run, Pallas kernels for 0% -> 0%
where the time goes in v10:
time: 185 us
  waiting for transfers between devices  53.2 us (29%)
  blocking collectives  50.5 us (27%)
  matrix products  46.4 us (25%)
  between operations  14.2 us (8%)
  starting transfers between devices  11.9 us (6%)
  other arithmetic  4.78 us (3%)
  local copies, waits for them, and re-layouts  4 us (2%)
    all_to_all x1, blocking collectives, per_device(): got = lax.all_to_all(send, 'dp', split_axis=0, concat_axis=0, tiled=True)  50.5 us
    all_to_all x1, waiting for transfers between devices, per_device(): back = lax.all_to_all(back, 'dp', split_axis=0, concat_axis=0, tiled=True)  32.3 us
    ppermute x3, waiting for transfers between devices, tensor_sum(): lax.ppermute(mine, 'tensor', [(t, t ^ f) for t in range(n)])  17.7 us
    dot_general x1, matrix products, per_device(): lax.dot_general(cot_late, weight_late, (((1,), (1,)), ((), ())), preferre...  8.65 us
    dot_general x1, matrix products, per_device(): jnp.einsum('sd,sar->adr', got_tok, grad_spread, preferred_element_type=jn...  6.31 us
    dot_general x1, matrix products, per_device(): jnp.dot(pick, payload, preferred_element_type=jnp.float32)  5.42 us
    dot_general x1, matrix products, per_device(): jnp.einsum('st,sc->tc', pick, back[:, query_portion:], preferred_element_...  4.49 us
    all_to_all x1, starting transfers between devices, per_device(): back = lax.all_to_all(back, 'dp', split_axis=0, concat_axis=0, tiled=True)  4.49 us
  transfers between devices with their start and end apart: 8, of which 5 were waited for; matrix products, arithmetic and copies ran while one was open for 25% of the time, Pallas kernels for 0%

profile of v10, /device:TPU:1, one launch (start us, length us, event | category | flops | bytes accessed | tf_op | source)
XLA Modules:
  0.0 185.0 jit_solution(2865575584120289899)
XLA Ops:
  7.2 0.7 all-gather.2.cloned.1.call-update
  8.0 0.7 add_select_fusion.1
  8.7 1.2 reduce-window.6
  9.8 0.2 slice_reduce_fusion
  10.2 0.1 fusion.52
  10.4 5.4 %convolution_convert_fusion = bf16[1024,1664]{1,0:T(8,128)(2,1)} fusion(bf16[512,128]{1,0:T(8,128)(2,1)S(1)} %fusion.52, bf16[512,512]{1,0:T(8,128)(2,1)} %param.7, bf16[512,1024]{1,0:T(8,128)(2,1)} %param.6, s32[512]{0:T(512)S(1)} %multiply_add_fusion), kind=kOutput, calls=%fused_computation.3 | convolution fusion | flops 1752170496 | bytes 5113856 | tf_op jit(solution)/shard_map/dot_general | solution.py:57
  15.8 8.7 %fusion.60 = f32[512,8192]{1,0:T(8,128)} fusion(bf16[512,512]{1,0:T(8,128)(2,1)S(1)} %copy-done.4, bf16[8192,512]{1,0:T(8,128)(2,1)S(1)} %copy-done.2), kind=kOutput, calls=%fused_computation.84 | convolution fusion | flops 4294967296 | bytes 25690112 | tf_op jit(solution)/shard_map/dot_general | solution.py:62
  24.5 50.5 %all_to_all.24 = bf16[16,64,1664]{2,1,0:T(8,128)(2,1)S(1)} all-to-all(bf16[16,64,1664]{2,1,0:T(8,128)(2,1)} %bitcast.60), channel_id=1, replica_groups=mesh['dp'=16,'tensor'=8] {'dp'}, dimensions={0} | all-to-all | bytes 6815744 | tf_op jit(solution)/shard_map/all_to_all | solution.py:66
  74.9 1.8 copy-done.3
  76.9 4.0 %fusion.19 = f32[1024,1024]{0,1:S(1)} fusion(bf16[1024,1024]{0,1:T(8,128)(2,1)S(1)} %bitcast.51, bf16[1024,1664]{1,0:T(8,128)(2,1)} %bitcast.56), kind=kOutput, calls=%fused_computation.23 | convolution fusion | flops 2147483648 | bytes 8388608
  80.9 0.5 multiply_reduce_fusion.1
  81.4 0.7 copy-done.6
  82.1 2.6 %multiply_reduce_fusion = f32[1024,64]{0,1:T(8,128)S(1)} fusion(bf16[16,64,512]{2,1,0:T(8,128)(2,1)S(1)} %copy-done.6, f32[1024,16]{0,1:T(8,128)S(1)} %convert_element_type.37, bf16[1024,1664]{1,0:T(8,128)(2,1)} %bitcast.57), kind=kOutput, calls=%fused_computation.1 | convolution fusion | flops 1075773440 | bytes 2424832 | tf_op jit(solution)/shard_map/sq,arq->sar/dot_general | solution.py:75
  84.7 1.9 %collective-permute-start = (f32[512,128]{0,1:T(8,128)S(1)}, f32[512,128]{0,1:T(8,128)S(1)}, u32[]{:S(2)}, u32[]{:S(2)}) collective-permute-start(f32[512,128]{0,1:T(8,128)S(1)} %broadcast_select_fusion.2), channel_id=1, source_target_pairs={{0,1},{1,0},{2,3},{3,2},{4,5},{5,4},{6,7},{7,6},{8,9},{9,8},{10,11... | collective-permute-start | bytes 786440 | tf_op jit(solution)/shard_map/ppermute | solution.py:16
  86.6 1.3 collective-permute-done
  88.0 1.4 collective-permute-start.1
  89.4 2.4 %collective-permute-start.2 = (f32[512,128]{0,1:T(8,128)S(1)}, f32[512,128]{0,1:T(8,128)S(1)}, u32[]{:S(2)}, u32[]{:S(2)}) collective-permute-start(f32[512,128]{0,1:T(8,128)S(1)} %select_add_fusion), channel_id=1, source_target_pairs={{0,4},{1,5},{2,6},{3,7},{4,0},{5,1},{6,2},{7,3},{8,12},{9,13},{10,... | collective-permute-start | bytes 786440 | tf_op jit(solution)/shard_map/ppermute | solution.py:18
  91.9 7.1 %collective-permute-done.1 = f32[512,128]{0,1:T(8,128)S(1)} collective-permute-done((f32[512,128]{0,1:T(8,128)S(1)}, f32[512,128]{0,1:T(8,128)S(1)}, u32[]{:S(2)}, u32[]{:S(2)}) %collective-permute-start.1) | collective-permute-done | bytes 262176 | tf_op jit(solution)/shard_map/ppermute | solution.py:18
  99.0 10.6 %collective-permute-done.2 = f32[512,128]{0,1:T(8,128)S(1)} collective-permute-done((f32[512,128]{0,1:T(8,128)S(1)}, f32[512,128]{0,1:T(8,128)S(1)}, u32[]{:S(2)}, u32[]{:S(2)}) %collective-permute-start.2) | collective-permute-done | bytes 262176 | tf_op jit(solution)/shard_map/ppermute | solution.py:18
  109.7 1.6 collective-permute-start.4
  111.2 1.2 collective-permute-done.4
  112.5 1.3 fusion.14
  113.8 2.4 %bitcast_convert_fusion = bf16[1024,1024]{1,0:T(8,128)(2,1)S(1)} fusion(bf16[16,1024,64]{1,2,0:T(8,128)(2,1)S(1)} %copy-done, bf16[1024,64]{0,1:T(8,128)(2,1)S(1)} %fusion.51, bf16[1024,16]{0,1:T(8,128)(2,1)S(1)} %copy.23), kind=kOutput, calls=%fused_computation | convolution fusion | flops 2149580800 | bytes 4358144 | tf_op jit(solution)/shard_map/sar,adr->sd/dot_general | solution.py:90
  116.2 1.9 %pad_maximum_fusion = bf16[1024,1536]{1,0:T(8,128)(2,1)} fusion(bf16[1024,1024]{1,0:T(8,128)(2,1)S(1)} %bitcast_convert_fusion, bf16[1024,512]{1,0:T(8,128)(2,1)S(1)} %fusion.14), kind=kLoop, calls=%fused_computation.4 | loop fusion | flops 6291456 | bytes 6291456 | tf_op jit(solution)/shard_map/concatenate | solution.py:100
  118.1 4.5 %all-to-all-start.1 = ((bf16[16,64,1536]{2,1,0:T(8,128)(2,1)}), bf16[16,64,1536]{2,1,0:T(8,128)(2,1)}, u32[]{:S(2)}, u32[]{:S(2)}) async-start(bf16[16,64,1536]{2,1,0:T(8,128)(2,1)} %bitcast.10), calls=%async_computation.1 | async-start | bytes 6291456 | tf_op jit(solution)/shard_map/all_to_all | solution.py:102
  122.6 4.0 %fusion.28 = f32[16,64,512]{2,1,0:T(8,128)} fusion(bf16[1024,64]{0,1:T(8,128)(2,1)S(1)} %fusion.48, bf16[1024,16]{0,1:T(8,128)(2,1)S(1)} %copy.23, bf16[1024,1664]{1,0:T(8,128)(2,1)} %bitcast.58), kind=kOutput, calls=%fused_computation.30 | convolution fusion | flops 1075314688 | bytes 3309568 | tf_op jit(solution)/shard_map/sar,sq->arq/dot_general | solution.py:94
  126.5 6.3 %fusion.8 = f32[16,1024,64]{1,2,0:T(8,128)} fusion(bf16[1024,1664]{1,0:T(8,128)(2,1)} %bitcast.59, bf16[1024,64]{0,1:T(8,128)(2,1)S(1)} %fusion.51, bf16[1024,16]{0,1:T(8,128)(2,1)S(1)} %copy.23), kind=kOutput, calls=%fused_computation.13 | convolution fusion | flops 2148532224 | bytes 6455296 | tf_op jit(solution)/shard_map/sd,sar->adr/dot_general | solution.py:93
  132.8 1.1 copy-done.5
  134.0 4.5 %fusion.59 = f32[512,512]{1,0:T(8,128)S(1)} fusion(bf16[512,8192]{1,0:T(8,128)(2,1)S(1)} %copy-done.5, bf16[8192,512]{1,0:T(8,128)(2,1)S(1)} %bitcast.53), kind=kOutput, calls=%fused_computation.83 | convolution fusion | flops 4294967296 | bytes 17825792 | tf_op jit(solution)/shard_map/dot_general | solution.py:104
  138.4 32.3 %all-to-all-done.1 = bf16[16,64,1536]{2,1,0:T(8,128)(2,1)} async-done(((bf16[16,64,1536]{2,1,0:T(8,128)(2,1)}), bf16[16,64,1536]{2,1,0:T(8,128)(2,1)}, u32[]{:S(2)}, u32[]{:S(2)}) %all-to-all-start.1) | async-done | bytes 3145760 | tf_op jit(solution)/shard_map/all_to_all | solution.py:102
  170.8 2.9 %fusion.34 = bf16[512,512]{1,0:T(8,128)(2,1)} fusion(f32[512,512]{1,0:T(8,128)S(1)} %fusion.59, bf16[1024,1536]{1,0:T(8,128)(2,1)} %bitcast.11, s32[512]{0:T(512)S(1)} %multiply_add_fusion), kind=kOutput, calls=%fused_computation.32 | convolution fusion | flops 537919488 | bytes 2623488 | tf_op jit(solution)/shard_map/st,sc->tc/dot_general | solution.py:106
  173.7 4.5 %add_convert_fusion = bf16[512,1024]{1,0:T(8,128)(2,1)} fusion(f32[512,1024]{1,0:T(8,128)} %reduce-scatter.2.cloned.1.call-done, bf16[1024,1536]{1,0:T(8,128)(2,1)} %bitcast.11, s32[512]{0:T(512)S(1)} %multiply_add_fusion), kind=kOutput, calls=%fused_computation.19 | convolution fusion | flops 1075314688 | bytes 5244928 | tf_op jit(solution)/shard_map/st,sc->tc/dot_general | solution.py:109
  (37 shorter events, 0.8 us)
Async XLA Ops:
  7.2 69.7 %copy-start = (bf16[16,1024,64]{1,2,0:T(8,128)(2,1)S(1)}, bf16[16,1024,64]{1,2,0:T(8,128)(2,1)}, u32[]{:S(2)}) copy-start(bf16[16,1024,64]{1,2,0:T(8,128)(2,1)} %param.9) | copy-start | bytes 6291460
  7.2 110.9 %all-gather.2.cloned.1.call-start = ((), (), s32[]{:S(2)}) async-start(), calls=%async_computation.3 | async-start | bytes 9437184 | tf_op jit(solution)/shard_map/all_gather | solution.py:44
  7.9 165.8 %reduce-scatter.2.cloned.1.call-start = ((), (), s32[]{:S(2)}) async-start(), calls=%async_computation.4 | async-start | bytes 18874368 | tf_op jit(solution)/shard_map/reduce_scatter | solution.py:65
  10.3 5.5 %copy-start.2 = (bf16[8192,512]{1,0:T(8,128)(2,1)S(1)}, bf16[8192,512]{1,0:T(8,128)(2,1)}, u32[]{:S(2)}) copy-start(bf16[8192,512]{1,0:T(8,128)(2,1)} %param.8) | copy-start | bytes 25165828
  10.4 5.4 %copy-start.4 = (bf16[512,512]{1,0:T(8,128)(2,1)S(1)}, bf16[512,512]{1,0:T(8,128)(2,1)}, u32[]{:S(2)}) copy-start(bf16[512,512]{1,0:T(8,128)(2,1)} %param.7) | copy-start | bytes 1572868
  74.9 1.8 copy-start.3
  80.9 1.2 copy-start.6
  84.7 3.2 %collective-permute-start = (f32[512,128]{0,1:T(8,128)S(1)}, f32[512,128]{0,1:T(8,128)S(1)}, u32[]{:S(2)}, u32[]{:S(2)}) collective-permute-start(f32[512,128]{0,1:T(8,128)S(1)} %broadcast_select_fusion.2), channel_id=1, source_target_pairs={{0,1},{1,0},{2,3},{3,2},{4,5},{5,4},{6,7},{7,6},{8,9},{9,8},{10,11... | collective-permute-start | bytes 786440 | tf_op jit(solution)/shard_map/ppermute | solution.py:16
  88.0 11.0 %collective-permute-start.1 = (f32[512,128]{0,1:T(8,128)S(1)}, f32[512,128]{0,1:T(8,128)S(1)}, u32[]{:S(2)}, u32[]{:S(2)}) collective-permute-start(f32[512,128]{0,1:T(8,128)S(1)} %select_add_fusion), channel_id=1, source_target_pairs={{0,2},{1,3},{2,0},{3,1},{4,6},{5,7},{6,4},{7,5},{8,10},{9,11},{10,... | collective-permute-start | bytes 786440 | tf_op jit(solution)/shard_map/ppermute | solution.py:18
  89.4 20.2 %collective-permute-start.2 = (f32[512,128]{0,1:T(8,128)S(1)}, f32[512,128]{0,1:T(8,128)S(1)}, u32[]{:S(2)}, u32[]{:S(2)}) collective-permute-start(f32[512,128]{0,1:T(8,128)S(1)} %select_add_fusion), channel_id=1, source_target_pairs={{0,4},{1,5},{2,6},{3,7},{4,0},{5,1},{6,2},{7,3},{8,12},{9,13},{10,... | collective-permute-start | bytes 786440 | tf_op jit(solution)/shard_map/ppermute | solution.py:18
  91.8 17.8 %collective-permute-start.3 = (f32[512,128]{0,1:T(8,128)S(1)}, f32[512,128]{0,1:T(8,128)S(1)}, u32[]{:S(2)}, u32[]{:S(2)}) collective-permute-start(f32[512,128]{0,1:T(8,128)S(1)} %select_add_fusion), channel_id=1, source_target_pairs={{0,6},{1,7},{2,4},{3,5},{4,2},{5,3},{6,0},{7,1},{8,14},{9,15},{10,... | collective-permute-start | bytes 786440 | tf_op jit(solution)/shard_map/ppermute | solution.py:18
  109.7 2.7 %collective-permute-start.4 = (f32[512,128]{0,1:T(8,128)S(1)}, f32[512,128]{0,1:T(8,128)S(1)}, u32[]{:S(2)}, u32[]{:S(2)}) collective-permute-start(f32[512,128]{0,1:T(8,128)S(1)} %add_add_fusion), channel_id=1, source_target_pairs={{0,1},{1,0},{2,3},{3,2},{4,5},{5,4},{6,7},{7,6},{8,9},{9,8},{10,11... | collective-permute-start | bytes 786440 | tf_op jit(solution)/shard_map/ppermute | solution.py:26
  118.1 52.7 %all-to-all-start.1 = ((bf16[16,64,1536]{2,1,0:T(8,128)(2,1)}), bf16[16,64,1536]{2,1,0:T(8,128)(2,1)}, u32[]{:S(2)}, u32[]{:S(2)}) async-start(bf16[16,64,1536]{2,1,0:T(8,128)(2,1)} %bitcast.10), calls=%async_computation.1 | async-start | bytes 6291456 | tf_op jit(solution)/shard_map/all_to_all | solution.py:102
  122.5 10.3 %slice-start = ((s8[8388608]{0:T(1024)(128)(4,1)}), s8[4194304]{0:T(1024)(128)(4,1)S(1)}, s32[]{:S(2)}) async-start(s8[8388608]{0:T(1024)(128)(4,1)} %bitcast.52), calls=%async_computation.5 | async-start | bytes 8388608
  126.5 6.3 %slice-start.1 = ((s8[8388608]{0:T(1024)(128)(4,1)}), s8[4194304]{0:T(1024)(128)(4,1)S(1)}, s32[]{:S(2)}) async-start(s8[8388608]{0:T(1024)(128)(4,1)} %bitcast.52), calls=%async_computation.6 | async-start | bytes 8388608
  126.5 7.4 %copy-start.5 = (bf16[512,8192]{1,0:T(8,128)(2,1)S(1)}, bf16[512,8192]{1,0:T(8,128)(2,1)}, u32[]{:S(2)}) copy-start(bf16[512,8192]{1,0:T(8,128)(2,1)} %all-gather.2.cloned.1.call-done) | copy-start | bytes 25165828
  170.8 7.4 %copy-start.1 = (bf16[16,1024,64]{1,2,0:T(8,128)(2,1)S(1)}, bf16[16,1024,64]{1,2,0:T(8,128)(2,1)}, u32[]{:S(2)}) copy-start(bf16[16,1024,64]{1,2,0:T(8,128)(2,1)} %param.9) | copy-start | bytes 6291460
Sparse Core Ops, SparseCore 0:
  9.7 53.2 all-gather.1
  65.5 102.2 reduce-scatter.1

commit v11 on v10

--- a/solution.py
+++ b/solution.py
@@ -15,7 +15,13 @@
     pair = [(t, t ^ 1) for t in range(n)]
     mine = keep + lax.ppermute(give, "tensor", pair)
     if n == 8:
-        got = [lax.ppermute(mine, "tensor", [(t, t ^ f) for t in range(n)]) for f in (2, 4, 6)]
+        got = [lax.ppermute(mine, "tensor", [(t, t ^ f) for t in range(n)]) for f in (2, 6)]
+        far = [(t, t ^ 4) for t in range(n)]
+        quarter = mine.shape[0] // 2
+        got.insert(1, jnp.concatenate(
+            [lax.ppermute(mine[:quarter], "tensor", far), lax.ppermute(mine[quarter:], "tensor", far)],
+            axis=0,
+        ))
         mine = (mine + got[0]) + (got[1] + got[2])
     else:
         step = 2

time: 185 us -> 185 us (level)
  waiting for transfers between devices: 53.2 us -> 50.9 us
  starting transfers between devices: 11.9 us -> 14 us
    ppermute x3 -> x2, waiting for transfers between devices: 17.7 us -> 0.01 us  [tensor_sum(): lax.ppermute(mine, 'tensor', [(t, t ^ f) for t in range(n)])]
    ppermute x0 -> x2, waiting for transfers between devices: none -> 15.4 us  [the longest x1 11.2 us: tensor_sum(): lax.ppermute(mine[:quarter], 'tensor', far)]
    ppermute x0 -> x2, starting transfers between devices: none -> 3.05 us  [the longest x1 2.28 us: tensor_sum(): lax.ppermute(mine[quarter:], 'tensor', far)]
    ppermute x3 -> x2, starting transfers between devices: 3.94 us -> 3.11 us  [tensor_sum(): lax.ppermute(mine, 'tensor', [(t, t ^ f) for t in range(n)])]
  transfers between devices with their start and end apart: 8 -> 9, of which waited for: 5 -> 5; matrix products, arithmetic and copies ran while one was open for 25% -> 25% of each run, Pallas kernels for 0% -> 0%
where the time goes in v11:
time: 185 us
  waiting for transfers between devices  50.9 us (28%)
  blocking collectives  50.5 us (27%)
  matrix products  46.5 us (25%)
  between operations  14.2 us (8%)
  starting transfers between devices  14 us (8%)
  other arithmetic  4.78 us (3%)
  local copies, waits for them, and re-layouts  4.04 us (2%)
    all_to_all x1, blocking collectives, per_device(): got = lax.all_to_all(send, 'dp', split_axis=0, concat_axis=0, tiled=True)  50.5 us
    all_to_all x1, waiting for transfers between devices, per_device(): back = lax.all_to_all(back, 'dp', split_axis=0, concat_axis=0, tiled=True)  32.2 us
    ppermute x1, waiting for transfers between devices, tensor_sum(): lax.ppermute(mine[:quarter], 'tensor', far)  11.2 us
    dot_general x1, matrix products, per_device(): lax.dot_general(cot_late, weight_late, (((1,), (1,)), ((), ())), preferre...  8.65 us
    dot_general x1, matrix products, per_device(): jnp.einsum('sd,sar->adr', got_tok, grad_spread, preferred_element_type=jn...  6.36 us
    dot_general x1, matrix products, per_device(): jnp.dot(pick, payload, preferred_element_type=jnp.float32)  5.42 us
    dot_general x1, matrix products, per_device(): jnp.einsum('st,sc->tc', pick, back[:, query_portion:], preferred_element_...  4.49 us
    all_to_all x1, starting transfers between devices, per_device(): back = lax.all_to_all(back, 'dp', split_axis=0, concat_axis=0, tiled=True)  4.49 us
  transfers between devices with their start and end apart: 9, of which 5 were waited for; matrix products, arithmetic and copies ran while one was open for 25% of the time, Pallas kernels for 0%

profile of v11, /device:TPU:1, one launch (start us, length us, event | category | flops | bytes accessed | tf_op | source)
XLA Modules:
  0.0 184.9 jit_solution(269381455220164846)
XLA Ops:
  7.2 0.7 all-gather.2.cloned.1.call-update
  8.0 0.7 add_select_fusion.1
  8.7 1.2 reduce-window.6
  10.4 5.4 %convolution_convert_fusion = bf16[1024,1664]{1,0:T(8,128)(2,1)} fusion(bf16[512,128]{1,0:T(8,128)(2,1)S(1)} %fusion.53, bf16[512,512]{1,0:T(8,128)(2,1)} %param.7, bf16[512,1024]{1,0:T(8,128)(2,1)} %param.6, s32[512]{0:T(512)S(1)} %multiply_add_fusion), kind=kOutput, calls=%fused_computation.3 | convolution fusion | flops 1752170496 | bytes 5113856 | tf_op jit(solution)/shard_map/dot_general | solution.py:63
  15.8 8.7 %fusion.62 = f32[512,8192]{1,0:T(8,128)} fusion(bf16[512,512]{1,0:T(8,128)(2,1)S(1)} %copy-done.4, bf16[8192,512]{1,0:T(8,128)(2,1)S(1)} %copy-done.2), kind=kOutput, calls=%fused_computation.86 | convolution fusion | flops 4294967296 | bytes 25690112 | tf_op jit(solution)/shard_map/dot_general | solution.py:68
  24.5 50.5 %all_to_all.24 = bf16[16,64,1664]{2,1,0:T(8,128)(2,1)S(1)} all-to-all(bf16[16,64,1664]{2,1,0:T(8,128)(2,1)} %bitcast.60), channel_id=1, replica_groups=mesh['dp'=16,'tensor'=8] {'dp'}, dimensions={0} | all-to-all | bytes 6815744 | tf_op jit(solution)/shard_map/all_to_all | solution.py:72
  74.9 1.8 copy-done.3
  76.9 4.0 %fusion.19 = f32[1024,1024]{0,1:S(1)} fusion(bf16[1024,1024]{0,1:T(8,128)(2,1)S(1)} %bitcast.51, bf16[1024,1664]{1,0:T(8,128)(2,1)} %bitcast.56), kind=kOutput, calls=%fused_computation.23 | convolution fusion | flops 2147483648 | bytes 8388608
  80.9 0.5 multiply_reduce_fusion.1
  81.4 0.7 copy-done.6
  82.1 2.6 %multiply_reduce_fusion = f32[1024,64]{0,1:T(8,128)S(1)} fusion(bf16[16,64,512]{2,1,0:T(8,128)(2,1)S(1)} %copy-done.6, f32[1024,16]{0,1:T(8,128)S(1)} %convert_element_type.37, bf16[1024,1664]{1,0:T(8,128)(2,1)} %bitcast.57), kind=kOutput, calls=%fused_computation.1 | convolution fusion | flops 1075773440 | bytes 2424832 | tf_op jit(solution)/shard_map/sq,arq->sar/dot_general | solution.py:81
  84.7 1.9 %collective-permute-start = (f32[512,128]{0,1:T(8,128)S(1)}, f32[512,128]{0,1:T(8,128)S(1)}, u32[]{:S(2)}, u32[]{:S(2)}) collective-permute-start(f32[512,128]{0,1:T(8,128)S(1)} %broadcast_select_fusion.2), channel_id=1, source_target_pairs={{0,1},{1,0},{2,3},{3,2},{4,5},{5,4},{6,7},{7,6},{8,9},{9,8},{10,11... | collective-permute-start | bytes 786440 | tf_op jit(solution)/shard_map/ppermute | solution.py:16
  86.6 1.3 collective-permute-done
  88.0 1.4 collective-permute-start.1
  89.4 1.7 collective-permute-start.4
  91.1 0.8 collective-permute-start.2
  91.9 2.3 %collective-permute-start.3 = (f32[256,128]{0,1:T(8,128)S(1)}, f32[256,128]{0,1:T(8,128)S(1)}, u32[]{:S(2)}, u32[]{:S(2)}) collective-permute-start(f32[256,128]{0,1:T(8,128)S(1)} %get-tuple-element.19), channel_id=1, source_target_pairs={{0,4},{1,5},{2,6},{3,7},{4,0},{5,1},{6,2},{7,3},{8,12},{9,13},{10,... | collective-permute-start | bytes 393224 | tf_op jit(solution)/shard_map/ppermute | solution.py:22
  94.2 11.2 %collective-permute-done.2 = f32[256,128]{0,1:T(8,128)S(1)} collective-permute-done((f32[256,128]{0,1:T(8,128)S(1)}, f32[256,128]{0,1:T(8,128)S(1)}, u32[]{:S(2)}, u32[]{:S(2)}) %collective-permute-start.2) | collective-permute-done | bytes 131104 | tf_op jit(solution)/shard_map/ppermute | solution.py:22
  105.4 4.2 %collective-permute-done.3 = f32[256,128]{0,1:T(8,128)S(1)} collective-permute-done((f32[256,128]{0,1:T(8,128)S(1)}, f32[256,128]{0,1:T(8,128)S(1)}, u32[]{:S(2)}, u32[]{:S(2)}) %collective-permute-start.3) | collective-permute-done | bytes 131104 | tf_op jit(solution)/shard_map/ppermute | solution.py:22
  109.7 1.4 collective-permute-start.5
  111.1 1.2 collective-permute-done.5
  112.4 1.3 fusion.14
  113.7 2.4 %bitcast_convert_fusion = bf16[1024,1024]{1,0:T(8,128)(2,1)S(1)} fusion(bf16[16,1024,64]{1,2,0:T(8,128)(2,1)S(1)} %copy-done, bf16[1024,64]{0,1:T(8,128)(2,1)S(1)} %fusion.51, bf16[1024,16]{0,1:T(8,128)(2,1)S(1)} %copy.23), kind=kOutput, calls=%fused_computation | convolution fusion | flops 2149580800 | bytes 4358144 | tf_op jit(solution)/shard_map/sar,adr->sd/dot_general | solution.py:96
  116.0 1.9 %pad_maximum_fusion = bf16[1024,1536]{1,0:T(8,128)(2,1)} fusion(bf16[1024,1024]{1,0:T(8,128)(2,1)S(1)} %bitcast_convert_fusion, bf16[1024,512]{1,0:T(8,128)(2,1)S(1)} %fusion.14), kind=kLoop, calls=%fused_computation.4 | loop fusion | flops 6291456 | bytes 6291456 | tf_op jit(solution)/shard_map/concatenate | solution.py:106
  117.9 4.5 %all-to-all-start.1 = ((bf16[16,64,1536]{2,1,0:T(8,128)(2,1)}), bf16[16,64,1536]{2,1,0:T(8,128)(2,1)}, u32[]{:S(2)}, u32[]{:S(2)}) async-start(bf16[16,64,1536]{2,1,0:T(8,128)(2,1)} %bitcast.10), calls=%async_computation.1 | async-start | bytes 6291456 | tf_op jit(solution)/shard_map/all_to_all | solution.py:108
  122.4 4.0 %fusion.28 = f32[16,64,512]{2,1,0:T(8,128)} fusion(bf16[1024,64]{0,1:T(8,128)(2,1)S(1)} %fusion.48, bf16[1024,16]{0,1:T(8,128)(2,1)S(1)} %copy.23, bf16[1024,1664]{1,0:T(8,128)(2,1)} %bitcast.58), kind=kOutput, calls=%fused_computation.30 | convolution fusion | flops 1075314688 | bytes 3309568 | tf_op jit(solution)/shard_map/sar,sq->arq/dot_general | solution.py:100
  126.4 6.4 %fusion.8 = f32[16,1024,64]{1,2,0:T(8,128)} fusion(bf16[1024,1664]{1,0:T(8,128)(2,1)} %bitcast.59, bf16[1024,64]{0,1:T(8,128)(2,1)S(1)} %fusion.51, bf16[1024,16]{0,1:T(8,128)(2,1)S(1)} %copy.23), kind=kOutput, calls=%fused_computation.13 | convolution fusion | flops 2148532224 | bytes 6455296 | tf_op jit(solution)/shard_map/sd,sar->adr/dot_general | solution.py:99
  132.8 1.1 copy-done.5
  133.9 4.5 %fusion.61 = f32[512,512]{1,0:T(8,128)S(1)} fusion(bf16[512,8192]{1,0:T(8,128)(2,1)S(1)} %copy-done.5, bf16[8192,512]{1,0:T(8,128)(2,1)S(1)} %bitcast.53), kind=kOutput, calls=%fused_computation.85 | convolution fusion | flops 4294967296 | bytes 17825792 | tf_op jit(solution)/shard_map/dot_general | solution.py:110
  138.4 32.2 %all-to-all-done.1 = bf16[16,64,1536]{2,1,0:T(8,128)(2,1)} async-done(((bf16[16,64,1536]{2,1,0:T(8,128)(2,1)}), bf16[16,64,1536]{2,1,0:T(8,128)(2,1)}, u32[]{:S(2)}, u32[]{:S(2)}) %all-to-all-start.1) | async-done | bytes 3145760 | tf_op jit(solution)/shard_map/all_to_all | solution.py:108
  170.6 2.9 %fusion.34 = bf16[512,512]{1,0:T(8,128)(2,1)} fusion(f32[512,512]{1,0:T(8,128)S(1)} %fusion.61, bf16[1024,1536]{1,0:T(8,128)(2,1)} %bitcast.11, s32[512]{0:T(512)S(1)} %multiply_add_fusion), kind=kOutput, calls=%fused_computation.32 | convolution fusion | flops 537919488 | bytes 2623488 | tf_op jit(solution)/shard_map/st,sc->tc/dot_general | solution.py:112
  173.5 4.5 %add_convert_fusion = bf16[512,1024]{1,0:T(8,128)(2,1)} fusion(f32[512,1024]{1,0:T(8,128)} %reduce-scatter.2.cloned.1.call-done, bf16[1024,1536]{1,0:T(8,128)(2,1)} %bitcast.11, s32[512]{0:T(512)S(1)} %multiply_add_fusion), kind=kOutput, calls=%fused_computation.19 | convolution fusion | flops 1075314688 | bytes 5244928 | tf_op jit(solution)/shard_map/st,sc->tc/dot_general | solution.py:115
  (40 shorter events, 1.1 us)
Async XLA Ops:
  7.2 69.7 %copy-start = (bf16[16,1024,64]{1,2,0:T(8,128)(2,1)S(1)}, bf16[16,1024,64]{1,2,0:T(8,128)(2,1)}, u32[]{:S(2)}) copy-start(bf16[16,1024,64]{1,2,0:T(8,128)(2,1)} %param.9) | copy-start | bytes 6291460
  7.2 110.7 %all-gather.2.cloned.1.call-start = ((), (), s32[]{:S(2)}) async-start(), calls=%async_computation.3 | async-start | bytes 9437184 | tf_op jit(solution)/shard_map/all_gather | solution.py:50
  7.9 165.6 %reduce-scatter.2.cloned.1.call-start = ((), (), s32[]{:S(2)}) async-start(), calls=%async_computation.4 | async-start | bytes 18874368 | tf_op jit(solution)/shard_map/reduce_scatter | solution.py:71
  10.3 5.5 %copy-start.2 = (bf16[8192,512]{1,0:T(8,128)(2,1)S(1)}, bf16[8192,512]{1,0:T(8,128)(2,1)}, u32[]{:S(2)}) copy-start(bf16[8192,512]{1,0:T(8,128)(2,1)} %param.8) | copy-start | bytes 25165828
  10.4 5.4 %copy-start.4 = (bf16[512,512]{1,0:T(8,128)(2,1)S(1)}, bf16[512,512]{1,0:T(8,128)(2,1)}, u32[]{:S(2)}) copy-start(bf16[512,512]{1,0:T(8,128)(2,1)} %param.7) | copy-start | bytes 1572868
  74.9 1.8 copy-start.3
  80.9 1.2 copy-start.6
  84.7 3.2 %collective-permute-start = (f32[512,128]{0,1:T(8,128)S(1)}, f32[512,128]{0,1:T(8,128)S(1)}, u32[]{:S(2)}, u32[]{:S(2)}) collective-permute-start(f32[512,128]{0,1:T(8,128)S(1)} %broadcast_select_fusion.2), channel_id=1, source_target_pairs={{0,1},{1,0},{2,3},{3,2},{4,5},{5,4},{6,7},{7,6},{8,9},{9,8},{10,11... | collective-permute-start | bytes 786440 | tf_op jit(solution)/shard_map/ppermute | solution.py:16
  88.0 21.6 %collective-permute-start.1 = (f32[512,128]{0,1:T(8,128)S(1)}, f32[512,128]{0,1:T(8,128)S(1)}, u32[]{:S(2)}, u32[]{:S(2)}) collective-permute-start(f32[512,128]{0,1:T(8,128)S(1)} %select_add_fusion), channel_id=1, source_target_pairs={{0,2},{1,3},{2,0},{3,1},{4,6},{5,7},{6,4},{7,5},{8,10},{9,11},{10,... | collective-permute-start | bytes 786440 | tf_op jit(solution)/shard_map/ppermute | solution.py:18
  89.4 20.2 %collective-permute-start.4 = (f32[512,128]{0,1:T(8,128)S(1)}, f32[512,128]{0,1:T(8,128)S(1)}, u32[]{:S(2)}, u32[]{:S(2)}) collective-permute-start(f32[512,128]{0,1:T(8,128)S(1)} %select_add_fusion), channel_id=1, source_target_pairs={{0,6},{1,7},{2,4},{3,5},{4,2},{5,3},{6,0},{7,1},{8,14},{9,15},{10,... | collective-permute-start | bytes 786440 | tf_op jit(solution)/shard_map/ppermute | solution.py:18
  91.1 14.2 %collective-permute-start.2 = (f32[256,128]{0,1:T(8,128)S(1)}, f32[256,128]{0,1:T(8,128)S(1)}, u32[]{:S(2)}, u32[]{:S(2)}) collective-permute-start(f32[256,128]{0,1:T(8,128)S(1)} %get-tuple-element.18), channel_id=1, source_target_pairs={{0,4},{1,5},{2,6},{3,7},{4,0},{5,1},{6,2},{7,3},{8,12},{9,13},{10,... | collective-permute-start | bytes 393224 | tf_op jit(solution)/shard_map/ppermute | solution.py:22
  91.9 17.7 %collective-permute-start.3 = (f32[256,128]{0,1:T(8,128)S(1)}, f32[256,128]{0,1:T(8,128)S(1)}, u32[]{:S(2)}, u32[]{:S(2)}) collective-permute-start(f32[256,128]{0,1:T(8,128)S(1)} %get-tuple-element.19), channel_id=1, source_target_pairs={{0,4},{1,5},{2,6},{3,7},{4,0},{5,1},{6,2},{7,3},{8,12},{9,13},{10,... | collective-permute-start | bytes 393224 | tf_op jit(solution)/shard_map/ppermute | solution.py:22
  109.7 2.6 %collective-permute-start.5 = (f32[512,128]{0,1:T(8,128)S(1)}, f32[512,128]{0,1:T(8,128)S(1)}, u32[]{:S(2)}, u32[]{:S(2)}) collective-permute-start(f32[512,128]{0,1:T(8,128)S(1)} %fusion.52), channel_id=1, source_target_pairs={{0,1},{1,0},{2,3},{3,2},{4,5},{5,4},{6,7},{7,6},{8,9},{9,8},{10,11... | collective-permute-start | bytes 786440 | tf_op jit(solution)/shard_map/ppermute | solution.py:32
  117.9 52.7 %all-to-all-start.1 = ((bf16[16,64,1536]{2,1,0:T(8,128)(2,1)}), bf16[16,64,1536]{2,1,0:T(8,128)(2,1)}, u32[]{:S(2)}, u32[]{:S(2)}) async-start(bf16[16,64,1536]{2,1,0:T(8,128)(2,1)} %bitcast.10), calls=%async_computation.1 | async-start | bytes 6291456 | tf_op jit(solution)/shard_map/all_to_all | solution.py:108
  122.4 10.3 %slice-start = ((s8[8388608]{0:T(1024)(128)(4,1)}), s8[4194304]{0:T(1024)(128)(4,1)S(1)}, s32[]{:S(2)}) async-start(s8[8388608]{0:T(1024)(128)(4,1)} %bitcast.52), calls=%async_computation.5 | async-start | bytes 8388608
  126.4 6.4 %slice-start.1 = ((s8[8388608]{0:T(1024)(128)(4,1)}), s8[4194304]{0:T(1024)(128)(4,1)S(1)}, s32[]{:S(2)}) async-start(s8[8388608]{0:T(1024)(128)(4,1)} %bitcast.52), calls=%async_computation.6 | async-start | bytes 8388608
  126.4 7.5 %copy-start.5 = (bf16[512,8192]{1,0:T(8,128)(2,1)S(1)}, bf16[512,8192]{1,0:T(8,128)(2,1)}, u32[]{:S(2)}) copy-start(bf16[512,8192]{1,0:T(8,128)(2,1)} %all-gather.2.cloned.1.call-done) | copy-start | bytes 25165828
  170.6 7.4 %copy-start.1 = (bf16[16,1024,64]{1,2,0:T(8,128)(2,1)S(1)}, bf16[16,1024,64]{1,2,0:T(8,128)(2,1)}, u32[]{:S(2)}) copy-start(bf16[16,1024,64]{1,2,0:T(8,128)(2,1)} %param.9) | copy-start | bytes 6291460
Sparse Core Ops, SparseCore 0:
  9.7 53.2 all-gather.1
  65.5 102.2 reduce-scatter.1
